TPU v7x, 32 devices: a whole 2x2x4 slice. The times are simulated.
32 devices in a mesh: groups: 2 (over y), tensor: 4 (over z), seq: 2 (over x), load: 2 (over core).
Axes of the slice: x: 2, y: 2, z: 4, core: 2. Of those that a mesh axis runs over, the one named last changes fastest.
Arguments:
- tokens: bfloat16 [1024, 16384], P(('groups', 'tensor'), ('seq', 'load')), parts along dimension 0, may hold values from -21 to 21
- weight_query: bfloat16 [16384, 16384], P(('seq', 'load'), 'tensor'), may hold values from -0.046875 to 0.046875
- weight_keyval: bfloat16 [16384, 2048], P(('seq', 'load'), 'tensor'), may hold values from -0.046875 to 0.046875
- down_query: bfloat16 [16384, 1024], P(('seq', 'load'), ('groups', 'tensor')), parts along dimension 1, may hold values from -0.046875 to 0.046875
- down_keyval: bfloat16 [16384, 1024], P(('seq', 'load'), ('groups', 'tensor')), parts along dimension 1, may hold values from -0.046875 to 0.046875
- up_query: bfloat16 [1024, 16384], P(('groups', 'load'), 'tensor'), parts along dimension 0, may hold values from -0.5 to 0.5
- up_keyval: bfloat16 [1024, 2048], P(('groups', 'load'), 'tensor'), parts along dimension 0, may hold values from -0.5 to 0.5
- adapter_rank: int32 [8], P('groups'), parts along dimension 0, may hold values from 8 to 128, as said below
- token_lengths: int32 [8], P('groups'), parts along dimension 0, may hold values from 1 to 384, 512 in all
- adapter_slot: int32 [8], P('groups'), parts along dimension 0, may hold values from 0 to 3, each once
Outputs:
- context: bfloat16 [1024, 16384], P(('groups', 'seq', 'load'), 'tensor'), parts along dimension 0
- kv_cache: bfloat16 [1024, 2048], P(('groups', 'seq', 'load'), 'tensor'), parts along dimension 0
There are 2 independent parts, one for each index of `groups`. A program takes and returns all parts, laid end to end along the dimension named above; an argument that names none is the same for every part. Nothing has to cross between parts.
Inputs may be any that keep to these rules, and one draw needn't show every extreme that they name: `adapter_rank`: each rank is a power of two; some tenant has rank 128 and some has rank 8. `token_lengths`: the lengths sum to 512; some tenant has exactly 384 tokens. `adapter_slot`: each slot belongs to exactly one tenant.
All inputs are finite; a program needn't handle non-finite values.
Results may differ from a plain program's by a relative error of at most 0.0025.
The roundings to bfloat16 on the way count: a program that leaves them out, or rounds other values in their place, can miss the bound.
Values may be sent and summed in bfloat16 or wider, within the bound.
No kernel may reach another device: no remote copies, remote signals or barrier semaphores. Data moves between devices by JAX's collectives and lax.ppermute only.
A program may use at most 128 MiB of HBM per device.

v0:
```python
import math

import jax
import jax.numpy as jnp
from jax import lax
from jax.sharding import PartitionSpec as P

HEADS = 128
KV_HEADS = 8
HEAD_DIM = 128
TENANTS = 4


ROPE_BASE = 500000.0
ADAPTER_ALPHA = 8.0


def product(left, right):
    return jnp.dot(left, right, preferred_element_type=jnp.float32)


def rotate_pairs(values, position, first_col):
    pair_count = values.shape[1] // 2
    pair_col = first_col + 2 * jnp.arange(pair_count, dtype=jnp.int32)
    within = pair_col % HEAD_DIM // 2
    frequency = jnp.exp(-(2.0 * within.astype(jnp.float32) / HEAD_DIM) * math.log(ROPE_BASE))
    angles = position.astype(jnp.float32)[:, None] * frequency[None, :]
    pair_view = values.reshape(values.shape[0], pair_count, 2)
    even_part = pair_view[:, :, 0]
    odd_part = pair_view[:, :, 1]
    cosine = jnp.cos(angles)
    sine_angle = jnp.sin(angles)
    turned = jnp.stack(
        [even_part * cosine - odd_part * sine_angle, even_part * sine_angle + odd_part * cosine],
        axis=2,
    )
    return turned.reshape(values.shape)


def tenant_table(token_ids, adapter_rank, token_lengths, adapter_slot):
    segment_ends = jnp.cumsum(token_lengths)
    begins = segment_ends - token_lengths
    owned_rows = (token_ids[:, None] >= begins[None, :]) & (
        token_ids[:, None] < segment_ends[None, :]
    )
    zero_int = jnp.zeros((), jnp.int32)
    own_rank = jnp.sum(jnp.where(owned_rows, adapter_rank[None, :], zero_int), axis=1)
    own_slot = jnp.sum(jnp.where(owned_rows, adapter_slot[None, :], zero_int), axis=1)
    own_first = jnp.sum(jnp.where(owned_rows, begins[None, :], zero_int), axis=1)
    slot_hot = own_slot[:, None] == jnp.arange(TENANTS, dtype=jnp.int32)[None, :]
    return (own_rank, own_first, slot_hot)


def select_slot(down_values, slot_hot):
    shaped = down_values.reshape(down_values.shape[0], -1, TENANTS)
    return jnp.sum(jnp.where(slot_hot[:, None, :], shaped, 0.0), axis=2)


def scale_ranks(picked, own_rank, first_rank):
    rank_index = first_rank + jnp.arange(picked.shape[1], dtype=jnp.int32)
    keep_mask = rank_index[None, :] < own_rank[:, None]
    factor = ADAPTER_ALPHA / jnp.sqrt(own_rank.astype(jnp.float32))
    return jnp.where(keep_mask, picked * factor[:, None], 0.0).astype(jnp.bfloat16)


def widen_slots(low_values, slot_hot):
    wide_rows = jnp.where(
        slot_hot[:, None, :], low_values[:, :, None], jnp.zeros((), low_values.dtype)
    )
    return wide_rows.reshape(low_values.shape[0], -1)


def shards(
    tokens,
    weight_query,
    weight_keyval,
    down_query,
    down_keyval,
    up_query,
    up_keyval,
    adapter_rank,
    token_lengths,
    adapter_slot,
):
    tensor_count = lax.axis_size("tensor")
    block_count = lax.axis_size(("seq", "load"))
    tensor_index = lax.axis_index("tensor")
    block_index = lax.axis_index(("seq", "load"))
    query_cols = weight_query.shape[1]
    keyval_cols = weight_keyval.shape[1]
    rank_share = down_query.shape[1] // TENANTS
    block_rows = tokens.shape[0] * tensor_count // block_count
    shard_rows = lax.all_gather(tokens, "tensor", axis=0, tiled=True)
    piece_ids = jnp.arange(shard_rows.shape[0], dtype=jnp.int32)
    piece_rank, piece_first, piece_hot = tenant_table(
        piece_ids, adapter_rank, token_lengths, adapter_slot
    )
    columns_list = [
        product(shard_rows, weight_query),
        product(shard_rows, weight_keyval),
        select_slot(product(shard_rows, down_query), piece_hot),
        select_slot(product(shard_rows, down_keyval), piece_hot),
    ]
    partial_terms = jnp.concatenate(columns_list, axis=1)
    summed = lax.psum_scatter(partial_terms, ("seq", "load"), scatter_dimension=0, tiled=True)
    token_ids = block_index * block_rows + jnp.arange(block_rows, dtype=jnp.int32)
    own_rank, own_first, slot_hot = tenant_table(
        token_ids, adapter_rank, token_lengths, adapter_slot
    )
    position = token_ids - own_first
    low_start = query_cols + keyval_cols
    first_rank = tensor_index * rank_share
    low_query = scale_ranks(summed[:, low_start : low_start + rank_share], own_rank, first_rank)
    low_keyval = scale_ranks(summed[:, low_start + rank_share :], own_rank, first_rank)
    full_query, full_keyval = (
        lax.all_gather(low_query, "tensor", axis=1, tiled=True),
        lax.all_gather(low_keyval, "tensor", axis=1, tiled=True),
    )
    wide_query = widen_slots(full_query, slot_hot)
    wide_keyval = widen_slots(full_keyval, slot_hot)
    up_query_all, up_keyval_all = (
        lax.all_gather(up_query, "load", axis=0, tiled=True),
        lax.all_gather(up_keyval, "load", axis=0, tiled=True),
    )
    delta_query = product(wide_query, up_query_all)
    delta_keyval = product(wide_keyval, up_keyval_all)
    query_rows = rotate_pairs(
        summed[:, :query_cols] + delta_query, position, tensor_index * query_cols
    ).astype(jnp.bfloat16)
    keyval = summed[:, query_cols:low_start] + delta_keyval
    kv_first_col = tensor_index * keyval_cols
    is_key = kv_first_col + jnp.arange(keyval_cols, dtype=jnp.int32) < KV_HEADS * HEAD_DIM
    kv_local = jnp.where(
        is_key[None, :], rotate_pairs(keyval, position, kv_first_col), keyval
    ).astype(jnp.bfloat16)
    kv_all = lax.all_gather(kv_local, "tensor", axis=1, tiled=True)
    heads_here = query_cols // HEAD_DIM
    group_size = HEADS // KV_HEADS
    kv_here = max(heads_here // group_size, 1)
    per_kv = heads_here // kv_here
    kv_first = tensor_index * heads_here // group_size
    key_cols = KV_HEADS * HEAD_DIM
    key_heads = lax.dynamic_slice_in_dim(
        kv_all, kv_first * HEAD_DIM, kv_here * HEAD_DIM, 1
    ).reshape(block_rows, kv_here, HEAD_DIM)
    value_heads = lax.dynamic_slice_in_dim(
        kv_all, key_cols + kv_first * HEAD_DIM, kv_here * HEAD_DIM, 1
    ).reshape(block_rows, kv_here, HEAD_DIM)
    grouped = query_rows.reshape(block_rows, kv_here, per_kv, HEAD_DIM)
    running_top = jnp.full((kv_here, per_kv, block_rows), -1e30, jnp.float32)
    piece_keys = lax.all_gather(key_heads, ("seq", "load"), axis=0, tiled=True)
    piece_values = lax.all_gather(value_heads, ("seq", "load"), axis=0, tiled=True)
    key_ids = jnp.arange(piece_keys.shape[0], dtype=jnp.int32)
    visible = (key_ids[None, :] >= own_first[:, None]) & (key_ids[None, :] <= token_ids[:, None])
    scores = jnp.einsum(
        "qghd,kgd->ghqk", grouped, piece_keys, preferred_element_type=jnp.float32
    ) / math.sqrt(HEAD_DIM)
    scores = jnp.where(visible, scores, -1e30)
    new_top = jnp.maximum(running_top, jnp.max(scores, axis=3))
    exp_scores = jnp.where(visible, jnp.exp(scores - new_top[..., None]), 0.0)
    new_sum = jnp.sum(exp_scores, axis=3)
    new_acc = jnp.einsum(
        "ghqk,kgd->ghqd",
        exp_scores.astype(jnp.bfloat16),
        piece_values,
        preferred_element_type=jnp.float32,
    )
    state_tuple = (new_top, new_sum, new_acc)
    final_top, row_total, accumulated = state_tuple
    context = (accumulated / row_total[..., None]).astype(jnp.bfloat16)
    context = jnp.transpose(context, (2, 0, 1, 3)).reshape(block_rows, query_cols)
    return (context, kv_local)


def solution(mesh):
    placed = (
        P(("groups", "tensor"), ("seq", "load")),
        P(("seq", "load"), "tensor"),
        P(("seq", "load"), "tensor"),
        P(("seq", "load"), ("groups", "tensor")),
        P(("seq", "load"), ("groups", "tensor")),
        P(("groups", "load"), "tensor"),
        P(("groups", "load"), "tensor"),
        P("groups"),
        P("groups"),
        P("groups"),
    )
    return jax.shard_map(
        shards,
        mesh=mesh,
        in_specs=placed,
        out_specs=(P(("groups", "seq", "load"), "tensor"), P(("groups", "seq", "load"), "tensor")),
        check_vma=False,
    )
```

profile of v0, /device:TPU:0, one launch (start us, length us, event | category | flops | bytes accessed | tf_op | source)
XLA Modules:
  0.0 307.8 jit_solution(12603682997678167109)
XLA Ops:
  8.8 0.8 reduce-window.8
  11.0 82.9 %all-gather.3.cloned.1.call-done = bf16[512,4096]{1,0:T(8,128)(2,1)} async-done(((bf16[128,4096]{1,0:T(8,128)(2,1)}), bf16[512,4096]{1,0:T(8,128)(2,1)}) %all-gather.3.cloned.1.call-update) | async-done | bytes 4194320 | tf_op jit(solution)/shard_map/all_gather | solution.py:93
  93.9 3.7 %fusion.46 = f32[512,128]{0,1:T(8,128)S(1)} fusion(bf16[512,4096]{1,0:T(8,128)(2,1)} %all-gather.3.cloned.1.call-done, bf16[4096,128]{1,0:T(8,128)(2,1)S(1)} %copy-done), kind=kOutput, calls=%fused_computation.100 | convolution fusion | flops 536870912 | bytes 5505024 | tf_op jit(solution)/shard_map/dot_general | solution.py:19
  97.7 3.7 %fusion.47 = f32[512,128]{0,1:T(8,128)S(1)} fusion(bf16[512,4096]{1,0:T(8,128)(2,1)} %all-gather.3.cloned.1.call-done, bf16[4096,128]{1,0:T(8,128)(2,1)S(1)} %copy-done.4), kind=kOutput, calls=%fused_computation.101 | convolution fusion | flops 536870912 | bytes 5505024 | tf_op jit(solution)/shard_map/dot_general | solution.py:19
  101.9 26.5 %fusion.44 = f32[512,4096]{0,1:T(8,128)} fusion(bf16[512,4096]{1,0:T(8,128)(2,1)} %all-gather.3.cloned.1.call-done, bf16[4096,4096]{1,0:T(8,128)(2,1)} %param.11), kind=kOutput, calls=%fused_computation.98 | convolution fusion | flops 17179869184 | bytes 46137344 | tf_op jit(solution)/shard_map/dot_general | solution.py:19
  128.4 4.7 %fusion.45 = f32[512,512]{0,1:T(8,128)S(1)} fusion(bf16[512,4096]{1,0:T(8,128)(2,1)S(1)} %copy-done.2, bf16[4096,512]{1,0:T(8,128)(2,1)} %param.12), kind=kOutput, calls=%fused_computation.99 | convolution fusion | flops 2147483648 | bytes 9437184 | tf_op jit(solution)/shard_map/dot_general | solution.py:19
  133.1 9.8 %pad_maximum_fusion = f32[512,4672]{0,1:T(8,128)} fusion(f32[512,32]{0,1:T(8,128)S(1)} %get-tuple-element.13, f32[512,32]{0,1:T(8,128)S(1)} %get-tuple-element.12, f32[512,512]{0,1:T(8,128)S(1)} %fusion.45, f32[512,4096]{0,1:T(8,128)S(1)} %copy-done.3), kind=kLoop, calls=%fused_computation | loop fusion | flops 7176192 | bytes 19136512 | tf_op jit(solution)/shard_map/concatenate | solution.py:104
  143.8 2.2 all_gather.26
  146.1 76.7 %reduce-scatter.2.cloned.1.call-done = f32[128,4672]{0,1:T(8,128)} async-done(((f32[512,4672]{0,1:T(8,128)}), f32[128,4672]{0,1:T(8,128)}) %reduce-scatter.2.cloned.1.call-update) | async-done | bytes 2392080 | tf_op jit(solution)/shard_map/reduce_scatter | solution.py:105
  222.8 0.8 fusion.27
  223.7 13.2 %all_gather.25 = bf16[128,128]{0,1:T(8,128)(2,1)S(1)} all-gather(bf16[128,32]{0,1:T(8,128)(2,1)S(1)} %get-tuple-element.17), channel_id=1, replica_groups=mesh['groups'=2,'tensor'=4,'seq'=2,'load'=2] {'tensor'}, dimensions={1}, use_global_device_ids=true | all-gather | bytes 40960 | tf_op jit(solution)/shard_map/all_gather | solution.py:117
  236.8 13.1 %all_gather.29 = bf16[128,128]{0,1:T(8,128)(2,1)S(1)} all-gather(bf16[128,32]{0,1:T(8,128)(2,1)S(1)} %get-tuple-element.18), channel_id=1, replica_groups=mesh['groups'=2,'tensor'=4,'seq'=2,'load'=2] {'tensor'}, dimensions={1}, use_global_device_ids=true | all-gather | bytes 40960 | tf_op jit(solution)/shard_map/all_gather | solution.py:116
  250.1 1.3 convolution_add_fusion.1
  253.4 15.4 %all_gather.27 = bf16[128,2048]{0,1:T(8,128)(2,1)S(1)} all-gather(bf16[128,512]{0,1:T(8,128)(2,1)S(1)} %select_convert_fusion), channel_id=1, replica_groups=mesh['groups'=2,'tensor'=4,'seq'=2,'load'=2] {'tensor'}, dimensions={1}, use_global_device_ids=true | all-gather | bytes 655360 | tf_op jit(solution)/shard_map/all_gather | solution.py:136
  269.0 5.8 %all_gather.28 = bf16[512,2,128]{2,0,1:T(8,128)(2,1)S(1)} all-gather(bf16[128,2,128]{2,0,1:T(8,128)(2,1)S(1)} %copy.60), channel_id=1, replica_groups=mesh['groups'=2,'tensor'=4,'seq'=2,'load'=2] {'seq','load'}, dimensions={0}, use_global_device_ids=true | all-gather | bytes 327680 | tf_op jit(solution)/shard_map/all_gather | solution.py:151
  274.8 4.6 %convolution_add_fusion = f32[128,4096]{0,1:T(8,128)S(1)} fusion(bf16[128,512]{0,1:T(8,128)(2,1)S(1)} %bitcast.63, bf16[512,4096]{1,0:T(8,128)(2,1)} %all-gather.5.cloned.1.call-done, f32[128,4672]{0,1:T(8,128)} %reduce-scatter.2.cloned.1.call-done), kind=kOutput, calls=%fused_computation.6 | convolution fusion | flops 537395200 | bytes 8519680 | tf_op jit(solution)/shard_map/dot_general | solution.py:19
  279.4 1.7 fusion.42
  282.4 4.2 %fusion.14 = (bf16[128,2048,1]{1,0,2:T(8,128)(2,1)S(1)}, bf16[128,2048,1]{1,0,2:T(8,128)(2,1)S(1)}) fusion(f32[128,2048,1]{1,0,2:T(8,128)S(1)} %copy.79, f32[128,2048,1]{1,0,2:T(8,128)S(1)} %copy.78, f32[2048]{0:T(1024)S(1)} %fusion.35, f32[128]{0:T(128)S(1)} %subtract_convert_fusion), kind=kLoop, calls=%fused_computation.19 | loop fusion | flops 2359296 | bytes 3154432 | tf_op jit(solution)/shard_map/convert
  286.7 0.8 copy.64
  287.5 1.3 fusion
  288.8 5.9 %all_gather.31 = bf16[512,2,128]{0,2,1:T(8,128)(2,1)S(1)} all-gather(bf16[128,2,128]{0,2,1:T(8,128)(2,1)S(1)} %bitcast.66), channel_id=1, replica_groups=mesh['groups'=2,'tensor'=4,'seq'=2,'load'=2] {'seq','load'}, dimensions={0}, use_global_device_ids=true | all-gather | bytes 327680 | tf_op jit(solution)/shard_map/all_gather | solution.py:152
  294.7 2.0 fusion.1
  296.8 2.2 fusion.6
  299.0 1.3 copy.67
  (54 shorter events, 7.4 us)
Async XLA Ops:
  8.0 85.9 %copy-start = (bf16[4096,128]{1,0:T(8,128)(2,1)S(1)}, bf16[4096,128]{1,0:T(8,128)(2,1)}, u32[]{:S(2)}) copy-start(bf16[4096,128]{1,0:T(8,128)(2,1)} %param.13) | copy-start | bytes 3145732
  8.0 89.7 %copy-start.4 = (bf16[4096,128]{1,0:T(8,128)(2,1)S(1)}, bf16[4096,128]{1,0:T(8,128)(2,1)}, u32[]{:S(2)}) copy-start(bf16[4096,128]{1,0:T(8,128)(2,1)} %param.14) | copy-start | bytes 3145732
  8.0 85.9 %all-gather.3.cloned.1.call-start = ((), (), s32[]{:S(2)}) async-start(), calls=%async_computation.1 | async-start | bytes 5242880 | tf_op jit(solution)/shard_map/all_gather | solution.py:93
  8.8 214.1 %reduce-scatter.2.cloned.1.call-start = ((), (), s32[]{:S(2)}) async-start(), calls=%async_computation.2 | async-start | bytes 11960320 | tf_op jit(solution)/shard_map/reduce_scatter | solution.py:105
  101.9 26.5 %copy-start.2 = (bf16[512,4096]{1,0:T(8,128)(2,1)S(1)}, bf16[512,4096]{1,0:T(8,128)(2,1)}, u32[]{:S(2)}) copy-start(bf16[512,4096]{1,0:T(8,128)(2,1)} %all-gather.3.cloned.1.call-done) | copy-start | bytes 12582916
  128.4 4.7 %copy-start.3 = (f32[512,4096]{0,1:T(8,128)S(1)}, f32[512,4096]{0,1:T(8,128)}, u32[]{:S(2)}) copy-start(f32[512,4096]{0,1:T(8,128)} %fusion.44) | copy-start | bytes 25165828
  142.9 0.7 copy-start.6
  142.9 0.7 copy-start.7
  142.9 1.0 copy-start.5
  142.9 131.9 %all-gather.5.cloned.1.call-start = ((), (), s32[]{:S(2)}) async-start(), calls=%async_computation.3 | async-start | bytes 6291456 | tf_op jit(solution)/shard_map/all_gather | solution.py:122
  296.8 3.5 %copy-start.1 = (bf16[4096,128]{1,0:T(8,128)(2,1)S(1)}, bf16[4096,128]{1,0:T(8,128)(2,1)}, u32[]{:S(2)}) copy-start(bf16[4096,128]{1,0:T(8,128)(2,1)} %param.13) | copy-start | bytes 3145732
Sparse Core Ops, SparseCore 0:
  10.4 83.4 all-gather.2
  143.0 79.7 reduce-scatter.1
Sparse Core Ops, SparseCore 1:
  144.9 12.6 all-gather.4
where the time goes:
time: 308 us
  waiting for transfers between devices  161 us (52%)
  blocking collectives  55.6 us (18%)
  matrix products  48 us (16%)
  other arithmetic  20.6 us (7%)
  between operations  15.8 us (5%)
  local copies, waits for them, and re-layouts  6.82 us (2%)
    all_gather x1, waiting for transfers between devices, shards(): shard_rows = lax.all_gather(tokens, 'tensor', axis=0, tiled=True)  82.9 us
    reduce_scatter x1, waiting for transfers between devices, shards(): lax.psum_scatter(partial_terms, ('seq', 'load'), scatter_dimension=0, til...  76.7 us
    dot_general x6, matrix products, product(): return jnp.dot(left, right, preferred_element_type=jnp.float32)  44.5 us
    all_gather x1, blocking collectives, shards(): kv_all = lax.all_gather(kv_local, 'tensor', axis=1, tiled=True)  15.4 us
    all_gather x1, blocking collectives, shards(): lax.all_gather(low_keyval, 'tensor', axis=1, tiled=True)  13.2 us
    all_gather x1, blocking collectives, shards(): lax.all_gather(low_query, 'tensor', axis=1, tiled=True)  13.1 us
    concatenate x1, other arithmetic, shards(): partial_terms = jnp.concatenate(columns_list, axis=1)  9.75 us
  transfers between devices with their start and end apart: 3, of which 2 were waited for; matrix products, arithmetic and copies ran while one was open for 2% of the time, Pallas kernels for 0%

commit v1 on v0

--- a/solution.py
+++ b/solution.py
@@ -82,28 +82,47 @@
     token_lengths,
     adapter_slot,
 ):
-    tensor_count = lax.axis_size("tensor")
-    block_count = lax.axis_size(("seq", "load"))
+    ring = lax.axis_size("tensor")
+    split = lax.axis_size(("seq", "load"))
     tensor_index = lax.axis_index("tensor")
     block_index = lax.axis_index(("seq", "load"))
     query_cols = weight_query.shape[1]
     keyval_cols = weight_keyval.shape[1]
     rank_share = down_query.shape[1] // TENANTS
-    block_rows = tokens.shape[0] * tensor_count // block_count
-    shard_rows = lax.all_gather(tokens, "tensor", axis=0, tiled=True)
-    piece_ids = jnp.arange(shard_rows.shape[0], dtype=jnp.int32)
-    piece_rank, piece_first, piece_hot = tenant_table(
-        piece_ids, adapter_rank, token_lengths, adapter_slot
-    )
-    columns_list = [
-        product(shard_rows, weight_query),
-        product(shard_rows, weight_keyval),
-        select_slot(product(shard_rows, down_query), piece_hot),
-        select_slot(product(shard_rows, down_keyval), piece_hot),
-    ]
-    partial_terms = jnp.concatenate(columns_list, axis=1)
-    summed = lax.psum_scatter(partial_terms, ("seq", "load"), scatter_dimension=0, tiled=True)
-    token_ids = block_index * block_rows + jnp.arange(block_rows, dtype=jnp.int32)
+    chunk = tokens.shape[0]
+    piece = chunk // split
+    local_rows = ring * piece
+
+    up_query_all = lax.all_gather(up_query, "load", axis=0, tiled=True)
+    up_keyval_all = lax.all_gather(up_keyval, "load", axis=0, tiled=True)
+
+    shift = [(i, (i + 1) % ring) for i in range(ring)]
+    held = tokens
+    reduced = []
+    for step in range(ring):
+        following = lax.ppermute(held, "tensor", shift) if step < ring - 1 else None
+        owner = (tensor_index - step) % ring
+        block_ids = owner * chunk + jnp.arange(chunk, dtype=jnp.int32)
+        _, _, block_hot = tenant_table(block_ids, adapter_rank, token_lengths, adapter_slot)
+        partial = jnp.concatenate(
+            [
+                product(held, weight_query),
+                product(held, weight_keyval),
+                select_slot(product(held, down_query), block_hot),
+                select_slot(product(held, down_keyval), block_hot),
+            ],
+            axis=1,
+        )
+        reduced.append(
+            lax.psum_scatter(partial, ("seq", "load"), scatter_dimension=0, tiled=True)
+        )
+        held = following
+    steps_of_owner = (tensor_index - jnp.arange(ring, dtype=jnp.int32)) % ring
+    summed = jnp.take(jnp.stack(reduced), steps_of_owner, axis=0).reshape(local_rows, -1)
+
+    owners = jnp.arange(ring, dtype=jnp.int32)
+    piece_ids = jnp.arange(piece, dtype=jnp.int32)
+    token_ids = (owners[:, None] * chunk + block_index * piece + piece_ids[None, :]).reshape(-1)
     own_rank, own_first, slot_hot = tenant_table(
         token_ids, adapter_rank, token_lengths, adapter_slot
     )
@@ -112,16 +131,13 @@
     first_rank = tensor_index * rank_share
     low_query = scale_ranks(summed[:, low_start : low_start + rank_share], own_rank, first_rank)
     low_keyval = scale_ranks(summed[:, low_start + rank_share :], own_rank, first_rank)
-    full_query, full_keyval = (
-        lax.all_gather(low_query, "tensor", axis=1, tiled=True),
-        lax.all_gather(low_keyval, "tensor", axis=1, tiled=True),
-    )
+    low_both = lax.all_gather(
+        jnp.concatenate([low_query, low_keyval], axis=1), "tensor", axis=1
+    )
+    full_query = low_both[:, :, :rank_share].reshape(local_rows, -1)
+    full_keyval = low_both[:, :, rank_share:].reshape(local_rows, -1)
     wide_query = widen_slots(full_query, slot_hot)
     wide_keyval = widen_slots(full_keyval, slot_hot)
-    up_query_all, up_keyval_all = (
-        lax.all_gather(up_query, "load", axis=0, tiled=True),
-        lax.all_gather(up_keyval, "load", axis=0, tiled=True),
-    )
     delta_query = product(wide_query, up_query_all)
     delta_keyval = product(wide_keyval, up_keyval_all)
     query_rows = rotate_pairs(
@@ -142,34 +158,43 @@
     key_cols = KV_HEADS * HEAD_DIM
     key_heads = lax.dynamic_slice_in_dim(
         kv_all, kv_first * HEAD_DIM, kv_here * HEAD_DIM, 1
-    ).reshape(block_rows, kv_here, HEAD_DIM)
+    ).reshape(local_rows, kv_here, HEAD_DIM)
     value_heads = lax.dynamic_slice_in_dim(
         kv_all, key_cols + kv_first * HEAD_DIM, kv_here * HEAD_DIM, 1
-    ).reshape(block_rows, kv_here, HEAD_DIM)
-    grouped = query_rows.reshape(block_rows, kv_here, per_kv, HEAD_DIM)
-    running_top = jnp.full((kv_here, per_kv, block_rows), -1e30, jnp.float32)
-    piece_keys = lax.all_gather(key_heads, ("seq", "load"), axis=0, tiled=True)
-    piece_values = lax.all_gather(value_heads, ("seq", "load"), axis=0, tiled=True)
-    key_ids = jnp.arange(piece_keys.shape[0], dtype=jnp.int32)
+    ).reshape(local_rows, kv_here, HEAD_DIM)
+    both_heads = lax.all_gather(
+        jnp.concatenate([key_heads, value_heads], axis=1), ("seq", "load"), axis=0, tiled=True
+    )
+    piece_keys = both_heads[:, :kv_here]
+    piece_values = both_heads[:, kv_here:]
+    key_ids = (
+        owners[None, :, None] * chunk
+        + jnp.arange(split, dtype=jnp.int32)[:, None, None] * piece
+        + piece_ids[None, None, :]
+    ).reshape(-1)
+    grouped = query_rows.reshape(local_rows, kv_here, per_kv, HEAD_DIM)
     visible = (key_ids[None, :] >= own_first[:, None]) & (key_ids[None, :] <= token_ids[:, None])
     scores = jnp.einsum(
         "qghd,kgd->ghqk", grouped, piece_keys, preferred_element_type=jnp.float32
     ) / math.sqrt(HEAD_DIM)
     scores = jnp.where(visible, scores, -1e30)
-    new_top = jnp.maximum(running_top, jnp.max(scores, axis=3))
-    exp_scores = jnp.where(visible, jnp.exp(scores - new_top[..., None]), 0.0)
-    new_sum = jnp.sum(exp_scores, axis=3)
-    new_acc = jnp.einsum(
+    row_top = jnp.max(scores, axis=3)
+    exp_scores = jnp.where(visible, jnp.exp(scores - row_top[..., None]), 0.0)
+    row_total = jnp.sum(exp_scores, axis=3)
+    accumulated = jnp.einsum(
         "ghqk,kgd->ghqd",
         exp_scores.astype(jnp.bfloat16),
         piece_values,
         preferred_element_type=jnp.float32,
     )
-    state_tuple = (new_top, new_sum, new_acc)
-    final_top, row_total, accumulated = state_tuple
     context = (accumulated / row_total[..., None]).astype(jnp.bfloat16)
-    context = jnp.transpose(context, (2, 0, 1, 3)).reshape(block_rows, query_cols)
-    return (context, kv_local)
+    context = jnp.transpose(context, (2, 0, 1, 3)).reshape(local_rows, query_cols)
+
+    outgoing = jnp.concatenate([context, kv_local], axis=1)
+    by_owner = outgoing.reshape(split, ring // split, piece, -1)
+    arrived = lax.all_to_all(by_owner, ("seq", "load"), 0, 0)
+    placed = jnp.transpose(arrived, (1, 0, 2, 3)).reshape(local_rows, -1)
+    return (placed[:, :query_cols], placed[:, query_cols:])
 
 
 def solution(mesh):

time: 308 us -> 316 us (1.026)
  waiting for transfers between devices: 161 us -> 103 us
  matrix products: 48 us -> 91 us
  local copies, waits for them, and re-layouts: 6.82 us -> 31 us
  other arithmetic: 20.6 us -> 13.9 us
  starting transfers between devices: 0.12 us -> 3.57 us
    all_gather x2 -> x1, waiting for transfers between devices: 82.9 us -> 0.01 us  [shards(): up_query_all = lax.all_gather(up_query, 'load', axis=0, tiled=True)]
    ppermute x0 -> x3, waiting for transfers between devices: none -> 76.5 us  [shards(): following = lax.ppermute(held, 'tensor', shift) if step < ring - 1 else None]
    reduce_scatter x1 -> x4, waiting for transfers between devices: 76.7 us -> 25.9 us  [shards(): lax.psum_scatter(partial, ('seq', 'load'), scatter_dimension=0, tiled=True)]
    dot_general x6 -> x18, matrix products: 44.5 us -> 81.8 us  [product(): return jnp.dot(left, right, preferred_element_type=jnp.float32)]
    all_to_all x0 -> x1, blocking collectives: none -> 18.4 us  [shards(): arrived = lax.all_to_all(by_owner, ('seq', 'load'), 0, 0)]
    all_gather x5 -> x3, blocking collectives: 40.2 us -> 22.5 us  [the longest x1 13.5 us: shards(): lax.all_gather(jnp.concatenate([low_query, low_keyval], axis=1), 'tensor'...]
    concatenate x0 -> x6, local copies, waits for them, and re-layouts: none -> 14.9 us  [the longest x4 14.3 us: shards(): jnp.concatenate([product(held, weight_query), product(held, weight_keyval...]
    concatenate x1 -> x3, other arithmetic: 9.75 us -> 0.18 us  [the longest x1 0.09 us: shards(): jnp.concatenate([low_query, low_keyval], axis=1)]
  transfers between devices with their start and end apart: 3 -> 8, of which waited for: 2 -> 4; matrix products, arithmetic and copies ran while one was open for 2% -> 26% of each run, Pallas kernels for 0% -> 0%
where the time goes in v1:
time: 316 us; the launch traced here: 315 us
  waiting for transfers between devices  103 us (33%)
  matrix products  91 us (29%)
  blocking collectives  56.9 us (18%)
  local copies, waits for them, and re-layouts  31 us (10%)
  between operations  15.9 us (5%)
  other arithmetic  13.9 us (4%)
  starting transfers between devices  3.57 us (1%)
    dot_general x18, matrix products, product(): return jnp.dot(left, right, preferred_element_type=jnp.float32)  81.8 us
    ppermute x3, waiting for transfers between devices, shards(): following = lax.ppermute(held, 'tensor', shift) if step < ring - 1 else None  76.5 us
    reduce_scatter x4, waiting for transfers between devices, shards(): lax.psum_scatter(partial, ('seq', 'load'), scatter_dimension=0, tiled=True)  25.9 us
    all_to_all x1, blocking collectives, shards(): arrived = lax.all_to_all(by_owner, ('seq', 'load'), 0, 0)  18.4 us
    all_gather x1, blocking collectives, shards(): kv_all = lax.all_gather(kv_local, 'tensor', axis=1, tiled=True)  16 us
    concatenate x4, local copies, waits for them, and re-layouts, shards(): jnp.concatenate([product(held, weight_query), product(held, weight_keyval...  14.3 us
    all_gather x1, blocking collectives, shards(): lax.all_gather(jnp.concatenate([low_query, low_keyval], axis=1), 'tensor'...  13.5 us
    all_gather x1, blocking collectives, shards(): lax.all_gather(jnp.concatenate([key_heads, value_heads], axis=1), ('seq',...  6.51 us
  transfers between devices with their start and end apart: 8, of which 4 were waited for; matrix products, arithmetic and copies ran while one was open for 26% of the time, Pallas kernels for 0%

profile of v1, /device:TPU:0, one launch (start us, length us, event | category | flops | bytes accessed | tf_op | source)
XLA Modules:
  0.0 315.2 jit_solution(80680660956528715)
XLA Ops:
  9.9 16.9 %fusion.47 = f32[128,4096]{1,0:T(8,128)} fusion(bf16[128,4096]{1,0:T(8,128)(2,1)} %param.10, bf16[4096,4096]{1,0:T(8,128)(2,1)} %param.11), kind=kOutput, calls=%fused_computation.135 | convolution fusion | flops 4294967296 | bytes 36700160 | tf_op jit(solution)/shard_map/dot_general | solution.py:19
  29.1 3.6 %concatenate.26 = f32[128,4672]{1,0:T(8,128)} concatenate(f32[128,4096]{1,0:T(8,128)} %fusion.47, f32[128,512]{1,0:T(8,128)S(1)} %fusion.48, f32[128,32]{1,0:T(8,128)S(1)} %copy.64, f32[128,32]{1,0:T(8,128)S(1)} %copy.65), dimensions={1} | concatenate | bytes 4784128 | tf_op jit(solution)/shard_map/concatenate | solution.py:107
  32.7 3.1 collective-permute-start
  35.8 25.2 %collective-permute-done = bf16[128,4096]{1,0:T(8,128)(2,1)S(1)} collective-permute-done((bf16[128,4096]{1,0:T(8,128)(2,1)S(1)}, bf16[128,4096]{1,0:T(8,128)(2,1)S(1)}, u32[]{:S(2)}, u32[]{:S(2)}) %collective-permute-start) | collective-permute-done | bytes 1048608 | tf_op jit(solution)/shard_map/ppermute | solution.py:103
  63.6 2.9 fusion.52
  66.5 14.3 %fusion.51 = f32[128,4096]{1,0:T(8,128)} fusion(bf16[128,4096]{1,0:T(8,128)(2,1)S(1)} %collective-permute-done, bf16[4096,4096]{1,0:T(8,128)(2,1)} %param.11), kind=kOutput, calls=%fused_computation.139 | convolution fusion | flops 4294967296 | bytes 36700160 | tf_op jit(solution)/shard_map/dot_general | solution.py:19
  80.8 3.6 %concatenate.27 = f32[128,4672]{1,0:T(8,128)} concatenate(f32[128,4096]{1,0:T(8,128)} %fusion.51, f32[128,512]{1,0:T(8,128)S(1)} %fusion.52, f32[128,32]{1,0:T(8,128)S(1)} %copy.66, f32[128,32]{1,0:T(8,128)S(1)} %copy.67), dimensions={1} | concatenate | bytes 4784128 | tf_op jit(solution)/shard_map/concatenate | solution.py:107
  84.7 26.1 %collective-permute-done.1 = bf16[128,4096]{1,0:T(8,128)(2,1)S(1)} collective-permute-done((bf16[128,4096]{1,0:T(8,128)(2,1)S(1)}, bf16[128,4096]{1,0:T(8,128)(2,1)S(1)}, u32[]{:S(2)}, u32[]{:S(2)}) %collective-permute-start.1) | collective-permute-done | bytes 1048608 | tf_op jit(solution)/shard_map/ppermute | solution.py:103
  113.4 3.0 fusion.56
  116.4 14.3 %fusion.55 = f32[128,4096]{1,0:T(8,128)} fusion(bf16[128,4096]{1,0:T(8,128)(2,1)S(1)} %collective-permute-done.1, bf16[4096,4096]{1,0:T(8,128)(2,1)} %param.11), kind=kOutput, calls=%fused_computation.143 | convolution fusion | flops 4294967296 | bytes 36700160 | tf_op jit(solution)/shard_map/dot_general | solution.py:19
  130.7 3.6 %concatenate.28 = f32[128,4672]{1,0:T(8,128)} concatenate(f32[128,4096]{1,0:T(8,128)} %fusion.55, f32[128,512]{1,0:T(8,128)S(1)} %fusion.56, f32[128,32]{1,0:T(8,128)S(1)} %copy.68, f32[128,32]{1,0:T(8,128)S(1)} %copy.69), dimensions={1} | concatenate | bytes 4784128 | tf_op jit(solution)/shard_map/concatenate | solution.py:107
  134.5 25.2 %collective-permute-done.2 = bf16[128,4096]{1,0:T(8,128)(2,1)S(1)} collective-permute-done((bf16[128,4096]{1,0:T(8,128)(2,1)S(1)}, bf16[128,4096]{1,0:T(8,128)(2,1)S(1)}, u32[]{:S(2)}, u32[]{:S(2)}) %collective-permute-start.2) | collective-permute-done | bytes 1048608 | tf_op jit(solution)/shard_map/ppermute | solution.py:103
  162.2 2.9 fusion.60
  165.2 14.3 %fusion.59 = f32[128,4096]{1,0:T(8,128)} fusion(bf16[128,4096]{1,0:T(8,128)(2,1)S(1)} %collective-permute-done.2, bf16[4096,4096]{1,0:T(8,128)(2,1)} %param.11), kind=kOutput, calls=%fused_computation.147 | convolution fusion | flops 4294967296 | bytes 36700160 | tf_op jit(solution)/shard_map/dot_general | solution.py:19
  179.5 3.6 %concatenate.29 = f32[128,4672]{1,0:T(8,128)} concatenate(f32[128,4096]{1,0:T(8,128)} %fusion.59, f32[128,512]{1,0:T(8,128)S(1)} %fusion.60, f32[128,32]{1,0:T(8,128)S(1)} %copy.70, f32[128,32]{1,0:T(8,128)S(1)} %copy.71), dimensions={1} | concatenate | bytes 4784128 | tf_op jit(solution)/shard_map/concatenate | solution.py:107
  188.6 25.8 %reduce-scatter.11.cloned.1.call-done = f32[32,4672]{1,0:T(8,128)} async-done(((f32[128,4672]{1,0:T(8,128)}), f32[32,4672]{1,0:T(8,128)}) %reduce-scatter.11.cloned.1.call-update) | async-done | bytes 598032 | tf_op jit(solution)/shard_map/reduce_scatter | solution.py:117
  220.6 13.5 %all-gather = bf16[128,256]{0,1:T(8,128)(2,1)S(1)} all-gather(bf16[128,64]{0,1:T(8,128)(2,1)S(1)} %copy.72), channel_id=2, replica_groups=mesh['groups'=2,'tensor'=4,'seq'=2,'load'=2] {'tensor'}, dimensions={1}, use_global_device_ids=true | all-gather | bytes 81920 | tf_op jit(solution)/shard_map/all_gather | solution.py:134
  237.2 4.3 %convolution_add_fusion = f32[128,4096]{1,0:T(8,128)} fusion(bf16[128,512]{0,1:T(8,128)(2,1)S(1)} %bitcast.120, bf16[512,4096]{1,0:T(8,128)(2,1)} %all-gather.3.cloned.1.call-done, f32[128,4672]{1,0:T(8,128)S(1)} %bitcast_select_fusion.4), kind=kOutput, calls=%fused_computation.5 | convolution fusion | flops 537395200 | bytes 8519680 | tf_op jit(solution)/shard_map/dot_general | solution.py:19
  249.1 4.2 %fusion.15 = (bf16[128,2048,1]{1,0,2:T(8,128)(2,1)S(1)}, bf16[128,2048,1]{1,0,2:T(8,128)(2,1)S(1)}) fusion(f32[128,2048,1]{1,0,2:T(8,128)S(1)} %copy.97, f32[128,2048,1]{1,0,2:T(8,128)S(1)} %copy.96, f32[2048]{0:T(1024)S(1)} %fusion.35, f32[128]{0:T(128)S(1)} %copy-done.10), kind=kLoop, calls=%fused_computation.24 | loop fusion | flops 2359296 | bytes 3154432 | tf_op jit(solution)/shard_map/convert
  254.4 16.0 %all_gather.21 = bf16[128,2048]{1,0:T(8,128)(2,1)S(1)} all-gather(bf16[128,512]{1,0:T(8,128)(2,1)S(1)} %select_convert_fusion), channel_id=1, replica_groups=mesh['groups'=2,'tensor'=4,'seq'=2,'load'=2] {'tensor'}, dimensions={1}, use_global_device_ids=true | all-gather | bytes 655360 | tf_op jit(solution)/shard_map/all_gather | solution.py:152
  270.9 6.5 %all_gather.22 = bf16[512,4,128]{2,0,1:T(8,128)(2,1)S(1)} all-gather(bf16[128,4,128]{2,0,1:T(8,128)(2,1)S(1)} %pad_maximum_fusion.3), channel_id=1, replica_groups=mesh['groups'=2,'tensor'=4,'seq'=2,'load'=2] {'seq','load'}, dimensions={0}, use_global_device_ids=true | all-gather | bytes 655360 | tf_op jit(solution)/shard_map/all_gather | solution.py:165
  277.4 5.1 %fusion.46 = (f32[2,16,128]{2,1,0:T(8,128)S(1)}, bf16[2,16,128,512]{2,3,1,0:T(8,128)(2,1)}) fusion(pred[128,512]{0,1:T(8,128)(4,1)S(1)} %compare_and_fusion, bf16[128,2,16,128]{0,3,2,1:T(8,128)(2,1)S(1)} %bitcast.114, bf16[512,4,128]{2,0,1:T(8,128)(2,1)S(1)} %all_gather.22), kind=kOutput, calls=%fused_computation.134 | convolution fusion | flops 549454336 | bytes 5652480 | tf_op jit(solution)/shard_map/sub | solution.py:182
  282.5 4.1 %fusion.7 = bf16[128,2,16,128]{3,0,2,1:T(8,128)(2,1)S(1)} fusion(bf16[2,16,128,512]{2,3,1,0:T(8,128)(2,1)} %get-tuple-element.34, f32[128,2,16]{0,2,1:T(8,128)S(1)} %bitcast.138, bf16[512,4,128]{2,0,1:T(8,128)(2,1)S(1)} %all_gather.22), kind=kOutput, calls=%fused_computation.14 | convolution fusion | flops 537919488 | bytes 5521408 | tf_op jit(solution)/shard_map/ghqk,kgd->ghqd/dot_general | solution.py:184
  287.9 18.4 %all_to_all.5 = bf16[4,1,32,4608]{3,2,1,0:T(8,128)(2,1)S(1)} all-to-all(bf16[4,1,32,4608]{3,2,1,0:T(8,128)(2,1)S(1)} %maximum_bitcast_fusion), channel_id=1, replica_groups=mesh['groups'=2,'tensor'=4,'seq'=2,'load'=2] {'seq','load'}, dimensions={0} | all-to-all | bytes 2359296 | tf_op jit(solution)/shard_map/all_to_all | solution.py:195
  (131 shorter events, 38.9 us)
Async XLA Ops:
  8.0 19.5 %copy-start = (bf16[4096,128]{1,0:T(8,128)(2,1)S(1)}, bf16[4096,128]{1,0:T(8,128)(2,1)}, u32[]{:S(2)}) copy-start(bf16[4096,128]{1,0:T(8,128)(2,1)} %param.14) | copy-start | bytes 3145732
  8.0 180.5 %reduce-scatter.5.cloned.1.call-start = ((), (), s32[]{:S(2)}) async-start(), calls=%async_computation.5 | async-start | bytes 3031040 | tf_op jit(solution)/shard_map/reduce_scatter | solution.py:117
  9.9 16.9 %copy-start.2 = (bf16[4096,512]{1,0:T(8,128)(2,1)S(1)}, bf16[4096,512]{1,0:T(8,128)(2,1)}, u32[]{:S(2)}) copy-start(bf16[4096,512]{1,0:T(8,128)(2,1)} %param.12) | copy-start | bytes 12582916
  9.9 16.9 %copy-start.3 = (bf16[128,4096]{1,0:T(8,128)(2,1)S(1)}, bf16[128,4096]{1,0:T(8,128)(2,1)}, u32[]{:S(2)}) copy-start(bf16[128,4096]{1,0:T(8,128)(2,1)} %param.10) | copy-start | bytes 3145732
  26.7 1.4 copy-start.4
  27.5 1.1 copy-start.12
  27.6 1.1 copy-start.13
  32.7 155.9 %reduce-scatter.7.cloned.1.call-start = ((), (), s32[]{:S(2)}) async-start(), calls=%async_computation.6 | async-start | bytes 3031040 | tf_op jit(solution)/shard_map/reduce_scatter | solution.py:117
  32.7 28.3 %collective-permute-start = (bf16[128,4096]{1,0:T(8,128)(2,1)S(1)}, bf16[128,4096]{1,0:T(8,128)(2,1)S(1)}, u32[]{:S(2)}, u32[]{:S(2)}) collective-permute-start(bf16[128,4096]{1,0:T(8,128)(2,1)S(1)} %copy-done.3), channel_id=1, source_target_pairs={{0,4},{4,8},{8,12},{12,0},{1,5},{5,9},{9,13},{13,1},{2,6},{6,10},{... | collective-permute-start | bytes 3145736 | tf_op jit(solution)/shard_map/ppermute | solution.py:103
  84.4 104.1 %reduce-scatter.9.cloned.1.call-start = ((), (), s32[]{:S(2)}) async-start(), calls=%async_computation.7 | async-start | bytes 3031040 | tf_op jit(solution)/shard_map/reduce_scatter | solution.py:117
  84.5 26.4 %collective-permute-start.1 = (bf16[128,4096]{1,0:T(8,128)(2,1)S(1)}, bf16[128,4096]{1,0:T(8,128)(2,1)S(1)}, u32[]{:S(2)}, u32[]{:S(2)}) collective-permute-start(bf16[128,4096]{1,0:T(8,128)(2,1)S(1)} %collective-permute-done), channel_id=1, source_target_pairs={{0,4},{4,8},{8,12},{12,0},{1,5},{5,9},{9,13},{13,1},{2,6},{6,10},{... | collective-permute-start | bytes 3145736 | tf_op jit(solution)/shard_map/ppermute | solution.py:103
  134.3 80.0 %reduce-scatter.11.cloned.1.call-start = ((), (), s32[]{:S(2)}) async-start(), calls=%async_computation.8 | async-start | bytes 3031040 | tf_op jit(solution)/shard_map/reduce_scatter | solution.py:117
  134.4 25.2 %collective-permute-start.2 = (bf16[128,4096]{1,0:T(8,128)(2,1)S(1)}, bf16[128,4096]{1,0:T(8,128)(2,1)S(1)}, u32[]{:S(2)}, u32[]{:S(2)}) collective-permute-start(bf16[128,4096]{1,0:T(8,128)(2,1)S(1)} %collective-permute-done.1), channel_id=1, source_target_pairs={{0,4},{4,8},{8,12},{12,0},{1,5},{5,9},{9,13},{13,1},{2,6},{6,10},{... | collective-permute-start | bytes 3145736 | tf_op jit(solution)/shard_map/ppermute | solution.py:103
  183.1 1.9 copy-start.9
  183.1 54.1 %all-gather.3.cloned.1.call-start = ((), (), s32[]{:S(2)}) async-start(), calls=%async_computation.9 | async-start | bytes 6291456 | tf_op jit(solution)/shard_map/all_gather | solution.py:96
  220.4 14.6 %copy-start.10 = (f32[128]{0:T(128)S(1)}, f32[128]{0:T(128)}, u32[]{:S(2)}) copy-start(f32[128]{0:T(128)} %subtract_convert_fusion) | copy-start | bytes 1540
  234.5 7.0 %copy-start.6 = (f32[128,512]{1,0:T(8,128)}, f32[128,512]{1,0:T(8,128)S(1)}, u32[]{:S(2)}) copy-start(f32[128,512]{1,0:T(8,128)S(1)} %convolution_add_fusion.1) | copy-start | bytes 786436
  246.0 2.4 copy-start.5
  253.4 1.0 copy-start.7
  253.4 1.0 copy-start.8
  253.4 1.0 copy-start.11
  287.8 20.3 %copy-start.1 = (bf16[4096,128]{1,0:T(8,128)(2,1)S(1)}, bf16[4096,128]{1,0:T(8,128)(2,1)}, u32[]{:S(2)}) copy-start(bf16[4096,128]{1,0:T(8,128)(2,1)} %param.14) | copy-start | bytes 3145732
Sparse Core Ops, SparseCore 0:
  32.8 36.1 reduce-scatter.4
  84.6 32.8 reduce-scatter.6
  134.5 31.3 reduce-scatter.8
  183.2 31.1 reduce-scatter.10
Sparse Core Ops, SparseCore 1:
  185.1 11.2 all-gather.2

commit v2 on v0

--- a/solution.py
+++ b/solution.py
@@ -90,44 +90,44 @@
     keyval_cols = weight_keyval.shape[1]
     rank_share = down_query.shape[1] // TENANTS
     block_rows = tokens.shape[0] * tensor_count // block_count
+    up_query_all = lax.all_gather(up_query, "load", axis=0, tiled=True)
+    up_keyval_all = lax.all_gather(up_keyval, "load", axis=0, tiled=True)
     shard_rows = lax.all_gather(tokens, "tensor", axis=0, tiled=True)
     piece_ids = jnp.arange(shard_rows.shape[0], dtype=jnp.int32)
     piece_rank, piece_first, piece_hot = tenant_table(
         piece_ids, adapter_rank, token_lengths, adapter_slot
     )
-    columns_list = [
-        product(shard_rows, weight_query),
-        product(shard_rows, weight_keyval),
-        select_slot(product(shard_rows, down_query), piece_hot),
-        select_slot(product(shard_rows, down_keyval), piece_hot),
-    ]
-    partial_terms = jnp.concatenate(columns_list, axis=1)
-    summed = lax.psum_scatter(partial_terms, ("seq", "load"), scatter_dimension=0, tiled=True)
+    small_terms = jnp.concatenate(
+        [
+            product(shard_rows, weight_keyval),
+            select_slot(product(shard_rows, down_query), piece_hot),
+            select_slot(product(shard_rows, down_keyval), piece_hot),
+        ],
+        axis=1,
+    )
+    small_summed = lax.psum_scatter(small_terms, ("seq", "load"), scatter_dimension=0, tiled=True)
+    query_summed = lax.psum_scatter(
+        product(shard_rows, weight_query), ("seq", "load"), scatter_dimension=0, tiled=True
+    )
     token_ids = block_index * block_rows + jnp.arange(block_rows, dtype=jnp.int32)
     own_rank, own_first, slot_hot = tenant_table(
         token_ids, adapter_rank, token_lengths, adapter_slot
     )
     position = token_ids - own_first
-    low_start = query_cols + keyval_cols
     first_rank = tensor_index * rank_share
-    low_query = scale_ranks(summed[:, low_start : low_start + rank_share], own_rank, first_rank)
-    low_keyval = scale_ranks(summed[:, low_start + rank_share :], own_rank, first_rank)
-    full_query, full_keyval = (
-        lax.all_gather(low_query, "tensor", axis=1, tiled=True),
-        lax.all_gather(low_keyval, "tensor", axis=1, tiled=True),
+    low_query = scale_ranks(
+        small_summed[:, keyval_cols : keyval_cols + rank_share], own_rank, first_rank
     )
+    low_keyval = scale_ranks(small_summed[:, keyval_cols + rank_share :], own_rank, first_rank)
+    low_both = lax.all_gather(
+        jnp.concatenate([low_query, low_keyval], axis=1), "tensor", axis=1
+    )
+    full_query = low_both[:, :, :rank_share].reshape(block_rows, -1)
+    full_keyval = low_both[:, :, rank_share:].reshape(block_rows, -1)
     wide_query = widen_slots(full_query, slot_hot)
     wide_keyval = widen_slots(full_keyval, slot_hot)
-    up_query_all, up_keyval_all = (
-        lax.all_gather(up_query, "load", axis=0, tiled=True),
-        lax.all_gather(up_keyval, "load", axis=0, tiled=True),
-    )
-    delta_query = product(wide_query, up_query_all)
     delta_keyval = product(wide_keyval, up_keyval_all)
-    query_rows = rotate_pairs(
-        summed[:, :query_cols] + delta_query, position, tensor_index * query_cols
-    ).astype(jnp.bfloat16)
-    keyval = summed[:, query_cols:low_start] + delta_keyval
+    keyval = small_summed[:, :keyval_cols] + delta_keyval
     kv_first_col = tensor_index * keyval_cols
     is_key = kv_first_col + jnp.arange(keyval_cols, dtype=jnp.int32) < KV_HEADS * HEAD_DIM
     kv_local = jnp.where(
@@ -146,27 +146,31 @@
     value_heads = lax.dynamic_slice_in_dim(
         kv_all, key_cols + kv_first * HEAD_DIM, kv_here * HEAD_DIM, 1
     ).reshape(block_rows, kv_here, HEAD_DIM)
+    both_heads = lax.all_gather(
+        jnp.concatenate([key_heads, value_heads], axis=1), ("seq", "load"), axis=0, tiled=True
+    )
+    piece_keys = both_heads[:, :kv_here]
+    piece_values = both_heads[:, kv_here:]
+    delta_query = product(wide_query, up_query_all)
+    query_rows = rotate_pairs(
+        query_summed + delta_query, position, tensor_index * query_cols
+    ).astype(jnp.bfloat16)
     grouped = query_rows.reshape(block_rows, kv_here, per_kv, HEAD_DIM)
-    running_top = jnp.full((kv_here, per_kv, block_rows), -1e30, jnp.float32)
-    piece_keys = lax.all_gather(key_heads, ("seq", "load"), axis=0, tiled=True)
-    piece_values = lax.all_gather(value_heads, ("seq", "load"), axis=0, tiled=True)
     key_ids = jnp.arange(piece_keys.shape[0], dtype=jnp.int32)
     visible = (key_ids[None, :] >= own_first[:, None]) & (key_ids[None, :] <= token_ids[:, None])
     scores = jnp.einsum(
         "qghd,kgd->ghqk", grouped, piece_keys, preferred_element_type=jnp.float32
     ) / math.sqrt(HEAD_DIM)
     scores = jnp.where(visible, scores, -1e30)
-    new_top = jnp.maximum(running_top, jnp.max(scores, axis=3))
-    exp_scores = jnp.where(visible, jnp.exp(scores - new_top[..., None]), 0.0)
-    new_sum = jnp.sum(exp_scores, axis=3)
-    new_acc = jnp.einsum(
+    row_top = jnp.max(scores, axis=3)
+    exp_scores = jnp.where(visible, jnp.exp(scores - row_top[..., None]), 0.0)
+    row_total = jnp.sum(exp_scores, axis=3)
+    accumulated = jnp.einsum(
         "ghqk,kgd->ghqd",
         exp_scores.astype(jnp.bfloat16),
         piece_values,
         preferred_element_type=jnp.float32,
     )
-    state_tuple = (new_top, new_sum, new_acc)
-    final_top, row_total, accumulated = state_tuple
     context = (accumulated / row_total[..., None]).astype(jnp.bfloat16)
     context = jnp.transpose(context, (2, 0, 1, 3)).reshape(block_rows, query_cols)
     return (context, kv_local)

time: 308 us -> 247 us (0.80)
  waiting for transfers between devices: 161 us -> 114 us
  blocking collectives: 55.6 us -> 41.2 us
  other arithmetic: 20.6 us -> 10 us
  local copies, waits for them, and re-layouts: 6.82 us -> 13.8 us
  matrix products: 48 us -> 51.8 us
    reduce_scatter x1 -> x2, waiting for transfers between devices: 76.7 us -> 30.1 us  [the longest x1 30 us: shards(): lax.psum_scatter(product(shard_rows, weight_query), ('seq', 'load'), scat...]
    all_gather x5 -> x3, blocking collectives: 40.2 us -> 26.5 us  [the longest x1 13.1 us: shards(): lax.all_gather(jnp.concatenate([low_query, low_keyval], axis=1), 'tensor'...]
    concatenate x1 -> x3, other arithmetic: 9.75 us -> 1.13 us  [the longest x1 1.11 us: shards(): jnp.concatenate([product(shard_rows, weight_keyval), select_slot(product(...]
    sub x0 -> x1, matrix products: none -> 5.13 us  [shards(): exp_scores = jnp.where(visible, jnp.exp(scores - row_top[..., None]), 0.0)]
    unnamed x22 -> x20, local copies, waits for them, and re-layouts: 3.76 us -> 7.72 us
  transfers between devices with their start and end apart: 3 -> 4, of which waited for: 2 -> 2; matrix products, arithmetic and copies ran while one was open for 2% -> 13% of each run, Pallas kernels for 0% -> 0%
where the time goes in v2:
time: 247 us
  waiting for transfers between devices  114 us (46%)
  matrix products  51.8 us (21%)
  blocking collectives  41.2 us (17%)
  between operations  15.5 us (6%)
  local copies, waits for them, and re-layouts  13.8 us (6%)
  other arithmetic  10 us (4%)
    all_gather x1, waiting for transfers between devices, shards(): shard_rows = lax.all_gather(tokens, 'tensor', axis=0, tiled=True)  82.8 us
    dot_general x6, matrix products, product(): return jnp.dot(left, right, preferred_element_type=jnp.float32)  43.6 us
    reduce_scatter x1, waiting for transfers between devices, shards(): lax.psum_scatter(product(shard_rows, weight_query), ('seq', 'load'), scat...  30 us
    all_gather x1, blocking collectives, shards(): kv_all = lax.all_gather(kv_local, 'tensor', axis=1, tiled=True)  14.8 us
    all_gather x1, blocking collectives, shards(): lax.all_gather(jnp.concatenate([low_query, low_keyval], axis=1), 'tensor'...  13.1 us
    all_gather x1, blocking collectives, shards(): lax.all_gather(jnp.concatenate([key_heads, value_heads], axis=1), ('seq',...  11.2 us
    unnamed x20, local copies, waits for them, and re-layouts  7.72 us
    sub x1, matrix products, shards(): exp_scores = jnp.where(visible, jnp.exp(scores - row_top[..., None]), 0.0)  5.13 us
  transfers between devices with their start and end apart: 4, of which 2 were waited for; matrix products, arithmetic and copies ran while one was open for 13% of the time, Pallas kernels for 0%

profile of v2, /device:TPU:0, one launch (start us, length us, event | category | flops | bytes accessed | tf_op | source)
XLA Modules:
  0.0 246.6 jit_solution(16451269611372410420)
XLA Ops:
  8.8 0.9 reduce-window.8
  11.1 82.8 %all-gather.4.cloned.1.call-done = bf16[512,4096]{1,0:T(8,128)(2,1)} async-done(((bf16[128,4096]{1,0:T(8,128)(2,1)}), bf16[512,4096]{1,0:T(8,128)(2,1)}) %all-gather.4.cloned.1.call-update) | async-done | bytes 4194320 | tf_op jit(solution)/shard_map/all_gather | solution.py:95
  93.9 3.7 %fusion.47 = f32[512,128]{0,1:T(8,128)S(1)} fusion(bf16[512,4096]{1,0:T(8,128)(2,1)} %all-gather.4.cloned.1.call-done, bf16[4096,128]{1,0:T(8,128)(2,1)S(1)} %copy-done), kind=kOutput, calls=%fused_computation.104 | convolution fusion | flops 536870912 | bytes 5505024 | tf_op jit(solution)/shard_map/dot_general | solution.py:19
  97.7 3.7 %fusion.48 = f32[512,128]{0,1:T(8,128)S(1)} fusion(bf16[512,4096]{1,0:T(8,128)(2,1)} %all-gather.4.cloned.1.call-done, bf16[4096,128]{1,0:T(8,128)(2,1)S(1)} %copy-done.2), kind=kOutput, calls=%fused_computation.105 | convolution fusion | flops 536870912 | bytes 5505024 | tf_op jit(solution)/shard_map/dot_general | solution.py:19
  101.9 5.8 %fusion.46 = f32[512,512]{0,1:T(8,128)S(1)} fusion(bf16[512,4096]{1,0:T(8,128)(2,1)} %all-gather.4.cloned.1.call-done, bf16[4096,512]{1,0:T(8,128)(2,1)} %param.12), kind=kOutput, calls=%fused_computation.103 | convolution fusion | flops 2147483648 | bytes 9437184 | tf_op jit(solution)/shard_map/dot_general | solution.py:19
  107.7 1.1 pad_maximum_fusion
  109.5 24.1 %fusion.49 = f32[512,4096]{1,0:T(8,128)} fusion(bf16[512,4096]{1,0:T(8,128)(2,1)} %all-gather.4.cloned.1.call-done, bf16[4096,4096]{1,0:T(8,128)(2,1)} %param.11), kind=kOutput, calls=%fused_computation.106 | convolution fusion | flops 17179869184 | bytes 46137344 | tf_op jit(solution)/shard_map/dot_general | solution.py:19
  134.5 2.2 all_gather.24
  136.8 0.8 fusion.28
  137.6 13.1 %all-gather = bf16[128,256]{0,1:T(8,128)(2,1)S(1)} all-gather(bf16[128,64]{0,1:T(8,128)(2,1)S(1)} %pad_maximum_fusion.4), channel_id=2, replica_groups=mesh['groups'=2,'tensor'=4,'seq'=2,'load'=2] {'tensor'}, dimensions={1}, use_global_device_ids=true | all-gather | bytes 81920 | tf_op jit(solution)/shard_map/all_gather | solution.py:122
  150.9 1.3 convolution_add_fusion.1
  154.3 14.8 %all_gather.25 = bf16[128,2048]{0,1:T(8,128)(2,1)S(1)} all-gather(bf16[128,512]{0,1:T(8,128)(2,1)S(1)} %select_convert_fusion), channel_id=1, replica_groups=mesh['groups'=2,'tensor'=4,'seq'=2,'load'=2] {'tensor'}, dimensions={1}, use_global_device_ids=true | all-gather | bytes 655360 | tf_op jit(solution)/shard_map/all_gather | solution.py:136
  169.3 11.2 %all_gather.26 = bf16[512,4,128]{2,0,1:T(8,128)(2,1)} all-gather(bf16[128,4,128]{2,0,1:T(8,128)(2,1)S(1)} %pad_maximum_fusion.3), channel_id=1, replica_groups=mesh['groups'=2,'tensor'=4,'seq'=2,'load'=2] {'seq','load'}, dimensions={0}, use_global_device_ids=true | all-gather | bytes 655360 | tf_op jit(solution)/shard_map/all_gather | solution.py:149
  180.5 30.0 %reduce-scatter.5.cloned.1.call-done = f32[128,4096]{1,0:T(8,128)} async-done(((f32[512,4096]{1,0:T(8,128)}), f32[128,4096]{1,0:T(8,128)}) %reduce-scatter.5.cloned.1.call-update) | async-done | bytes 2097168 | tf_op jit(solution)/shard_map/reduce_scatter | solution.py:109
  210.5 5.0 %convolution_add_fusion = f32[128,4096]{1,0:T(8,128)} fusion(f32[128,4096]{1,0:T(8,128)} %reduce-scatter.5.cloned.1.call-done, bf16[128,512]{0,1:T(8,128)(2,1)S(1)} %bitcast.73, bf16[512,4096]{1,0:T(8,128)(2,1)} %all-gather.6.cloned.1.call-done), kind=kOutput, calls=%fused_computation.4 | convolution fusion | flops 537395200 | bytes 8519680 | tf_op jit(solution)/shard_map/dot_general | solution.py:19
  215.5 1.9 copy.55
  217.4 2.6 %fusion.42 = (f32[128,2048,1]{0,2,1:T(1,128)}, f32[128,2048,1]{0,2,1:T(1,128)}) fusion(f32[128,2048,2]{0,2,1:T(2,128)S(1)} %bitcast.69), kind=kLoop, calls=%fused_computation.99 | loop fusion | bytes 4194304 | tf_op jit(solution)/shard_map/slice | solution.py:30
  220.1 2.3 copy.73
  222.4 2.3 copy.74
  224.8 4.2 %fusion.15 = (bf16[128,2048,1]{1,0,2:T(8,128)(2,1)S(1)}, bf16[128,2048,1]{1,0,2:T(8,128)(2,1)S(1)}) fusion(f32[128,2048,1]{1,0,2:T(8,128)S(1)} %copy.74, f32[128,2048,1]{1,0,2:T(8,128)S(1)} %copy.73, f32[2048]{0:T(1024)S(1)} %fusion.36, f32[128]{0:T(128)S(1)} %subtract_convert_fusion), kind=kLoop, calls=%fused_computation.21 | loop fusion | flops 2359296 | bytes 3154432 | tf_op jit(solution)/shard_map/convert
  229.1 0.8 copy.58
  229.9 5.1 %fusion.45 = (f32[2,16,128]{2,1,0:T(8,128)S(1)}, bf16[2,16,128,512]{2,3,1,0:T(8,128)(2,1)}) fusion(pred[128,512]{0,1:T(8,128)(4,1)S(1)} %fusion.20, bf16[128,2,16,128]{0,3,2,1:T(8,128)(2,1)S(1)} %bitcast.71, bf16[512,4,128]{2,0,1:T(8,128)(2,1)S(1)} %copy-done.3), kind=kOutput, calls=%fused_computation.102 | convolution fusion | flops 549454336 | bytes 5652480 | tf_op jit(solution)/shard_map/sub | solution.py:166
  235.1 3.0 %fusion.7 = bf16[128,2,16,128]{0,3,2,1:T(8,128)(2,1)S(1)} fusion(bf16[2,16,128,512]{2,3,1,0:T(8,128)(2,1)} %get-tuple-element.34, f32[128,2,16]{0,2,1:T(8,128)S(1)} %bitcast.84, bf16[512,4,128]{2,0,1:T(8,128)(2,1)S(1)} %copy-done.3), kind=kOutput, calls=%fused_computation.11 | convolution fusion | flops 537919488 | bytes 5521408 | tf_op jit(solution)/shard_map/ghqk,kgd->ghqd/dot_general | solution.py:168
  238.1 1.3 copy.62
  (56 shorter events, 6.9 us)
Async XLA Ops:
  8.0 85.9 %copy-start = (bf16[4096,128]{1,0:T(8,128)(2,1)S(1)}, bf16[4096,128]{1,0:T(8,128)(2,1)}, u32[]{:S(2)}) copy-start(bf16[4096,128]{1,0:T(8,128)(2,1)} %param.13) | copy-start | bytes 3145732
  8.0 85.9 %all-gather.4.cloned.1.call-start = ((), (), s32[]{:S(2)}) async-start(), calls=%async_computation.2 | async-start | bytes 5242880 | tf_op jit(solution)/shard_map/all_gather | solution.py:95
  8.7 89.0 %copy-start.2 = (bf16[4096,128]{1,0:T(8,128)(2,1)S(1)}, bf16[4096,128]{1,0:T(8,128)(2,1)}, u32[]{:S(2)}) copy-start(bf16[4096,128]{1,0:T(8,128)(2,1)} %param.14) | copy-start | bytes 3145732
  8.8 128.1 %reduce-scatter.3.cloned.1.call-start = ((), (), s32[]{:S(2)}) async-start(), calls=%async_computation.3 | async-start | bytes 1474560 | tf_op jit(solution)/shard_map/reduce_scatter | solution.py:108
  108.8 71.7 %all-gather.6.cloned.1.call-start = ((), (), s32[]{:S(2)}) async-start(), calls=%async_computation.5 | async-start | bytes 6291456 | tf_op jit(solution)/shard_map/all_gather | solution.py:93
  109.4 101.1 %reduce-scatter.5.cloned.1.call-start = ((), (), s32[]{:S(2)}) async-start(), calls=%async_computation.4 | async-start | bytes 10485760 | tf_op jit(solution)/shard_map/reduce_scatter | solution.py:109
  133.5 0.7 copy-start.5
  133.5 0.7 copy-start.6
  133.5 1.0 copy-start.4
  224.8 5.1 %copy-start.3 = (bf16[512,4,128]{2,0,1:T(8,128)(2,1)S(1)}, bf16[512,4,128]{2,0,1:T(8,128)(2,1)}, u32[]{:S(2)}) copy-start(bf16[512,4,128]{2,0,1:T(8,128)(2,1)} %all_gather.26) | copy-start | bytes 1572868
  235.1 4.4 %copy-start.1 = (bf16[4096,128]{1,0:T(8,128)(2,1)S(1)}, bf16[4096,128]{1,0:T(8,128)(2,1)}, u32[]{:S(2)}) copy-start(bf16[4096,128]{1,0:T(8,128)(2,1)} %param.13) | copy-start | bytes 3145732
Sparse Core Ops, SparseCore 0:
  10.4 83.4 all-gather.3
  108.9 24.2 reduce-scatter.2
  136.0 74.4 reduce-scatter.4
Sparse Core Ops, SparseCore 1:
  110.8 12.1 all-gather.5

commit v3 on v2

--- a/solution.py
+++ b/solution.py
@@ -106,8 +106,18 @@
         axis=1,
     )
     small_summed = lax.psum_scatter(small_terms, ("seq", "load"), scatter_dimension=0, tiled=True)
+    seq_count = lax.axis_size("seq")
+    load_count = lax.axis_size("load")
+    by_core = shard_rows.reshape(seq_count, load_count, block_rows, -1)
+    core_terms = jnp.stack(
+        [
+            product(by_core[:, core].reshape(seq_count * block_rows, -1), weight_query)
+            for core in range(load_count)
+        ]
+    )
+    core_summed = lax.psum_scatter(core_terms, "load", scatter_dimension=0, tiled=True)
     query_summed = lax.psum_scatter(
-        product(shard_rows, weight_query), ("seq", "load"), scatter_dimension=0, tiled=True
+        core_summed.reshape(seq_count * block_rows, -1), "seq", scatter_dimension=0, tiled=True
     )
     token_ids = block_index * block_rows + jnp.arange(block_rows, dtype=jnp.int32)
     own_rank, own_first, slot_hot = tenant_table(
@@ -151,7 +161,7 @@
     )
     piece_keys = both_heads[:, :kv_here]
     piece_values = both_heads[:, kv_here:]
-    delta_query = product(wide_query, up_query_all)
+    delta_query = lax.optimization_barrier(product(wide_query, up_query_all))
     query_rows = rotate_pairs(
         query_summed + delta_query, position, tensor_index * query_cols
     ).astype(jnp.bfloat16)

time: 247 us -> 288 us (1.17)
  waiting for transfers between devices: 114 us -> 139 us
  matrix products: 51.8 us -> 59.7 us
  other arithmetic: 10 us -> 14.9 us
  local copies, waits for them, and re-layouts: 13.8 us -> 17.4 us
    reduce_scatter x1, waiting for transfers between devices: 0.02 us -> 23.8 us  [shards(): lax.psum_scatter(small_terms, ('seq', 'load'), scatter_dimension=0, tiled...]
    dot_general x6 -> x7, matrix products: 43.6 us -> 50.2 us  [product(): return jnp.dot(left, right, preferred_element_type=jnp.float32)]
    slice x0 -> x1, local copies, waits for them, and re-layouts: none -> 3.96 us  [shards(): by_core[:, core].reshape(seq_count * block_rows, -1)]
    add x0 -> x1, other arithmetic: none -> 3.11 us  [shards(): query_summed + delta_query]
    another operation x2 -> x3, other arithmetic: 5.13 us -> 8.16 us
    reduce_scatter x1 -> x2, waiting for transfers between devices: 30 us -> 28 us  [the longest x1 28 us: shards(): lax.psum_scatter(core_summed.reshape(seq_count * block_rows, -1), 'seq',...]
    unnamed x20 -> x18, local copies, waits for them, and re-layouts: 7.72 us -> 7.38 us
  transfers between devices with their start and end apart: 4 -> 5, of which waited for: 2 -> 3; matrix products, arithmetic and copies ran while one was open for 13% -> 9% of each run, Pallas kernels for 0% -> 0%
where the time goes in v3:
time: 288 us; the launch traced here: 287 us
  waiting for transfers between devices  139 us (48%)
  matrix products  59.7 us (21%)
  blocking collectives  42.2 us (15%)
  local copies, waits for them, and re-layouts  17.4 us (6%)
  other arithmetic  14.9 us (5%)
  between operations  14.1 us (5%)
    all_gather x1, waiting for transfers between devices, shards(): shard_rows = lax.all_gather(tokens, 'tensor', axis=0, tiled=True)  85.1 us
    dot_general x7, matrix products, product(): return jnp.dot(left, right, preferred_element_type=jnp.float32)  50.2 us
    reduce_scatter x1, waiting for transfers between devices, shards(): lax.psum_scatter(core_summed.reshape(seq_count * block_rows, -1), 'seq',...  28 us
    reduce_scatter x1, waiting for transfers between devices, shards(): lax.psum_scatter(small_terms, ('seq', 'load'), scatter_dimension=0, tiled...  23.8 us
    all_gather x1, blocking collectives, shards(): kv_all = lax.all_gather(kv_local, 'tensor', axis=1, tiled=True)  16 us
    all_gather x1, blocking collectives, shards(): lax.all_gather(jnp.concatenate([low_query, low_keyval], axis=1), 'tensor'...  13.2 us
    all_gather x1, blocking collectives, shards(): lax.all_gather(jnp.concatenate([key_heads, value_heads], axis=1), ('seq',...  10.8 us
    unnamed x18, local copies, waits for them, and re-layouts  7.38 us
  transfers between devices with their start and end apart: 5, of which 3 were waited for; matrix products, arithmetic and copies ran while one was open for 9% of the time, Pallas kernels for 0%

profile of v3, /device:TPU:0, one launch (start us, length us, event | category | flops | bytes accessed | tf_op | source)
XLA Modules:
  0.0 287.3 jit_solution(13952558010459111787)
XLA Ops:
  8.0 85.1 %all-gather.4.cloned.1.call-done = bf16[512,4096]{1,0:T(8,128)(2,1)} async-done(((bf16[128,4096]{1,0:T(8,128)(2,1)}), bf16[512,4096]{1,0:T(8,128)(2,1)}) %all-gather.4.cloned.1.call-update) | async-done | bytes 4194320 | tf_op jit(solution)/shard_map/all_gather | solution.py:95
  93.1 4.0 %fusion.42 = (bf16[2,1,128,4096]{3,2,1,0:T(8,128)(2,1)}, bf16[2,1,128,4096]{3,2,1,0:T(8,128)(2,1)S(1)}) fusion(bf16[2,2,128,4096]{3,2,1,0:T(8,128)(2,1)} %bitcast.79), kind=kLoop, calls=%fused_computation.101 | loop fusion | bytes 8388608 | tf_op jit(solution)/shard_map/slice | solution.py:114
  97.0 15.1 %convolution_bitcast_fusion = f32[1,256,4096]{2,1,0:T(8,128)S(1)} fusion(bf16[256,4096]{1,0:T(8,128)(2,1)S(1)} %bitcast.84, bf16[4096,4096]{1,0:T(8,128)(2,1)} %param.11), kind=kOutput, calls=%fused_computation.5 | convolution fusion | flops 8589934592 | bytes 39845888 | tf_op jit(solution)/shard_map/dot_general | solution.py:19
  112.1 15.7 %convolution_bitcast_fusion.1 = f32[1,256,4096]{2,1,0:T(8,128)S(1)} fusion(bf16[256,4096]{1,0:T(8,128)(2,1)} %bitcast.83, bf16[4096,4096]{1,0:T(8,128)(2,1)} %param.11), kind=kOutput, calls=%fused_computation.6 | convolution fusion | flops 8589934592 | bytes 39845888 | tf_op jit(solution)/shard_map/dot_general | solution.py:19
  127.8 3.8 %pad_maximum_fusion = f32[2,256,4096]{2,1,0:T(8,128)} fusion(f32[1,256,4096]{2,1,0:T(8,128)S(1)} %convolution_bitcast_fusion, f32[1,256,4096]{2,1,0:T(8,128)S(1)} %convolution_bitcast_fusion.1), kind=kLoop, calls=%fused_computation.1 | loop fusion | flops 2097152 | bytes 16777216 | tf_op jit(solution)/shard_map/stack | solution.py:112
  132.5 3.7 %fusion.48 = f32[512,128]{0,1:T(8,128)S(1)} fusion(bf16[512,4096]{1,0:T(8,128)(2,1)} %all-gather.4.cloned.1.call-done, bf16[4096,128]{1,0:T(8,128)(2,1)S(1)} %copy-done), kind=kOutput, calls=%fused_computation.107 | convolution fusion | flops 536870912 | bytes 5505024 | tf_op jit(solution)/shard_map/dot_general | solution.py:19
  136.3 3.8 %fusion.49 = f32[512,128]{0,1:T(8,128)S(1)} fusion(bf16[512,4096]{1,0:T(8,128)(2,1)} %all-gather.4.cloned.1.call-done, bf16[4096,128]{1,0:T(8,128)(2,1)S(1)} %copy-done.1), kind=kOutput, calls=%fused_computation.108 | convolution fusion | flops 536870912 | bytes 5505024 | tf_op jit(solution)/shard_map/dot_general | solution.py:19
  140.6 7.7 %fusion.47 = f32[512,512]{0,1:T(8,128)S(1)} fusion(bf16[512,4096]{1,0:T(8,128)(2,1)} %all-gather.4.cloned.1.call-done, bf16[4096,512]{1,0:T(8,128)(2,1)} %param.12), kind=kOutput, calls=%fused_computation.106 | convolution fusion | flops 2147483648 | bytes 9437184 | tf_op jit(solution)/shard_map/dot_general | solution.py:19
  150.8 2.2 all_gather.24
  153.1 23.8 %reduce-scatter.4.cloned.1.call-done = f32[128,576]{0,1:T(8,128)} async-done(((f32[512,576]{0,1:T(8,128)}), f32[128,576]{0,1:T(8,128)}) %reduce-scatter.4.cloned.1.call-update) | async-done | bytes 294928 | tf_op jit(solution)/shard_map/reduce_scatter | solution.py:108
  177.7 13.2 %all-gather = bf16[128,256]{0,1:T(8,128)(2,1)S(1)} all-gather(bf16[128,64]{0,1:T(8,128)(2,1)S(1)} %pad_maximum_fusion.5), channel_id=2, replica_groups=mesh['groups'=2,'tensor'=4,'seq'=2,'load'=2] {'tensor'}, dimensions={1}, use_global_device_ids=true | all-gather | bytes 81920 | tf_op jit(solution)/shard_map/all_gather | solution.py:132
  194.4 16.0 %all_gather.25 = bf16[128,2048]{0,1:T(8,128)(2,1)S(1)} all-gather(bf16[128,512]{0,1:T(8,128)(2,1)S(1)} %select_convert_fusion), channel_id=1, replica_groups=mesh['groups'=2,'tensor'=4,'seq'=2,'load'=2] {'tensor'}, dimensions={1}, use_global_device_ids=true | all-gather | bytes 655360 | tf_op jit(solution)/shard_map/all_gather | solution.py:146
  210.7 3.0 %fusion.50 = f32[128,4096]{1,0:T(8,128)S(1)} fusion(bf16[128,512]{0,1:T(8,128)(2,1)S(1)} %bitcast.87, bf16[512,4096]{1,0:T(8,128)(2,1)} %all-gather.6.cloned.1.call-done), kind=kOutput, calls=%fused_computation.109 | convolution fusion | flops 536870912 | bytes 6422528 | tf_op jit(solution)/shard_map/dot_general | solution.py:19
  213.7 10.8 %all_gather.26 = bf16[512,4,128]{2,0,1:T(8,128)(2,1)} all-gather(bf16[128,4,128]{2,0,1:T(8,128)(2,1)S(1)} %pad_maximum_fusion.4), channel_id=1, replica_groups=mesh['groups'=2,'tensor'=4,'seq'=2,'load'=2] {'seq','load'}, dimensions={0}, use_global_device_ids=true | all-gather | bytes 655360 | tf_op jit(solution)/shard_map/all_gather | solution.py:159
  224.5 28.0 %reduce-scatter.8.cloned.1.call-done = f32[128,4096]{1,0:T(8,128)} async-done(((f32[256,4096]{1,0:T(8,128)}), f32[128,4096]{1,0:T(8,128)}) %reduce-scatter.8.cloned.1.call-update) | async-done | bytes 2097168 | tf_op jit(solution)/shard_map/reduce_scatter | solution.py:119
  252.5 3.1 %add.135 = f32[128,4096]{1,0:T(8,128)} add(f32[128,4096]{1,0:T(8,128)} %reduce-scatter.8.cloned.1.call-done, f32[128,4096]{1,0:T(8,128)S(1)} %fusion.50) | non-fusion elementwise | flops 524288 | bytes 6291456 | tf_op jit(solution)/shard_map/add | solution.py:166
  255.6 1.9 copy.55
  257.5 2.6 fusion.43
  260.1 2.3 copy.73
  262.5 2.3 copy.74
  264.8 4.2 %fusion.15 = (bf16[128,2048,1]{1,0,2:T(8,128)(2,1)S(1)}, bf16[128,2048,1]{1,0,2:T(8,128)(2,1)S(1)}) fusion(f32[128,2048,1]{1,0,2:T(8,128)S(1)} %copy.74, f32[128,2048,1]{1,0,2:T(8,128)S(1)} %copy.73, f32[2048]{0:T(1024)S(1)} %fusion.36, f32[128]{0:T(128)S(1)} %subtract_convert_fusion), kind=kLoop, calls=%fused_computation.23 | loop fusion | flops 2359296 | bytes 3154432 | tf_op jit(solution)/shard_map/convert
  270.0 6.5 %fusion.46 = (f32[2,16,128]{2,1,0:T(8,128)S(1)}, bf16[2,16,128,512]{2,3,1,0:T(8,128)(2,1)}) fusion(pred[128,512]{0,1:T(8,128)(4,1)S(1)} %fusion.20, bf16[128,2,16,128]{0,3,2,1:T(8,128)(2,1)S(1)} %bitcast.85, bf16[512,4,128]{2,0,1:T(8,128)(2,1)} %all_gather.26), kind=kOutput, calls=%fused_computation.105 | convolution fusion | flops 549454336 | bytes 5652480 | tf_op jit(solution)/shard_map/sub | solution.py:176
  276.5 3.0 %fusion.7 = bf16[128,2,16,128]{0,3,2,1:T(8,128)(2,1)S(1)} fusion(bf16[2,16,128,512]{2,3,1,0:T(8,128)(2,1)} %get-tuple-element.36, f32[128,2,16]{0,2,1:T(8,128)S(1)} %bitcast.98, bf16[512,4,128]{2,0,1:T(8,128)(2,1)} %all_gather.26), kind=kOutput, calls=%fused_computation.13 | convolution fusion | flops 537919488 | bytes 5521408 | tf_op jit(solution)/shard_map/ghqk,kgd->ghqd/dot_general | solution.py:178
  279.5 1.3 copy.62
  (61 shorter events, 10.1 us)
Async XLA Ops:
  7.2 125.4 %copy-start = (bf16[4096,128]{1,0:T(8,128)(2,1)S(1)}, bf16[4096,128]{1,0:T(8,128)(2,1)}, u32[]{:S(2)}) copy-start(bf16[4096,128]{1,0:T(8,128)(2,1)} %param.13) | copy-start | bytes 3145732
  7.2 85.9 %all-gather.4.cloned.1.call-start = ((), (), s32[]{:S(2)}) async-start(), calls=%async_computation.3 | async-start | bytes 5242880 | tf_op jit(solution)/shard_map/all_gather | solution.py:95
  7.9 142.1 %reduce-scatter.6.cloned.1.call-start = ((), (), s32[]{:S(2)}) async-start(), calls=%async_computation.5 | async-start | bytes 12582912 | tf_op jit(solution)/shard_map/reduce_scatter | solution.py:118
  131.6 0.7 copy-start.5
  131.6 0.8 copy-start.3
  131.6 4.7 %copy-start.1 = (bf16[4096,128]{1,0:T(8,128)(2,1)S(1)}, bf16[4096,128]{1,0:T(8,128)(2,1)}, u32[]{:S(2)}) copy-start(bf16[4096,128]{1,0:T(8,128)(2,1)} %param.14) | copy-start | bytes 3145732
  131.6 45.3 %reduce-scatter.4.cloned.1.call-start = ((), (), s32[]{:S(2)}) async-start(), calls=%async_computation.4 | async-start | bytes 1474560 | tf_op jit(solution)/shard_map/reduce_scatter | solution.py:108
  149.4 1.3 copy-start.4
  149.4 1.4 copy-start.2
  149.4 61.3 %all-gather.6.cloned.1.call-start = ((), (), s32[]{:S(2)}) async-start(), calls=%async_computation.7 | async-start | bytes 6291456 | tf_op jit(solution)/shard_map/all_gather | solution.py:93
  150.0 102.5 %reduce-scatter.8.cloned.1.call-start = ((), (), s32[]{:S(2)}) async-start(), calls=%async_computation.6 | async-start | bytes 6291456 | tf_op jit(solution)/shard_map/reduce_scatter | solution.py:119
Sparse Core Ops, SparseCore 0:
  9.6 83.4 all-gather.3
  131.7 15.3 reduce-scatter.5
  149.9 26.9 reduce-scatter.3
  178.3 13.6 all-gather.5
  194.1 58.2 reduce-scatter.7

commit v4 on v2

--- a/solution.py
+++ b/solution.py
@@ -92,23 +92,38 @@
     block_rows = tokens.shape[0] * tensor_count // block_count
     up_query_all = lax.all_gather(up_query, "load", axis=0, tiled=True)
     up_keyval_all = lax.all_gather(up_keyval, "load", axis=0, tiled=True)
-    shard_rows = lax.all_gather(tokens, "tensor", axis=0, tiled=True)
-    piece_ids = jnp.arange(shard_rows.shape[0], dtype=jnp.int32)
+    piece_ids = jnp.arange(tokens.shape[0] * tensor_count, dtype=jnp.int32)
     piece_rank, piece_first, piece_hot = tenant_table(
         piece_ids, adapter_rank, token_lengths, adapter_slot
     )
-    small_terms = jnp.concatenate(
-        [
-            product(shard_rows, weight_keyval),
-            select_slot(product(shard_rows, down_query), piece_hot),
-            select_slot(product(shard_rows, down_keyval), piece_hot),
-        ],
-        axis=1,
-    )
+    halves = 2
+    half = tokens.shape[1] // halves
+    gathered = [
+        lax.all_gather(tokens[:, part * half : (part + 1) * half], "tensor", axis=0, tiled=True)
+        for part in range(halves)
+    ]
+    small_terms = None
+    query_terms = None
+    for part in range(halves):
+        rows_part = gathered[part]
+        if small_terms is not None:
+            rows_part, small_terms, query_terms = lax.optimization_barrier(
+                (rows_part, small_terms, query_terms)
+            )
+        feats = slice(part * half, (part + 1) * half)
+        small_part = jnp.concatenate(
+            [
+                product(rows_part, weight_keyval[feats]),
+                select_slot(product(rows_part, down_query[feats]), piece_hot),
+                select_slot(product(rows_part, down_keyval[feats]), piece_hot),
+            ],
+            axis=1,
+        )
+        query_part = product(rows_part, weight_query[feats])
+        small_terms = small_part if small_terms is None else small_terms + small_part
+        query_terms = query_part if query_terms is None else query_terms + query_part
     small_summed = lax.psum_scatter(small_terms, ("seq", "load"), scatter_dimension=0, tiled=True)
-    query_summed = lax.psum_scatter(
-        product(shard_rows, weight_query), ("seq", "load"), scatter_dimension=0, tiled=True
-    )
+    query_summed = lax.psum_scatter(query_terms, ("seq", "load"), scatter_dimension=0, tiled=True)
     token_ids = block_index * block_rows + jnp.arange(block_rows, dtype=jnp.int32)
     own_rank, own_first, slot_hot = tenant_table(
         token_ids, adapter_rank, token_lengths, adapter_slot
@@ -151,7 +166,7 @@
     )
     piece_keys = both_heads[:, :kv_here]
     piece_values = both_heads[:, kv_here:]
-    delta_query = product(wide_query, up_query_all)
+    delta_query = lax.optimization_barrier(product(wide_query, up_query_all))
     query_rows = rotate_pairs(
         query_summed + delta_query, position, tensor_index * query_cols
     ).astype(jnp.bfloat16)

time: 247 us -> 257 us (1.040)
  matrix products: 51.8 us -> 60.9 us
  waiting for transfers between devices: 114 us -> 106 us
  other arithmetic: 10 us -> 13.9 us
  local copies, waits for them, and re-layouts: 13.8 us -> 17.2 us
    all_gather x1 -> x2, waiting for transfers between devices: 82.8 us -> 71.8 us  [shards(): lax.all_gather(tokens[:, part * half:(part + 1) * half], 'tensor', axis=0...]
    dot_general x6 -> x10, matrix products: 43.6 us -> 52.8 us  [product(): return jnp.dot(left, right, preferred_element_type=jnp.float32)]
    add x0 -> x2, other arithmetic: none -> 5.67 us  [the longest x1 3.16 us: shards(): query_summed + delta_query]
    reduce_scatter x1, waiting for transfers between devices: 0.02 us -> 3.76 us  [shards(): lax.psum_scatter(small_terms, ('seq', 'load'), scatter_dimension=0, tiled...]
    reshape x2 -> x4, local copies, waits for them, and re-layouts: 0.15 us -> 2.9 us  [select_slot(): shaped = down_values.reshape(down_values.shape[0], -1, TENANTS)]
    unnamed x20 -> x24, local copies, waits for them, and re-layouts: 7.72 us -> 6.15 us
  transfers between devices with their start and end apart: 4 -> 5, of which waited for: 2 -> 4; matrix products, arithmetic and copies ran while one was open for 13% -> 18% of each run, Pallas kernels for 0% -> 0%
where the time goes in v4:
time: 257 us; the launch traced here: 256 us
  waiting for transfers between devices  106 us (41%)
  matrix products  60.9 us (24%)
  blocking collectives  42.2 us (16%)
  local copies, waits for them, and re-layouts  17.2 us (7%)
  between operations  15.6 us (6%)
  other arithmetic  13.9 us (5%)
    all_gather x2, waiting for transfers between devices, shards(): lax.all_gather(tokens[:, part * half:(part + 1) * half], 'tensor', axis=0...  71.8 us
    dot_general x10, matrix products, product(): return jnp.dot(left, right, preferred_element_type=jnp.float32)  52.8 us
    reduce_scatter x1, waiting for transfers between devices, shards(): lax.psum_scatter(query_terms, ('seq', 'load'), scatter_dimension=0, tiled...  29.5 us
    all_gather x1, blocking collectives, shards(): kv_all = lax.all_gather(kv_local, 'tensor', axis=1, tiled=True)  15.9 us
    all_gather x1, blocking collectives, shards(): lax.all_gather(jnp.concatenate([low_query, low_keyval], axis=1), 'tensor'...  13.2 us
    all_gather x1, blocking collectives, shards(): lax.all_gather(jnp.concatenate([key_heads, value_heads], axis=1), ('seq',...  10.8 us
    unnamed x24, local copies, waits for them, and re-layouts  6.15 us
  transfers between devices with their start and end apart: 5, of which 4 were waited for; matrix products, arithmetic and copies ran while one was open for 18% of the time, Pallas kernels for 0%

profile of v4, /device:TPU:0, one launch (start us, length us, event | category | flops | bytes accessed | tf_op | source)
XLA Modules:
  0.0 256.4 jit_solution(12737314236397675055)
XLA Ops:
  8.1 2.4 fusion.62
  11.6 48.1 %all-gather.7.cloned.1.call-done = bf16[512,2048]{1,0:T(8,128)(2,1)} async-done(((bf16[128,2048]{1,0:T(8,128)(2,1)}), bf16[512,2048]{1,0:T(8,128)(2,1)}) %all-gather.7.cloned.1.call-update) | async-done | bytes 2097168 | tf_op jit(solution)/shard_map/all_gather | solution.py:102
  59.7 2.6 fusion.37
  64.3 2.9 %fusion.17 = f32[512,512]{0,1:T(8,128)S(1)} fusion(bf16[512,2048]{1,0:T(8,128)(2,1)S(1)} %copy-done.1, bf16[4096,512]{1,0:T(8,128)(2,1)} %param.12), kind=kOutput, calls=%fused_computation.18 | convolution fusion | flops 1073741824 | bytes 5242880 | tf_op jit(solution)/shard_map/dot_general | solution.py:19
  67.6 14.6 %fusion.3 = f32[512,4096]{1,0:T(8,128)} fusion(bf16[512,2048]{1,0:T(8,128)(2,1)S(1)} %copy-done.1, bf16[4096,4096]{1,0:T(8,128)(2,1)} %param.11), kind=kOutput, calls=%fused_computation.3 | convolution fusion | flops 8589934592 | bytes 27262976 | tf_op jit(solution)/shard_map/dot_general | solution.py:19
  82.2 23.7 %all-gather.5.cloned.1.call-done = bf16[512,2048]{1,0:T(8,128)(2,1)} async-done(((bf16[128,2048]{1,0:T(8,128)(2,1)}), bf16[512,2048]{1,0:T(8,128)(2,1)}) %all-gather.5.cloned.1.call-update) | async-done | bytes 2097168 | tf_op jit(solution)/shard_map/all_gather | solution.py:102
  105.9 3.4 %fusion.33 = f32[512,128]{0,1:T(8,128)} fusion(bf16[512,2048]{1,0:T(8,128)(2,1)} %all-gather.5.cloned.1.call-done, bf16[4096,128]{1,0:T(8,128)(2,1)} %param.13), kind=kOutput, calls=%fused_computation.37 | convolution fusion | flops 268435456 | bytes 2883584 | tf_op jit(solution)/shard_map/dot_general | solution.py:19
  109.3 2.6 %fusion.31 = f32[512,128]{0,1:T(8,128)} fusion(bf16[512,2048]{1,0:T(8,128)(2,1)S(1)} %copy-done, bf16[4096,128]{1,0:T(8,128)(2,1)} %param.14), kind=kOutput, calls=%fused_computation.35 | convolution fusion | flops 268435456 | bytes 2883584 | tf_op jit(solution)/shard_map/dot_general | solution.py:19
  111.9 3.9 %fusion.15 = f32[512,512]{0,1:T(8,128)} fusion(bf16[512,2048]{1,0:T(8,128)(2,1)S(1)} %copy-done, bf16[4096,512]{1,0:T(8,128)(2,1)} %param.12), kind=kOutput, calls=%fused_computation.16 | convolution fusion | flops 1073741824 | bytes 5242880 | tf_op jit(solution)/shard_map/dot_general | solution.py:19
  119.8 2.5 maximum_add_fusion
  123.1 16.8 %fusion.6 = f32[512,4096]{1,0:T(8,128)} fusion(f32[512,4096]{1,0:T(8,128)} %fusion.3, bf16[512,2048]{1,0:T(8,128)(2,1)S(1)} %copy-done, bf16[4096,4096]{1,0:T(8,128)(2,1)} %param.11), kind=kOutput, calls=%fused_computation.8 | convolution fusion | flops 8592031744 | bytes 35651584 | tf_op jit(solution)/shard_map/dot_general | solution.py:19
  140.9 2.2 all_gather.28
  143.2 3.8 %reduce-scatter.3.cloned.1.call-done = f32[128,576]{0,1:T(8,128)} async-done(((f32[512,576]{0,1:T(8,128)}), f32[128,576]{0,1:T(8,128)}) %reduce-scatter.3.cloned.1.call-update) | async-done | bytes 294928 | tf_op jit(solution)/shard_map/reduce_scatter | solution.py:125
  147.7 13.2 %all-gather = bf16[128,256]{0,1:T(8,128)(2,1)S(1)} all-gather(bf16[128,64]{0,1:T(8,128)(2,1)S(1)} %pad_maximum_fusion.4), channel_id=2, replica_groups=mesh['groups'=2,'tensor'=4,'seq'=2,'load'=2] {'tensor'}, dimensions={1}, use_global_device_ids=true | all-gather | bytes 81920 | tf_op jit(solution)/shard_map/all_gather | solution.py:137
  161.1 4.0 %fusion.66 = f32[128,4096]{1,0:T(8,128)S(1)} fusion(bf16[128,512]{0,1:T(8,128)(2,1)S(1)} %bitcast.78, bf16[512,4096]{1,0:T(8,128)(2,1)} %all-gather.9.cloned.1.call-done), kind=kOutput, calls=%fused_computation.123 | convolution fusion | flops 536870912 | bytes 6422528 | tf_op jit(solution)/shard_map/dot_general | solution.py:19
  167.5 15.9 %all_gather.29 = bf16[128,2048]{0,1:T(8,128)(2,1)S(1)} all-gather(bf16[128,512]{0,1:T(8,128)(2,1)S(1)} %select_convert_fusion), channel_id=1, replica_groups=mesh['groups'=2,'tensor'=4,'seq'=2,'load'=2] {'tensor'}, dimensions={1}, use_global_device_ids=true | all-gather | bytes 655360 | tf_op jit(solution)/shard_map/all_gather | solution.py:151
  183.8 10.8 %all_gather.30 = bf16[512,4,128]{2,0,1:T(8,128)(2,1)} all-gather(bf16[128,4,128]{2,0,1:T(8,128)(2,1)S(1)} %pad_maximum_fusion.3), channel_id=1, replica_groups=mesh['groups'=2,'tensor'=4,'seq'=2,'load'=2] {'seq','load'}, dimensions={0}, use_global_device_ids=true | all-gather | bytes 655360 | tf_op jit(solution)/shard_map/all_gather | solution.py:164
  194.6 29.5 %reduce-scatter.5.cloned.1.call-done = f32[128,4096]{1,0:T(8,128)} async-done(((f32[512,4096]{1,0:T(8,128)}), f32[128,4096]{1,0:T(8,128)}) %reduce-scatter.5.cloned.1.call-update) | async-done | bytes 2097168 | tf_op jit(solution)/shard_map/reduce_scatter | solution.py:126
  224.1 3.2 %add.141 = f32[128,4096]{1,0:T(8,128)} add(f32[128,4096]{1,0:T(8,128)} %reduce-scatter.5.cloned.1.call-done, f32[128,4096]{1,0:T(8,128)S(1)} %fusion.66) | non-fusion elementwise | flops 524288 | bytes 6291456 | tf_op jit(solution)/shard_map/add | solution.py:171
  229.2 2.5 fusion.61
  231.6 2.3 copy.74
  234.7 4.2 %fusion.26 = (bf16[128,2048,1]{1,0,2:T(8,128)(2,1)S(1)}, bf16[128,2048,1]{1,0,2:T(8,128)(2,1)S(1)}) fusion(f32[128,2048,1]{1,0,2:T(8,128)S(1)} %copy.74, f32[128,2048,1]{1,0,2:T(8,128)S(1)} %copy.73, f32[2048]{0:T(1024)S(1)} %fusion.55, f32[128]{0:T(128)S(1)} %subtract_convert_fusion), kind=kLoop, calls=%fused_computation.30 | loop fusion | flops 2359296 | bytes 3154432 | tf_op jit(solution)/shard_map/convert
  239.9 5.1 %fusion.65 = (f32[2,16,128]{2,1,0:T(8,128)S(1)}, bf16[2,16,128,512]{2,3,1,0:T(8,128)(2,1)}) fusion(pred[128,512]{0,1:T(8,128)(4,1)S(1)} %fusion.39, bf16[128,2,16,128]{0,3,2,1:T(8,128)(2,1)S(1)} %bitcast.75, bf16[512,4,128]{2,0,1:T(8,128)(2,1)S(1)} %copy-done.3), kind=kOutput, calls=%fused_computation.122 | convolution fusion | flops 549454336 | bytes 5652480 | tf_op jit(solution)/shard_map/sub | solution.py:181
  245.0 3.0 %fusion.14 = bf16[128,2,16,128]{0,3,2,1:T(8,128)(2,1)S(1)} fusion(bf16[2,16,128,512]{2,3,1,0:T(8,128)(2,1)} %get-tuple-element.44, f32[128,2,16]{0,2,1:T(8,128)S(1)} %bitcast.88, bf16[512,4,128]{2,0,1:T(8,128)(2,1)S(1)} %copy-done.3), kind=kOutput, calls=%fused_computation.15 | convolution fusion | flops 537919488 | bytes 5521408 | tf_op jit(solution)/shard_map/ghqk,kgd->ghqd/dot_general | solution.py:183
  (73 shorter events, 17.9 us)
Async XLA Ops:
  8.0 3.3 %copy-start.8 = (s32[4]{0:T(128)S(1)}, s32[4]{0:T(128)}, u32[]{:S(2)}) copy-start(s32[4]{0:T(128)} %param.18) | copy-start | bytes 52
  8.0 3.5 %copy-start.6 = (s32[4]{0:T(128)S(1)}, s32[4]{0:T(128)}, u32[]{:S(2)}) copy-start(s32[4]{0:T(128)} %param.19) | copy-start | bytes 52
  8.0 51.7 %copy-start.2 = (bf16[4096,128]{1,0:T(8,128)(2,1)S(1)}, bf16[4096,128]{1,0:T(8,128)(2,1)}, u32[]{:S(2)}) copy-start(bf16[4096,128]{1,0:T(8,128)(2,1)} %param.13) | copy-start | bytes 3145732
  8.0 51.6 %all-gather.7.cloned.1.call-start = ((), (), s32[]{:S(2)}) async-start(), calls=%async_computation.3 | async-start | bytes 2621440 | tf_op jit(solution)/shard_map/all_gather | solution.py:102
  10.5 95.4 %all-gather.5.cloned.1.call-start = ((), (), s32[]{:S(2)}) async-start(), calls=%async_computation.2 | async-start | bytes 2621440 | tf_op jit(solution)/shard_map/all_gather | solution.py:102
  11.2 135.7 %reduce-scatter.3.cloned.1.call-start = ((), (), s32[]{:S(2)}) async-start(), calls=%async_computation.4 | async-start | bytes 1474560 | tf_op jit(solution)/shard_map/reduce_scatter | solution.py:125
  59.7 2.7 %copy-start.1 = (bf16[512,2048]{1,0:T(8,128)(2,1)S(1)}, bf16[512,2048]{1,0:T(8,128)(2,1)}, u32[]{:S(2)}) copy-start(bf16[512,2048]{1,0:T(8,128)(2,1)} %all-gather.7.cloned.1.call-done) | copy-start | bytes 6291460
  105.9 3.4 %copy-start = (bf16[512,2048]{1,0:T(8,128)(2,1)S(1)}, bf16[512,2048]{1,0:T(8,128)(2,1)}, u32[]{:S(2)}) copy-start(bf16[512,2048]{1,0:T(8,128)(2,1)} %all-gather.5.cloned.1.call-done) | copy-start | bytes 6291460
  122.3 38.8 %all-gather.9.cloned.1.call-start = ((), (), s32[]{:S(2)}) async-start(), calls=%async_computation.6 | async-start | bytes 6291456 | tf_op jit(solution)/shard_map/all_gather | solution.py:93
  122.9 101.2 %reduce-scatter.5.cloned.1.call-start = ((), (), s32[]{:S(2)}) async-start(), calls=%async_computation.5 | async-start | bytes 10485760 | tf_op jit(solution)/shard_map/reduce_scatter | solution.py:126
  139.9 0.7 copy-start.7
  139.9 1.0 copy-start.5
  161.1 4.0 %copy-start.4 = (f32[128,576]{0,1:T(8,128)S(1)}, f32[128,576]{0,1:T(8,128)}, u32[]{:S(2)}) copy-start(f32[128,576]{0,1:T(8,128)} %reduce-scatter.3.cloned.1.call-done) | copy-start | bytes 884740
  238.9 1.0 copy-start.3
Sparse Core Ops, SparseCore 0:
  11.0 48.6 all-gather.6
  61.2 44.6 all-gather.4
  122.4 24.4 reduce-scatter.2
  149.5 74.5 reduce-scatter.4
Sparse Core Ops, SparseCore 1:
  124.3 12.2 all-gather.8

commit v5 on v2

--- a/solution.py
+++ b/solution.py
@@ -92,22 +92,40 @@
     block_rows = tokens.shape[0] * tensor_count // block_count
     up_query_all = lax.all_gather(up_query, "load", axis=0, tiled=True)
     up_keyval_all = lax.all_gather(up_keyval, "load", axis=0, tiled=True)
-    shard_rows = lax.all_gather(tokens, "tensor", axis=0, tiled=True)
-    piece_ids = jnp.arange(shard_rows.shape[0], dtype=jnp.int32)
-    piece_rank, piece_first, piece_hot = tenant_table(
-        piece_ids, adapter_rank, token_lengths, adapter_slot
-    )
-    small_terms = jnp.concatenate(
-        [
-            product(shard_rows, weight_keyval),
-            select_slot(product(shard_rows, down_query), piece_hot),
-            select_slot(product(shard_rows, down_keyval), piece_hot),
-        ],
-        axis=1,
-    )
-    small_summed = lax.psum_scatter(small_terms, ("seq", "load"), scatter_dimension=0, tiled=True)
+    ring = tensor_count
+    chunk = tokens.shape[0]
+    small_cols = keyval_cols + 2 * rank_share
+    small_terms = jnp.zeros((ring, chunk, small_cols), jnp.float32)
+    query_terms = jnp.zeros((ring, chunk, query_cols), jnp.float32)
+    shift = [(i, (i + 1) % ring) for i in range(ring)]
+    held = tokens
+    for step in range(ring):
+        following = lax.ppermute(held, "tensor", shift) if step < ring - 1 else None
+        owner = (tensor_index - step) % ring
+        block_ids = owner * chunk + jnp.arange(chunk, dtype=jnp.int32)
+        _, _, block_hot = tenant_table(block_ids, adapter_rank, token_lengths, adapter_slot)
+        small_block = jnp.concatenate(
+            [
+                product(held, weight_keyval),
+                select_slot(product(held, down_query), block_hot),
+                select_slot(product(held, down_keyval), block_hot),
+            ],
+            axis=1,
+        )
+        small_terms = lax.dynamic_update_slice_in_dim(small_terms, small_block[None], owner, 0)
+        query_terms = lax.dynamic_update_slice_in_dim(
+            query_terms, product(held, weight_query)[None], owner, 0
+        )
+        if following is not None:
+            following, small_terms, query_terms = lax.optimization_barrier(
+                (following, small_terms, query_terms)
+            )
+        held = following
+    small_summed = lax.psum_scatter(
+        small_terms.reshape(ring * chunk, -1), ("seq", "load"), scatter_dimension=0, tiled=True
+    )
     query_summed = lax.psum_scatter(
-        product(shard_rows, weight_query), ("seq", "load"), scatter_dimension=0, tiled=True
+        query_terms.reshape(ring * chunk, -1), ("seq", "load"), scatter_dimension=0, tiled=True
     )
     token_ids = block_index * block_rows + jnp.arange(block_rows, dtype=jnp.int32)
     own_rank, own_first, slot_hot = tenant_table(
@@ -151,7 +169,7 @@
     )
     piece_keys = both_heads[:, :kv_here]
     piece_values = both_heads[:, kv_here:]
-    delta_query = product(wide_query, up_query_all)
+    delta_query = lax.optimization_barrier(product(wide_query, up_query_all))
     query_rows = rotate_pairs(
         query_summed + delta_query, position, tensor_index * query_cols
     ).astype(jnp.bfloat16)

time: 247 us -> 235 us (0.951)
  waiting for transfers between devices: 114 us -> 43.3 us
  matrix products: 51.8 us -> 93.8 us
  other arithmetic: 10 us -> 15.5 us
  local copies, waits for them, and re-layouts: 13.8 us -> 19.2 us
  starting transfers between devices: 0.16 us -> 4.72 us
    all_gather x1 -> x0, waiting for transfers between devices: 82.8 us -> none  [shards(): shard_rows = lax.all_gather(tokens, 'tensor', axis=0, tiled=True)]
    dot_general x6 -> x18, matrix products: 43.6 us -> 85.6 us  [product(): return jnp.dot(left, right, preferred_element_type=jnp.float32)]
    ppermute x0 -> x3, waiting for transfers between devices: none -> 8.03 us  [shards(): following = lax.ppermute(held, 'tensor', shift) if step < ring - 1 else None]
    reduce_scatter x2, waiting for transfers between devices: 30.1 us -> 34.7 us  [the longest x1 29.1 us: shards(): lax.psum_scatter(query_terms.reshape(ring * chunk, -1), ('seq', 'load'),...]
    ppermute x0 -> x3, starting transfers between devices: none -> 4.6 us  [shards(): following = lax.ppermute(held, 'tensor', shift) if step < ring - 1 else None]
    broadcast_in_dim x0 -> x2, local copies, waits for them, and re-layouts: none -> 4.34 us  [the longest x1 4.25 us: shards(): query_terms = jnp.zeros((ring, chunk, query_cols), jnp.float32)]
    add x0 -> x5, other arithmetic: none -> 3.18 us  [the longest x1 3.16 us: shards(): query_summed + delta_query]
    unnamed x20 -> x43, local copies, waits for them, and re-layouts: 7.72 us -> 7.61 us
  transfers between devices with their start and end apart: 4 -> 6, of which waited for: 2 -> 4; matrix products, arithmetic and copies ran while one was open for 13% -> 42% of each run, Pallas kernels for 0% -> 0%
where the time goes in v5:
time: 235 us
  matrix products  93.8 us (40%)
  waiting for transfers between devices  43.3 us (18%)
  blocking collectives  42.3 us (18%)
  local copies, waits for them, and re-layouts  19.2 us (8%)
  between operations  16.1 us (7%)
  other arithmetic  15.5 us (7%)
  starting transfers between devices  4.72 us (2%)
    dot_general x18, matrix products, product(): return jnp.dot(left, right, preferred_element_type=jnp.float32)  85.6 us
    reduce_scatter x1, waiting for transfers between devices, shards(): lax.psum_scatter(query_terms.reshape(ring * chunk, -1), ('seq', 'load'),...  29.1 us
    all_gather x1, blocking collectives, shards(): kv_all = lax.all_gather(kv_local, 'tensor', axis=1, tiled=True)  16 us
    all_gather x1, blocking collectives, shards(): lax.all_gather(jnp.concatenate([low_query, low_keyval], axis=1), 'tensor'...  13.5 us
    all_gather x1, blocking collectives, shards(): lax.all_gather(jnp.concatenate([key_heads, value_heads], axis=1), ('seq',...  10.7 us
    ppermute x3, waiting for transfers between devices, shards(): following = lax.ppermute(held, 'tensor', shift) if step < ring - 1 else None  8.03 us
    unnamed x43, local copies, waits for them, and re-layouts  7.61 us
    reduce_scatter x1, waiting for transfers between devices, shards(): lax.psum_scatter(small_terms.reshape(ring * chunk, -1), ('seq', 'load'),...  5.61 us
  transfers between devices with their start and end apart: 6, of which 4 were waited for; matrix products, arithmetic and copies ran while one was open for 42% of the time, Pallas kernels for 0%

profile of v5, /device:TPU:0, one launch (start us, length us, event | category | flops | bytes accessed | tf_op | source)
XLA Modules:
  0.0 234.8 jit_solution(11444994646367894960)
XLA Ops:
  8.1 3.1 %collective-permute-start = (bf16[128,4096]{1,0:T(8,128)(2,1)}, bf16[128,4096]{1,0:T(8,128)(2,1)S(1)}, u32[]{:S(2)}, u32[]{:S(2)}) collective-permute-start(bf16[128,4096]{1,0:T(8,128)(2,1)} %param.10), channel_id=1, source_target_pairs={{0,4},{4,8},{8,12},{12,0},{1,5},{5,9},{9,13},{13,1},{2,6},{6,10},{... | collective-permute-start | bytes 3145736 | tf_op jit(solution)/shard_map/ppermute | solution.py:103
  17.8 4.3 %broadcast_in_dim.244 = f32[4,128,4096]{2,1,0:T(8,128)} broadcast(f32[]{:T(128)} %constant.130.clone.1), dimensions={} | broadcast | bytes 8388612 | tf_op jit(solution)/shard_map/broadcast_in_dim | solution.py:99
  22.1 14.3 %fusion.5 = f32[4,128,4096]{2,1,0:T(8,128)} fusion(f32[4,128,4096]{2,1,0:T(8,128)} %broadcast_in_dim.244, s32[]{:T(128)S(6)} %select_n.168, bf16[128,4096]{1,0:T(8,128)(2,1)S(1)} %copy-done.3, bf16[4096,4096]{1,0:T(8,128)(2,1)} %param.11), kind=kOutput, calls=%fused_computation.11 | convolution fusion | flops 4294967296 | bytes 36700164 | tf_op jit(solution)/shard_map/dot_general | solution.py:19
  36.6 2.9 %fusion.53 = f32[128,512]{1,0:T(8,128)S(1)} fusion(bf16[128,4096]{1,0:T(8,128)(2,1)S(1)} %copy-done.3, bf16[4096,512]{1,0:T(8,128)(2,1)} %param.12), kind=kOutput, calls=%fused_computation.130 | convolution fusion | flops 536870912 | bytes 5505024 | tf_op jit(solution)/shard_map/dot_general | solution.py:19
  42.4 14.3 %fusion.4 = f32[4,128,4096]{2,1,0:T(8,128)} fusion(f32[4,128,4096]{2,1,0:T(8,128)} %fusion.5, s32[]{:T(128)S(6)} %select_n.173, bf16[128,4096]{1,0:T(8,128)(2,1)S(1)} %collective-permute-done, bf16[4096,4096]{1,0:T(8,128)(2,1)} %param.11), kind=kOutput, calls=%fused_computation.9 | convolution fusion | flops 4294967296 | bytes 36700164 | tf_op jit(solution)/shard_map/dot_general | solution.py:19
  58.1 2.9 %fusion.56 = f32[128,512]{1,0:T(8,128)S(1)} fusion(bf16[128,4096]{1,0:T(8,128)(2,1)S(1)} %collective-permute-done, bf16[4096,512]{1,0:T(8,128)(2,1)} %param.12), kind=kOutput, calls=%fused_computation.133 | convolution fusion | flops 536870912 | bytes 5505024 | tf_op jit(solution)/shard_map/dot_general | solution.py:19
  61.1 6.4 %collective-permute-done.1 = bf16[128,4096]{1,0:T(8,128)(2,1)} collective-permute-done((bf16[128,4096]{1,0:T(8,128)(2,1)S(1)}, bf16[128,4096]{1,0:T(8,128)(2,1)}, u32[]{:S(2)}, u32[]{:S(2)}) %collective-permute-start.1) | collective-permute-done | bytes 1048608 | tf_op jit(solution)/shard_map/ppermute | solution.py:103
  67.5 16.7 %fusion.3 = f32[4,128,4096]{2,1,0:T(8,128)} fusion(f32[4,128,4096]{2,1,0:T(8,128)} %fusion.4, s32[]{:T(128)S(6)} %select_n.178, bf16[128,4096]{1,0:T(8,128)(2,1)} %collective-permute-done.1, bf16[4096,4096]{1,0:T(8,128)(2,1)} %param.11), kind=kOutput, calls=%fused_computation.7 | convolution fusion | flops 4294967296 | bytes 36700164 | tf_op jit(solution)/shard_map/dot_general | solution.py:19
  88.0 3.4 %fusion.59 = f32[128,512]{1,0:T(8,128)S(1)} fusion(bf16[128,4096]{1,0:T(8,128)(2,1)} %collective-permute-done.1, bf16[4096,512]{1,0:T(8,128)(2,1)} %param.12), kind=kOutput, calls=%fused_computation.136 | convolution fusion | flops 536870912 | bytes 5505024 | tf_op jit(solution)/shard_map/dot_general | solution.py:19
  97.2 17.0 %fusion.2 = f32[4,128,4096]{2,1,0:T(8,128)} fusion(f32[4,128,4096]{2,1,0:T(8,128)} %fusion.3, s32[]{:T(128)S(6)} %select_n.183, bf16[128,4096]{1,0:T(8,128)(2,1)S(1)} %collective-permute-done.2, bf16[4096,4096]{1,0:T(8,128)(2,1)} %param.11), kind=kOutput, calls=%fused_computation.5 | convolution fusion | flops 4294967296 | bytes 36700164 | tf_op jit(solution)/shard_map/dot_general | solution.py:19
  115.1 2.2 all_gather.20
  117.4 5.6 %reduce-scatter.3.cloned.1.call-done = f32[128,576]{1,0:T(8,128)} async-done(((f32[512,576]{1,0:T(8,128)}), f32[128,576]{1,0:T(8,128)}) %reduce-scatter.3.cloned.1.call-update) | async-done | bytes 294928 | tf_op jit(solution)/shard_map/reduce_scatter | solution.py:124
  124.3 13.5 %all-gather = bf16[128,256]{0,1:T(8,128)(2,1)S(1)} all-gather(bf16[128,64]{0,1:T(8,128)(2,1)S(1)} %copy.75), channel_id=2, replica_groups=mesh['groups'=2,'tensor'=4,'seq'=2,'load'=2] {'tensor'}, dimensions={1}, use_global_device_ids=true | all-gather | bytes 81920 | tf_op jit(solution)/shard_map/all_gather | solution.py:140
  138.0 3.8 %fusion.65 = f32[128,4096]{1,0:T(8,128)S(1)} fusion(bf16[128,512]{0,1:T(8,128)(2,1)S(1)} %bitcast.137, bf16[512,4096]{1,0:T(8,128)(2,1)} %all-gather.3.cloned.1.call-done), kind=kOutput, calls=%fused_computation.142 | convolution fusion | flops 536870912 | bytes 6422528 | tf_op jit(solution)/shard_map/dot_general | solution.py:19
  144.0 16.0 %all_gather.21 = bf16[128,2048]{1,0:T(8,128)(2,1)S(1)} all-gather(bf16[128,512]{1,0:T(8,128)(2,1)S(1)} %select_convert_fusion), channel_id=1, replica_groups=mesh['groups'=2,'tensor'=4,'seq'=2,'load'=2] {'tensor'}, dimensions={1}, use_global_device_ids=true | all-gather | bytes 655360 | tf_op jit(solution)/shard_map/all_gather | solution.py:154
  160.6 10.7 %all_gather.22 = bf16[512,4,128]{2,0,1:T(8,128)(2,1)} all-gather(bf16[128,4,128]{2,0,1:T(8,128)(2,1)S(1)} %pad_maximum_fusion.2), channel_id=1, replica_groups=mesh['groups'=2,'tensor'=4,'seq'=2,'load'=2] {'seq','load'}, dimensions={0}, use_global_device_ids=true | all-gather | bytes 655360 | tf_op jit(solution)/shard_map/all_gather | solution.py:167
  171.2 29.1 %reduce-scatter.5.cloned.1.call-done = f32[128,4096]{1,0:T(8,128)} async-done(((f32[512,4096]{1,0:T(8,128)}), f32[128,4096]{1,0:T(8,128)}) %reduce-scatter.5.cloned.1.call-update) | async-done | bytes 2097168 | tf_op jit(solution)/shard_map/reduce_scatter | solution.py:127
  200.3 3.2 %add.221 = f32[128,4096]{1,0:T(8,128)} add(f32[128,4096]{1,0:T(8,128)} %reduce-scatter.5.cloned.1.call-done, f32[128,4096]{1,0:T(8,128)S(1)} %fusion.65) | non-fusion elementwise | flops 524288 | bytes 6291456 | tf_op jit(solution)/shard_map/add | solution.py:174
  205.4 2.6 %fusion.49 = (f32[128,2048,1]{0,2,1:T(1,128)}, f32[128,2048,1]{0,2,1:T(1,128)}) fusion(f32[128,2048,2]{0,2,1:T(2,128)S(1)} %bitcast.131), kind=kLoop, calls=%fused_computation.126 | loop fusion | bytes 4194304 | tf_op jit(solution)/shard_map/slice | solution.py:30
  208.0 2.3 copy.102
  210.4 2.3 copy.101
  212.8 4.2 %fusion.19 = (bf16[128,2048,1]{1,0,2:T(8,128)(2,1)S(1)}, bf16[128,2048,1]{1,0,2:T(8,128)(2,1)S(1)}) fusion(f32[128,2048,1]{1,0,2:T(8,128)S(1)} %copy.102, f32[128,2048,1]{1,0,2:T(8,128)S(1)} %copy.101, f32[2048]{0:T(1024)S(1)} %fusion.44, f32[128]{0:T(128)S(1)} %subtract_convert_fusion), kind=kLoop, calls=%fused_computation.27 | loop fusion | flops 2359296 | bytes 3154432 | tf_op jit(solution)/shard_map/convert
  217.9 5.1 %fusion.52 = (f32[2,16,128]{2,1,0:T(8,128)S(1)}, bf16[2,16,128,512]{2,3,1,0:T(8,128)(2,1)}) fusion(pred[128,512]{0,1:T(8,128)(4,1)S(1)} %fusion.28, bf16[128,2,16,128]{0,3,2,1:T(8,128)(2,1)S(1)} %bitcast.133, bf16[512,4,128]{2,0,1:T(8,128)(2,1)S(1)} %copy-done.9), kind=kOutput, calls=%fused_computation.129 | convolution fusion | flops 549454336 | bytes 5652480 | tf_op jit(solution)/shard_map/sub | solution.py:184
  223.0 3.0 %fusion.11 = bf16[128,2,16,128]{0,3,2,1:T(8,128)(2,1)S(1)} fusion(bf16[2,16,128,512]{2,3,1,0:T(8,128)(2,1)} %get-tuple-element.66, f32[128,2,16]{0,2,1:T(8,128)S(1)} %bitcast.154, bf16[512,4,128]{2,0,1:T(8,128)(2,1)S(1)} %copy-done.9), kind=kOutput, calls=%fused_computation.18 | convolution fusion | flops 537919488 | bytes 5521408 | tf_op jit(solution)/shard_map/ghqk,kgd->ghqd/dot_general | solution.py:186
  (118 shorter events, 30.0 us)
Async XLA Ops:
  8.0 4.7 %copy-start = (bf16[4096,128]{1,0:T(8,128)(2,1)S(1)}, bf16[4096,128]{1,0:T(8,128)(2,1)}, u32[]{:S(2)}) copy-start(bf16[4096,128]{1,0:T(8,128)(2,1)} %param.13) | copy-start | bytes 3145732
  8.0 115.0 %reduce-scatter.3.cloned.1.call-start = ((), (), s32[]{:S(2)}) async-start(), calls=%async_computation.2 | async-start | bytes 1638400 | tf_op jit(solution)/shard_map/reduce_scatter | solution.py:124
  8.1 32.9 %collective-permute-start = (bf16[128,4096]{1,0:T(8,128)(2,1)}, bf16[128,4096]{1,0:T(8,128)(2,1)S(1)}, u32[]{:S(2)}, u32[]{:S(2)}) collective-permute-start(bf16[128,4096]{1,0:T(8,128)(2,1)} %param.10), channel_id=1, source_target_pairs={{0,4},{4,8},{8,12},{12,0},{1,5},{5,9},{9,13},{13,1},{2,6},{6,10},{... | collective-permute-start | bytes 3145736 | tf_op jit(solution)/shard_map/ppermute | solution.py:103
  11.1 6.6 %copy-start.12 = (s32[128]{0:T(128)}, s32[128]{0:T(128)S(1)}, u32[]{:S(2)}) copy-start(s32[128]{0:T(128)S(1)} %iota_add_fusion.5) | copy-start | bytes 1540
  17.8 4.3 %copy-start.3 = (bf16[128,4096]{1,0:T(8,128)(2,1)S(1)}, bf16[128,4096]{1,0:T(8,128)(2,1)}, u32[]{:S(2)}) copy-start(bf16[128,4096]{1,0:T(8,128)(2,1)} %param.10) | copy-start | bytes 3145732
  40.9 16.3 %copy-start.4 = (bf16[4096,128]{1,0:T(8,128)(2,1)S(1)}, bf16[4096,128]{1,0:T(8,128)(2,1)}, u32[]{:S(2)}) copy-start(bf16[4096,128]{1,0:T(8,128)(2,1)} %param.14) | copy-start | bytes 3145732
  40.9 26.5 %collective-permute-start.1 = (bf16[128,4096]{1,0:T(8,128)(2,1)S(1)}, bf16[128,4096]{1,0:T(8,128)(2,1)}, u32[]{:S(2)}, u32[]{:S(2)}) collective-permute-start(bf16[128,4096]{1,0:T(8,128)(2,1)S(1)} %collective-permute-done), channel_id=1, source_target_pairs={{0,4},{4,8},{8,12},{12,0},{1,5},{5,9},{9,13},{13,1},{2,6},{6,10},{... | collective-permute-start | bytes 3145736 | tf_op jit(solution)/shard_map/ppermute | solution.py:103
  61.1 24.8 %copy-start.5 = (bf16[4096,128]{1,0:T(8,128)(2,1)S(1)}, bf16[4096,128]{1,0:T(8,128)(2,1)}, u32[]{:S(2)}) copy-start(bf16[4096,128]{1,0:T(8,128)(2,1)} %param.14) | copy-start | bytes 3145732
  67.5 25.7 %collective-permute-start.2 = (bf16[128,4096]{1,0:T(8,128)(2,1)}, bf16[128,4096]{1,0:T(8,128)(2,1)S(1)}, u32[]{:S(2)}, u32[]{:S(2)}) collective-permute-start(bf16[128,4096]{1,0:T(8,128)(2,1)} %collective-permute-done.1), channel_id=1, source_target_pairs={{0,4},{4,8},{8,12},{12,0},{1,5},{5,9},{9,13},{13,1},{2,6},{6,10},{... | collective-permute-start | bytes 3145736 | tf_op jit(solution)/shard_map/ppermute | solution.py:103
  84.2 3.5 %copy-start.18 = (pred[128,4]{0,1:T(4,128)(4,1)S(1)}, pred[128,4]{0,1:T(4,128)(4,1)}, u32[]{:S(2)}) copy-start(pred[128,4]{0,1:T(4,128)(4,1)} %get-tuple-element.69) | copy-start | bytes 1540
  88.0 5.7 %copy-start.6 = (bf16[4096,128]{1,0:T(8,128)(2,1)S(1)}, bf16[4096,128]{1,0:T(8,128)(2,1)}, u32[]{:S(2)}) copy-start(bf16[4096,128]{1,0:T(8,128)(2,1)} %param.14) | copy-start | bytes 3145732
  88.0 6.3 %copy-start.2 = (bf16[4096,512]{1,0:T(8,128)(2,1)S(1)}, bf16[4096,512]{1,0:T(8,128)(2,1)}, u32[]{:S(2)}) copy-start(bf16[4096,512]{1,0:T(8,128)(2,1)} %param.12) | copy-start | bytes 12582916
  93.7 1.3 copy-start.17
  95.5 1.1 copy-start.7
  96.6 41.4 %all-gather.3.cloned.1.call-start = ((), (), s32[]{:S(2)}) async-start(), calls=%async_computation.4 | async-start | bytes 6291456 | tf_op jit(solution)/shard_map/all_gather | solution.py:93
  97.1 103.2 %reduce-scatter.5.cloned.1.call-start = ((), (), s32[]{:S(2)}) async-start(), calls=%async_computation.3 | async-start | bytes 10485760 | tf_op jit(solution)/shard_map/reduce_scatter | solution.py:127
  114.2 3.1 %copy-start.14 = (s32[128]{0:T(128)S(1)}, s32[128]{0:T(128)}, u32[]{:S(2)}) copy-start(s32[128]{0:T(128)} %get-tuple-element.34) | copy-start | bytes 1540
  114.2 3.1 %copy-start.15 = (s32[128]{0:T(128)S(1)}, s32[128]{0:T(128)}, u32[]{:S(2)}) copy-start(s32[128]{0:T(128)} %get-tuple-element.40) | copy-start | bytes 1540
  114.2 3.1 %copy-start.13 = (s32[128]{0:T(128)S(1)}, s32[128]{0:T(128)}, u32[]{:S(2)}) copy-start(s32[128]{0:T(128)} %copy-done.12) | copy-start | bytes 1540
  114.2 23.6 %copy-start.16 = (pred[128,4]{0,1:T(4,128)(4,1)S(1)}, pred[128,4]{0,1:T(4,128)(4,1)}, u32[]{:S(2)}) copy-start(pred[128,4]{0,1:T(4,128)(4,1)} %get-tuple-element.67) | copy-start | bytes 1540
  123.0 18.7 %copy-start.10 = (f32[128,576]{1,0:T(8,128)S(1)}, f32[128,576]{1,0:T(8,128)}, u32[]{:S(2)}) copy-start(f32[128,576]{1,0:T(8,128)} %reduce-scatter.3.cloned.1.call-done) | copy-start | bytes 884740
  144.0 59.5 %copy-start.8 = (bf16[128,512]{1,0:T(8,128)(2,1)}, bf16[128,512]{1,0:T(8,128)(2,1)S(1)}, u32[]{:S(2)}) copy-start(bf16[128,512]{1,0:T(8,128)(2,1)S(1)} %select_convert_fusion) | copy-start | bytes 393220
  212.8 5.1 %copy-start.9 = (bf16[512,4,128]{2,0,1:T(8,128)(2,1)S(1)}, bf16[512,4,128]{2,0,1:T(8,128)(2,1)}, u32[]{:S(2)}) copy-start(bf16[512,4,128]{2,0,1:T(8,128)(2,1)} %all_gather.22) | copy-start | bytes 1572868
  223.0 4.4 %copy-start.1 = (bf16[4096,128]{1,0:T(8,128)(2,1)S(1)}, bf16[4096,128]{1,0:T(8,128)(2,1)}, u32[]{:S(2)}) copy-start(bf16[4096,128]{1,0:T(8,128)(2,1)} %param.13) | copy-start | bytes 3145732
  (1 other events, 0.9 us)
Sparse Core Ops, SparseCore 0:
  96.7 26.2 reduce-scatter.2
  125.8 74.5 reduce-scatter.4
Sparse Core Ops, SparseCore 1:
  98.6 13.3 all-gather.2

commit v6 on v5

--- a/solution.py
+++ b/solution.py
@@ -68,6 +68,22 @@
         slot_hot[:, None, :], low_values[:, :, None], jnp.zeros((), low_values.dtype)
     )
     return wide_rows.reshape(low_values.shape[0], -1)
+
+
+def ring_reduce_scatter(blocks, axis):
+    count = lax.axis_size(axis)
+    me = lax.axis_index(axis)
+    if count == 1:
+        return blocks[0]
+    shift = [(i, (i + 1) % count) for i in range(count)]
+
+    def pick(step):
+        return lax.dynamic_index_in_dim(blocks, (me - 1 - step) % count, 0, keepdims=False)
+
+    total = pick(0)
+    for step in range(1, count):
+        total = lax.ppermute(total, axis, shift) + pick(step)
+    return total
 
 
 def shards(
@@ -121,9 +137,11 @@
                 (following, small_terms, query_terms)
             )
         held = following
-    small_summed = lax.psum_scatter(
-        small_terms.reshape(ring * chunk, -1), ("seq", "load"), scatter_dimension=0, tiled=True
-    )
+    seq_count = lax.axis_size("seq")
+    load_count = lax.axis_size("load")
+    by_core = small_terms.reshape(seq_count, load_count, block_rows, -1)
+    per_core = ring_reduce_scatter(jnp.moveaxis(by_core, 1, 0), "load")
+    small_summed = ring_reduce_scatter(per_core, "seq")
     query_summed = lax.psum_scatter(
         query_terms.reshape(ring * chunk, -1), ("seq", "load"), scatter_dimension=0, tiled=True
     )

time: 235 us -> 223 us (0.949)
  waiting for transfers between devices: 43.3 us -> 18.9 us
  local copies, waits for them, and re-layouts: 19.2 us -> 28.6 us
    reduce_scatter x1, waiting for transfers between devices: 29.1 us -> 8.17 us  [shards(): lax.psum_scatter(query_terms.reshape(ring * chunk, -1), ('seq', 'load'),...]
    ppermute x0 -> x2, waiting for transfers between devices: none -> 7.57 us  [ring_reduce_scatter(): total = lax.ppermute(total, axis, shift) + pick(step)]
    reduce_scatter x1 -> x0, waiting for transfers between devices: 5.61 us -> none  [shards(): lax.psum_scatter(small_terms.reshape(ring * chunk, -1), ('seq', 'load'),...]
    ppermute x3, waiting for transfers between devices: 8.03 us -> 3.16 us  [shards(): following = lax.ppermute(held, 'tensor', shift) if step < ring - 1 else None]
    dynamic_update_slice x0 -> x4, local copies, waits for them, and re-layouts: none -> 3.46 us  [shards(): lax.dynamic_update_slice_in_dim(small_terms, small_block[None], owner, 0)]
    reduce_sum x8, local copies, waits for them, and re-layouts: 0.77 us -> 3.31 us  [select_slot(): return jnp.sum(jnp.where(slot_hot[:, None, :], shaped, 0.0), axis=2)]
    unnamed x43 -> x39, local copies, waits for them, and re-layouts: 7.61 us -> 7.25 us
  transfers between devices with their start and end apart: 6 -> 7, of which waited for: 4 -> 3; matrix products, arithmetic and copies ran while one was open for 42% -> 49% of each run, Pallas kernels for 0% -> 0%
where the time goes in v6:
time: 223 us; the launch traced here: 222 us
  matrix products  94.4 us (42%)
  blocking collectives  43.1 us (19%)
  local copies, waits for them, and re-layouts  28.6 us (13%)
  waiting for transfers between devices  18.9 us (8%)
  between operations  16.2 us (7%)
  other arithmetic  15 us (7%)
  starting transfers between devices  6.25 us (3%)
    dot_general x18, matrix products, product(): return jnp.dot(left, right, preferred_element_type=jnp.float32)  84.9 us
    all_gather x1, blocking collectives, shards(): kv_all = lax.all_gather(kv_local, 'tensor', axis=1, tiled=True)  16 us
    all_gather x1, blocking collectives, shards(): lax.all_gather(jnp.concatenate([low_query, low_keyval], axis=1), 'tensor'...  13.5 us
    all_gather x1, blocking collectives, shards(): lax.all_gather(jnp.concatenate([key_heads, value_heads], axis=1), ('seq',...  10.9 us
    reduce_scatter x1, waiting for transfers between devices, shards(): lax.psum_scatter(query_terms.reshape(ring * chunk, -1), ('seq', 'load'),...  8.17 us
    ppermute x2, waiting for transfers between devices, ring_reduce_scatter(): total = lax.ppermute(total, axis, shift) + pick(step)  7.57 us
    unnamed x39, local copies, waits for them, and re-layouts  7.25 us
    sub x1, matrix products, shards(): exp_scores = jnp.where(visible, jnp.exp(scores - row_top[..., None]), 0.0)  6.51 us
  transfers between devices with their start and end apart: 7, of which 3 were waited for; matrix products, arithmetic and copies ran while one was open for 49% of the time, Pallas kernels for 0%

profile of v6, /device:TPU:0, one launch (start us, length us, event | category | flops | bytes accessed | tf_op | source)
XLA Modules:
  0.0 222.5 jit_solution(13121186132665858357)
XLA Ops:
  8.1 3.1 %collective-permute-start = (bf16[128,4096]{1,0:T(8,128)(2,1)}, bf16[128,4096]{1,0:T(8,128)(2,1)S(1)}, u32[]{:S(2)}, u32[]{:S(2)}) collective-permute-start(bf16[128,4096]{1,0:T(8,128)(2,1)} %param.10), channel_id=1, source_target_pairs={{0,4},{4,8},{8,12},{12,0},{1,5},{5,9},{9,13},{13,1},{2,6},{6,10},{... | collective-permute-start | bytes 3145736 | tf_op jit(solution)/shard_map/ppermute | solution.py:119
  16.3 4.8 %broadcast_in_dim.244 = f32[4,128,4096]{2,1,0:T(8,128)} broadcast(f32[]{:T(128)} %constant.167.clone.1), dimensions={} | broadcast | bytes 8388612 | tf_op jit(solution)/shard_map/broadcast_in_dim | solution.py:115
  21.1 15.5 %fusion.5 = f32[4,128,4096]{2,1,0:T(8,128)} fusion(f32[4,128,4096]{2,1,0:T(8,128)} %broadcast_in_dim.244, s32[]{:T(128)S(6)} %select_n.198, bf16[128,4096]{1,0:T(8,128)(2,1)S(1)} %copy-done.1, bf16[4096,4096]{1,0:T(8,128)(2,1)} %param.11), kind=kOutput, calls=%fused_computation.11 | convolution fusion | flops 4294967296 | bytes 36700164 | tf_op jit(solution)/shard_map/dot_general | solution.py:19
  37.5 2.9 %fusion.49 = f32[128,512]{1,0:T(8,128)S(1)} fusion(bf16[128,4096]{1,0:T(8,128)(2,1)S(1)} %copy-done.1, bf16[4096,512]{1,0:T(8,128)(2,1)} %param.12), kind=kOutput, calls=%fused_computation.135 | convolution fusion | flops 536870912 | bytes 5505024 | tf_op jit(solution)/shard_map/dot_general | solution.py:19
  43.4 14.3 %fusion.4 = f32[4,128,4096]{2,1,0:T(8,128)} fusion(f32[4,128,4096]{2,1,0:T(8,128)} %fusion.5, s32[]{:T(128)S(6)} %select_n.203, bf16[128,4096]{1,0:T(8,128)(2,1)S(1)} %collective-permute-done, bf16[4096,4096]{1,0:T(8,128)(2,1)} %param.11), kind=kOutput, calls=%fused_computation.9 | convolution fusion | flops 4294967296 | bytes 36700164 | tf_op jit(solution)/shard_map/dot_general | solution.py:19
  59.6 2.9 %fusion.52 = f32[128,512]{1,0:T(8,128)S(1)} fusion(bf16[128,4096]{1,0:T(8,128)(2,1)S(1)} %collective-permute-done, bf16[4096,512]{1,0:T(8,128)(2,1)} %param.12), kind=kOutput, calls=%fused_computation.138 | convolution fusion | flops 536870912 | bytes 5505024 | tf_op jit(solution)/shard_map/dot_general | solution.py:19
  65.2 3.2 %collective-permute-done.1 = bf16[128,4096]{1,0:T(8,128)(2,1)} collective-permute-done((bf16[128,4096]{1,0:T(8,128)(2,1)S(1)}, bf16[128,4096]{1,0:T(8,128)(2,1)}, u32[]{:S(2)}, u32[]{:S(2)}) %collective-permute-start.1) | collective-permute-done | bytes 1048608 | tf_op jit(solution)/shard_map/ppermute | solution.py:119
  68.4 16.7 %fusion.3 = f32[4,128,4096]{2,1,0:T(8,128)} fusion(f32[4,128,4096]{2,1,0:T(8,128)} %fusion.4, s32[]{:T(128)S(6)} %select_n.208, bf16[128,4096]{1,0:T(8,128)(2,1)} %collective-permute-done.1, bf16[4096,4096]{1,0:T(8,128)(2,1)} %param.11), kind=kOutput, calls=%fused_computation.7 | convolution fusion | flops 4294967296 | bytes 36700164 | tf_op jit(solution)/shard_map/dot_general | solution.py:19
  89.5 3.3 %fusion.55 = f32[128,512]{1,0:T(8,128)S(1)} fusion(bf16[128,4096]{1,0:T(8,128)(2,1)} %collective-permute-done.1, bf16[4096,512]{1,0:T(8,128)(2,1)} %param.12), kind=kOutput, calls=%fused_computation.141 | convolution fusion | flops 536870912 | bytes 5505024 | tf_op jit(solution)/shard_map/dot_general | solution.py:19
  95.4 14.2 %fusion.2 = f32[4,128,4096]{2,1,0:T(8,128)} fusion(f32[4,128,4096]{2,1,0:T(8,128)} %fusion.3, s32[]{:T(128)S(6)} %select_n.213, bf16[128,4096]{1,0:T(8,128)(2,1)S(1)} %collective-permute-done.2, bf16[4096,4096]{1,0:T(8,128)(2,1)} %param.11), kind=kOutput, calls=%fused_computation.5 | convolution fusion | flops 4294967296 | bytes 36700164 | tf_op jit(solution)/shard_map/dot_general | solution.py:19
  113.5 3.0 %fusion.58 = f32[128,512]{1,0:T(8,128)S(1)} fusion(bf16[128,4096]{1,0:T(8,128)(2,1)S(1)} %collective-permute-done.2, bf16[4096,512]{1,0:T(8,128)(2,1)} %param.12), kind=kOutput, calls=%fused_computation.144 | convolution fusion | flops 536870912 | bytes 5505024 | tf_op jit(solution)/shard_map/dot_general | solution.py:19
  117.6 2.7 %all_gather.20 = bf16[512,512]{1,0:T(8,128)(2,1)S(1)} all-gather(bf16[256,512]{1,0:T(8,128)(2,1)S(1)} %copy-done.6), channel_id=1, replica_groups=mesh['groups'=2,'tensor'=4,'seq'=2,'load'=2] {'load'}, dimensions={0}, use_global_device_ids=true | all-gather | bytes 786432 | tf_op jit(solution)/shard_map/all_gather | solution.py:110
  124.9 7.6 %collective-permute-done.4 = f32[128,576]{1,0:T(8,128)S(1)} collective-permute-done((f32[128,576]{1,0:T(8,128)S(1)}, f32[128,576]{1,0:T(8,128)S(1)}, u32[]{:S(2)}, u32[]{:S(2)}) %collective-permute-start.4) | collective-permute-done | bytes 294944 | tf_op jit(solution)/shard_map/ppermute | solution.py:85
  132.8 13.5 %all-gather = bf16[128,256]{0,1:T(8,128)(2,1)S(1)} all-gather(bf16[128,64]{0,1:T(8,128)(2,1)S(1)} %copy.115), channel_id=2, replica_groups=mesh['groups'=2,'tensor'=4,'seq'=2,'load'=2] {'tensor'}, dimensions={1}, use_global_device_ids=true | all-gather | bytes 81920 | tf_op jit(solution)/shard_map/all_gather | solution.py:158
  148.1 16.0 %all_gather.21 = bf16[128,2048]{1,0:T(8,128)(2,1)S(1)} all-gather(bf16[128,512]{1,0:T(8,128)(2,1)S(1)} %select_convert_fusion), channel_id=1, replica_groups=mesh['groups'=2,'tensor'=4,'seq'=2,'load'=2] {'tensor'}, dimensions={1}, use_global_device_ids=true | all-gather | bytes 655360 | tf_op jit(solution)/shard_map/all_gather | solution.py:172
  164.6 10.9 %all_gather.22 = bf16[512,4,128]{2,0,1:T(8,128)(2,1)} all-gather(bf16[128,4,128]{2,0,1:T(8,128)(2,1)S(1)} %pad_maximum_fusion.2), channel_id=1, replica_groups=mesh['groups'=2,'tensor'=4,'seq'=2,'load'=2] {'seq','load'}, dimensions={0}, use_global_device_ids=true | all-gather | bytes 655360 | tf_op jit(solution)/shard_map/all_gather | solution.py:185
  175.5 2.9 %fusion.61 = f32[128,4096]{1,0:T(8,128)S(1)} fusion(bf16[128,512]{0,1:T(8,128)(2,1)S(1)} %bitcast.136, bf16[512,4096]{1,0:T(8,128)(2,1)} %all-gather.3.cloned.1.call-done), kind=kOutput, calls=%fused_computation.147 | convolution fusion | flops 536870912 | bytes 6422528 | tf_op jit(solution)/shard_map/dot_general | solution.py:19
  178.5 8.2 %reduce-scatter.2.cloned.1.call-done = f32[128,4096]{1,0:T(8,128)} async-done(((f32[512,4096]{1,0:T(8,128)}), f32[128,4096]{1,0:T(8,128)}) %reduce-scatter.2.cloned.1.call-update) | async-done | bytes 2097168 | tf_op jit(solution)/shard_map/reduce_scatter | solution.py:145
  186.7 3.2 %add.269 = f32[128,4096]{1,0:T(8,128)} add(f32[128,4096]{1,0:T(8,128)} %reduce-scatter.2.cloned.1.call-done, f32[128,4096]{1,0:T(8,128)S(1)} %fusion.61) | non-fusion elementwise | flops 524288 | bytes 6291456 | tf_op jit(solution)/shard_map/add | solution.py:192
  191.7 2.6 %fusion.45 = (f32[128,2048,1]{0,2,1:T(1,128)}, f32[128,2048,1]{0,2,1:T(1,128)}) fusion(f32[128,2048,2]{0,2,1:T(2,128)S(1)} %bitcast.130), kind=kLoop, calls=%fused_computation.131 | loop fusion | bytes 4194304 | tf_op jit(solution)/shard_map/slice | solution.py:30
  196.7 2.3 %copy.141 = f32[128,2048,1]{1,0,2:T(8,128)S(1)} copy(f32[128,2048,1]{0,2,1:T(1,128)} %get-tuple-element.54) | data formatting | bytes 2097152
  199.1 4.2 %fusion.19 = (bf16[128,2048,1]{1,0,2:T(8,128)(2,1)S(1)}, bf16[128,2048,1]{1,0,2:T(8,128)(2,1)S(1)}) fusion(f32[128,2048,1]{1,0,2:T(8,128)S(1)} %copy.142, f32[128,2048,1]{1,0,2:T(8,128)S(1)} %copy.141, f32[2048]{0:T(1024)S(1)} %fusion.40, f32[128]{0:T(128)S(1)} %subtract_convert_fusion), kind=kLoop, calls=%fused_computation.26 | loop fusion | flops 2359296 | bytes 3154432 | tf_op jit(solution)/shard_map/convert
  204.2 6.5 %fusion.48 = (f32[2,16,128]{2,1,0:T(8,128)S(1)}, bf16[2,16,128,512]{2,3,1,0:T(8,128)(2,1)}) fusion(pred[128,512]{0,1:T(8,128)(4,1)S(1)} %fusion.24, bf16[128,2,16,128]{0,3,2,1:T(8,128)(2,1)S(1)} %bitcast.133, bf16[512,4,128]{2,0,1:T(8,128)(2,1)} %all_gather.22), kind=kOutput, calls=%fused_computation.134 | convolution fusion | flops 549454336 | bytes 5652480 | tf_op jit(solution)/shard_map/sub | solution.py:202
  210.7 3.0 %fusion.11 = bf16[128,2,16,128]{0,3,2,1:T(8,128)(2,1)S(1)} fusion(bf16[2,16,128,512]{2,3,1,0:T(8,128)(2,1)} %get-tuple-element.70, f32[128,2,16]{0,2,1:T(8,128)S(1)} %bitcast.155, bf16[512,4,128]{2,0,1:T(8,128)(2,1)} %all_gather.22), kind=kOutput, calls=%fused_computation.18 | convolution fusion | flops 537919488 | bytes 5521408 | tf_op jit(solution)/shard_map/ghqk,kgd->ghqd/dot_general | solution.py:204
  (129 shorter events, 39.0 us)
Async XLA Ops:
  8.0 4.8 %copy-start = (bf16[4096,128]{1,0:T(8,128)(2,1)S(1)}, bf16[4096,128]{1,0:T(8,128)(2,1)}, u32[]{:S(2)}) copy-start(bf16[4096,128]{1,0:T(8,128)(2,1)} %param.13) | copy-start | bytes 3145732
  8.0 6.6 %copy-start.1 = (bf16[128,4096]{1,0:T(8,128)(2,1)S(1)}, bf16[128,4096]{1,0:T(8,128)(2,1)}, u32[]{:S(2)}) copy-start(bf16[128,4096]{1,0:T(8,128)(2,1)} %param.10) | copy-start | bytes 3145732
  8.0 167.5 %all-gather.3.cloned.1.call-start = ((), (), s32[]{:S(2)}) async-start(), calls=%async_computation.2 | async-start | bytes 6291456 | tf_op jit(solution)/shard_map/all_gather | solution.py:109
  8.1 32.8 %collective-permute-start = (bf16[128,4096]{1,0:T(8,128)(2,1)}, bf16[128,4096]{1,0:T(8,128)(2,1)S(1)}, u32[]{:S(2)}, u32[]{:S(2)}) collective-permute-start(bf16[128,4096]{1,0:T(8,128)(2,1)} %param.10), channel_id=1, source_target_pairs={{0,4},{4,8},{8,12},{12,0},{1,5},{5,9},{9,13},{13,1},{2,6},{6,10},{... | collective-permute-start | bytes 3145736 | tf_op jit(solution)/shard_map/ppermute | solution.py:119
  11.2 175.5 %reduce-scatter.2.cloned.1.call-start = ((), (), s32[]{:S(2)}) async-start(), calls=%async_computation.1 | async-start | bytes 10485760 | tf_op jit(solution)/shard_map/reduce_scatter | solution.py:145
  21.1 15.5 %copy-start.15 = (s32[4]{0:T(128)S(1)}, s32[4]{0:T(128)}, u32[]{:S(2)}) copy-start(s32[4]{0:T(128)} %param.17) | copy-start | bytes 52
  21.1 15.5 %copy-start.16 = (s32[4]{0:T(128)S(1)}, s32[4]{0:T(128)}, u32[]{:S(2)}) copy-start(s32[4]{0:T(128)} %param.19) | copy-start | bytes 52
  40.8 1.0 copy-start.3
  40.8 17.3 %copy-start.2 = (bf16[4096,128]{1,0:T(8,128)(2,1)S(1)}, bf16[4096,128]{1,0:T(8,128)(2,1)}, u32[]{:S(2)}) copy-start(bf16[4096,128]{1,0:T(8,128)(2,1)} %param.14) | copy-start | bytes 3145732
  41.8 26.5 %collective-permute-start.1 = (bf16[128,4096]{1,0:T(8,128)(2,1)S(1)}, bf16[128,4096]{1,0:T(8,128)(2,1)}, u32[]{:S(2)}, u32[]{:S(2)}) collective-permute-start(bf16[128,4096]{1,0:T(8,128)(2,1)S(1)} %collective-permute-done), channel_id=1, source_target_pairs={{0,4},{4,8},{8,12},{12,0},{1,5},{5,9},{9,13},{13,1},{2,6},{6,10},{... | collective-permute-start | bytes 3145736 | tf_op jit(solution)/shard_map/ppermute | solution.py:119
  59.6 2.9 %copy-start.9 = (f32[128,32]{1,0:T(8,128)S(1)}, f32[128,32]{1,0:T(8,128)}, u32[]{:S(2)}) copy-start(f32[128,32]{1,0:T(8,128)} %copy.104) | copy-start | bytes 49156
  68.4 27.1 %collective-permute-start.2 = (bf16[128,4096]{1,0:T(8,128)(2,1)}, bf16[128,4096]{1,0:T(8,128)(2,1)S(1)}, u32[]{:S(2)}, u32[]{:S(2)}) collective-permute-start(bf16[128,4096]{1,0:T(8,128)(2,1)} %collective-permute-done.1), channel_id=1, source_target_pairs={{0,4},{4,8},{8,12},{12,0},{1,5},{5,9},{9,13},{13,1},{2,6},{6,10},{... | collective-permute-start | bytes 3145736 | tf_op jit(solution)/shard_map/ppermute | solution.py:119
  89.5 3.3 %copy-start.10 = (f32[128,32]{1,0:T(8,128)S(1)}, f32[128,32]{1,0:T(8,128)}, u32[]{:S(2)}) copy-start(f32[128,32]{1,0:T(8,128)} %copy.107) | copy-start | bytes 49156
  109.7 0.6 copy-start.12
  109.7 0.7 copy-start.13
  111.9 4.8 %copy-start.4 = (f32[4,128,576]{1,2,0:T(8,128)S(1)}, f32[4,128,576]{1,2,0:T(8,128)}, u32[]{:S(2)}) copy-start(f32[4,128,576]{1,2,0:T(8,128)} %constant_dynamic-update-slice_fusion.1) | copy-start | bytes 3538948
  113.5 3.0 %copy-start.7 = (f32[128,32]{1,0:T(8,128)S(1)}, f32[128,32]{1,0:T(8,128)}, u32[]{:S(2)}) copy-start(f32[128,32]{1,0:T(8,128)} %copy.111) | copy-start | bytes 49156
  113.5 3.0 %copy-start.8 = (f32[128,32]{1,0:T(8,128)S(1)}, f32[128,32]{1,0:T(8,128)}, u32[]{:S(2)}) copy-start(f32[128,32]{1,0:T(8,128)} %copy.110) | copy-start | bytes 49156
  113.5 4.2 %copy-start.6 = (bf16[256,512]{1,0:T(8,128)(2,1)S(1)}, bf16[256,512]{1,0:T(8,128)(2,1)}, u32[]{:S(2)}) copy-start(bf16[256,512]{1,0:T(8,128)(2,1)} %param.16) | copy-start | bytes 786436
  116.7 29.5 %copy-start.11 = (pred[128,4]{0,1:T(4,128)(4,1)S(1)}, pred[128,4]{0,1:T(4,128)(4,1)}, u32[]{:S(2)}) copy-start(pred[128,4]{0,1:T(4,128)(4,1)} %get-tuple-element.71) | copy-start | bytes 1540
  117.6 3.4 %collective-permute-start.3 = (f32[2,128,576]{1,2,0:T(8,128)}, f32[2,128,576]{1,2,0:T(8,128)}, u32[]{:S(2)}, u32[]{:S(2)}) collective-permute-start(f32[2,128,576]{1,2,0:T(8,128)} %dynamic-slice_bitcast_fusion), channel_id=1, source_target_pairs={{0,1},{1,0},{2,3},{3,2},{4,5},{5,4},{6,7},{7,6},{8,9},{9,8},{10,11... | collective-permute-start | bytes 1769480 | tf_op jit(solution)/shard_map/ppermute | solution.py:85
  121.0 26.2 %copy-start.14 = (f32[256]{0:T(256)S(1)}, f32[256]{0:T(256)}, u32[]{:S(2)}) copy-start(f32[256]{0:T(256)} %multiply_exponential_fusion) | copy-start | bytes 3076
  122.4 10.0 %collective-permute-start.4 = (f32[128,576]{1,0:T(8,128)S(1)}, f32[128,576]{1,0:T(8,128)S(1)}, u32[]{:S(2)}, u32[]{:S(2)}) collective-permute-start(f32[128,576]{1,0:T(8,128)S(1)} %bitcast.139), channel_id=1, source_target_pairs={{0,2},{2,0},{1,3},{3,1},{4,6},{6,4},{5,7},{7,5},{8,10},{10,8},{9,1... | collective-permute-start | bytes 884744 | tf_op jit(solution)/shard_map/ppermute | solution.py:85
  148.1 30.4 %copy-start.5 = (bf16[128,512]{1,0:T(8,128)(2,1)}, bf16[128,512]{1,0:T(8,128)(2,1)S(1)}, u32[]{:S(2)}) copy-start(bf16[128,512]{1,0:T(8,128)(2,1)S(1)} %select_convert_fusion) | copy-start | bytes 393220
Sparse Core Ops, SparseCore 0:
  11.3 15.5 all-gather.2
Sparse Core Ops, SparseCore 1:
  109.8 76.8 reduce-scatter.1

commit v7 on v6

--- a/solution.py
+++ b/solution.py
@@ -20,21 +20,21 @@
 
 
 def rotate_pairs(values, position, first_col):
-    pair_count = values.shape[1] // 2
-    pair_col = first_col + 2 * jnp.arange(pair_count, dtype=jnp.int32)
+    cols = values.shape[1]
+    width = HEAD_DIM if cols % HEAD_DIM == 0 else cols
+    col = jnp.arange(width, dtype=jnp.int32)
+    pair_col = first_col + col - col % 2
     within = pair_col % HEAD_DIM // 2
     frequency = jnp.exp(-(2.0 * within.astype(jnp.float32) / HEAD_DIM) * math.log(ROPE_BASE))
     angles = position.astype(jnp.float32)[:, None] * frequency[None, :]
-    pair_view = values.reshape(values.shape[0], pair_count, 2)
-    even_part = pair_view[:, :, 0]
-    odd_part = pair_view[:, :, 1]
     cosine = jnp.cos(angles)
     sine_angle = jnp.sin(angles)
-    turned = jnp.stack(
-        [even_part * cosine - odd_part * sine_angle, even_part * sine_angle + odd_part * cosine],
-        axis=2,
-    )
-    return turned.reshape(values.shape)
+    signed_sine = jnp.where((col % 2 == 0)[None, :], -sine_angle, sine_angle)
+    cosine = jnp.tile(cosine, (1, cols // width))
+    signed_sine = jnp.tile(signed_sine, (1, cols // width))
+    is_even = (jnp.arange(cols, dtype=jnp.int32) % 2 == 0)[None, :]
+    partner = jnp.where(is_even, jnp.roll(values, -1, axis=1), jnp.roll(values, 1, axis=1))
+    return values * cosine + partner * signed_sine
 
 
 def tenant_table(token_ids, adapter_rank, token_lengths, adapter_slot):

time: 223 us -> 210 us (0.942)
  local copies, waits for them, and re-layouts: 28.6 us -> 19.5 us
  matrix products: 94.4 us -> 87.1 us
  other arithmetic: 15 us -> 21.8 us
  waiting for transfers between devices: 18.9 us -> 15.9 us
    sub x1 -> x0, matrix products: 6.51 us -> none  [shards(): exp_scores = jnp.where(visible, jnp.exp(scores - row_top[..., None]), 0.0)]
    unnamed x39 -> x42, local copies, waits for them, and re-layouts: 7.25 us -> 2.63 us
    unnamed x0 -> x1, other arithmetic: none -> 4.37 us
    another operation x4 -> x1, other arithmetic: 5.16 us -> 0.83 us
    sub x1, other arithmetic: 0.56 us -> 4.59 us  [shards(): exp_scores = jnp.where(visible, jnp.exp(scores - row_top[..., None]), 0.0)]
    reduce_scatter x1, waiting for transfers between devices: 8.17 us -> 5.46 us  [shards(): lax.psum_scatter(query_terms.reshape(ring * chunk, -1), ('seq', 'load'),...]
  transfers between devices with their start and end apart: 7 -> 7, of which waited for: 3 -> 3; matrix products, arithmetic and copies ran while one was open for 49% -> 53% of each run, Pallas kernels for 0% -> 0%
where the time goes in v7:
time: 210 us
  matrix products  87.1 us (41%)
  blocking collectives  43.2 us (21%)
  other arithmetic  21.8 us (10%)
  local copies, waits for them, and re-layouts  19.5 us (9%)
  between operations  16.2 us (8%)
  waiting for transfers between devices  15.9 us (8%)
  starting transfers between devices  6.05 us (3%)
    dot_general x18, matrix products, product(): return jnp.dot(left, right, preferred_element_type=jnp.float32)  85.1 us
    all_gather x1, blocking collectives, shards(): kv_all = lax.all_gather(kv_local, 'tensor', axis=1, tiled=True)  16 us
    all_gather x1, blocking collectives, shards(): lax.all_gather(jnp.concatenate([low_query, low_keyval], axis=1), 'tensor'...  13.2 us
    all_gather x1, blocking collectives, shards(): lax.all_gather(jnp.concatenate([key_heads, value_heads], axis=1), ('seq',...  11.1 us
    ppermute x2, waiting for transfers between devices, ring_reduce_scatter(): total = lax.ppermute(total, axis, shift) + pick(step)  7.27 us
    reduce_scatter x1, waiting for transfers between devices, shards(): lax.psum_scatter(query_terms.reshape(ring * chunk, -1), ('seq', 'load'),...  5.46 us
    broadcast_in_dim x1, local copies, waits for them, and re-layouts, shards(): query_terms = jnp.zeros((ring, chunk, query_cols), jnp.float32)  4.78 us
    ppermute x3, starting transfers between devices, shards(): following = lax.ppermute(held, 'tensor', shift) if step < ring - 1 else None  4.6 us
  transfers between devices with their start and end apart: 7, of which 3 were waited for; matrix products, arithmetic and copies ran while one was open for 53% of the time, Pallas kernels for 0%

profile of v7, /device:TPU:0, one launch (start us, length us, event | category | flops | bytes accessed | tf_op | source)
XLA Modules:
  0.0 209.7 jit_solution(15467492953686906462)
XLA Ops:
  8.1 3.1 %collective-permute-start = (bf16[128,4096]{1,0:T(8,128)(2,1)}, bf16[128,4096]{1,0:T(8,128)(2,1)S(1)}, u32[]{:S(2)}, u32[]{:S(2)}) collective-permute-start(bf16[128,4096]{1,0:T(8,128)(2,1)} %param.10), channel_id=1, source_target_pairs={{0,4},{4,8},{8,12},{12,0},{1,5},{5,9},{9,13},{13,1},{2,6},{6,10},{... | collective-permute-start | bytes 3145736 | tf_op jit(solution)/shard_map/ppermute | solution.py:119
  12.9 1.7 fusion.44
  14.6 1.8 fusion.45
  16.4 4.8 %broadcast_in_dim.274 = f32[4,128,4096]{2,1,0:T(8,128)} broadcast(f32[]{:T(128)} %constant.193.clone.1), dimensions={} | broadcast | bytes 8388612 | tf_op jit(solution)/shard_map/broadcast_in_dim | solution.py:115
  21.2 15.4 %fusion.5 = f32[4,128,4096]{2,1,0:T(8,128)} fusion(f32[4,128,4096]{2,1,0:T(8,128)} %broadcast_in_dim.274, s32[]{:T(128)S(6)} %select_n.262, bf16[128,4096]{1,0:T(8,128)(2,1)S(1)} %copy-done.1, bf16[4096,4096]{1,0:T(8,128)(2,1)} %param.11), kind=kOutput, calls=%fused_computation.11 | convolution fusion | flops 4294967296 | bytes 36700164 | tf_op jit(solution)/shard_map/dot_general | solution.py:19
  37.5 2.9 %fusion.43 = f32[128,512]{1,0:T(8,128)S(1)} fusion(bf16[128,4096]{1,0:T(8,128)(2,1)S(1)} %copy-done.1, bf16[4096,512]{1,0:T(8,128)(2,1)} %param.12), kind=kOutput, calls=%fused_computation.141 | convolution fusion | flops 536870912 | bytes 5505024 | tf_op jit(solution)/shard_map/dot_general | solution.py:19
  43.4 14.3 %fusion.4 = f32[4,128,4096]{2,1,0:T(8,128)} fusion(f32[4,128,4096]{2,1,0:T(8,128)} %fusion.5, s32[]{:T(128)S(6)} %select_n.267, bf16[128,4096]{1,0:T(8,128)(2,1)S(1)} %collective-permute-done, bf16[4096,4096]{1,0:T(8,128)(2,1)} %param.11), kind=kOutput, calls=%fused_computation.9 | convolution fusion | flops 4294967296 | bytes 36700164 | tf_op jit(solution)/shard_map/dot_general | solution.py:19
  59.7 2.9 %fusion.46 = f32[128,512]{1,0:T(8,128)S(1)} fusion(bf16[128,4096]{1,0:T(8,128)(2,1)S(1)} %collective-permute-done, bf16[4096,512]{1,0:T(8,128)(2,1)} %param.12), kind=kOutput, calls=%fused_computation.144 | convolution fusion | flops 536870912 | bytes 5505024 | tf_op jit(solution)/shard_map/dot_general | solution.py:19
  65.3 3.1 %collective-permute-done.1 = bf16[128,4096]{1,0:T(8,128)(2,1)} collective-permute-done((bf16[128,4096]{1,0:T(8,128)(2,1)S(1)}, bf16[128,4096]{1,0:T(8,128)(2,1)}, u32[]{:S(2)}, u32[]{:S(2)}) %collective-permute-start.1) | collective-permute-done | bytes 1048608 | tf_op jit(solution)/shard_map/ppermute | solution.py:119
  68.4 16.7 %fusion.3 = f32[4,128,4096]{2,1,0:T(8,128)} fusion(f32[4,128,4096]{2,1,0:T(8,128)} %fusion.4, s32[]{:T(128)S(6)} %select_n.272, bf16[128,4096]{1,0:T(8,128)(2,1)} %collective-permute-done.1, bf16[4096,4096]{1,0:T(8,128)(2,1)} %param.11), kind=kOutput, calls=%fused_computation.7 | convolution fusion | flops 4294967296 | bytes 36700164 | tf_op jit(solution)/shard_map/dot_general | solution.py:19
  86.8 1.7 fusion.51
  89.5 3.3 %fusion.49 = f32[128,512]{1,0:T(8,128)S(1)} fusion(bf16[128,4096]{1,0:T(8,128)(2,1)} %collective-permute-done.1, bf16[4096,512]{1,0:T(8,128)(2,1)} %param.12), kind=kOutput, calls=%fused_computation.147 | convolution fusion | flops 536870912 | bytes 5505024 | tf_op jit(solution)/shard_map/dot_general | solution.py:19
  95.5 14.2 %fusion.2 = f32[4,128,4096]{2,1,0:T(8,128)} fusion(f32[4,128,4096]{2,1,0:T(8,128)} %fusion.3, s32[]{:T(128)S(6)} %select_n.277, bf16[128,4096]{1,0:T(8,128)(2,1)S(1)} %collective-permute-done.2, bf16[4096,4096]{1,0:T(8,128)(2,1)} %param.11), kind=kOutput, calls=%fused_computation.5 | convolution fusion | flops 4294967296 | bytes 36700164 | tf_op jit(solution)/shard_map/dot_general | solution.py:19
  114.5 3.1 %fusion.52 = f32[128,512]{1,0:T(8,128)S(1)} fusion(bf16[128,4096]{1,0:T(8,128)(2,1)S(1)} %collective-permute-done.2, bf16[4096,512]{1,0:T(8,128)(2,1)} %param.12), kind=kOutput, calls=%fused_computation.150 | convolution fusion | flops 536870912 | bytes 5505024 | tf_op jit(solution)/shard_map/dot_general | solution.py:19
  119.4 2.8 %all_gather.20 = bf16[512,512]{1,0:T(8,128)(2,1)S(1)} all-gather(bf16[256,512]{1,0:T(8,128)(2,1)S(1)} %copy-done.7), channel_id=1, replica_groups=mesh['groups'=2,'tensor'=4,'seq'=2,'load'=2] {'load'}, dimensions={0}, use_global_device_ids=true | all-gather | bytes 786432 | tf_op jit(solution)/shard_map/all_gather | solution.py:110
  127.6 7.3 %collective-permute-done.4 = f32[128,576]{1,0:T(8,128)S(1)} collective-permute-done((f32[128,576]{1,0:T(8,128)S(1)}, f32[128,576]{1,0:T(8,128)S(1)}, u32[]{:S(2)}, u32[]{:S(2)}) %collective-permute-start.4) | collective-permute-done | bytes 294944 | tf_op jit(solution)/shard_map/ppermute | solution.py:85
  135.8 13.2 %all-gather = bf16[128,256]{0,1:T(8,128)(2,1)S(1)} all-gather(bf16[128,64]{0,1:T(8,128)(2,1)S(1)} %copy.81), channel_id=2, replica_groups=mesh['groups'=2,'tensor'=4,'seq'=2,'load'=2] {'tensor'}, dimensions={1}, use_global_device_ids=true | all-gather | bytes 81920 | tf_op jit(solution)/shard_map/all_gather | solution.py:158
  150.7 16.0 %all_gather.21 = bf16[128,2048]{1,0:T(8,128)(2,1)S(1)} all-gather(bf16[128,512]{1,0:T(8,128)(2,1)S(1)} %fusion.21), channel_id=1, replica_groups=mesh['groups'=2,'tensor'=4,'seq'=2,'load'=2] {'tensor'}, dimensions={1}, use_global_device_ids=true | all-gather | bytes 655360 | tf_op jit(solution)/shard_map/all_gather | solution.py:172
  167.2 11.1 %all_gather.22 = bf16[512,4,128]{2,0,1:T(8,128)(2,1)} all-gather(bf16[128,4,128]{2,0,1:T(8,128)(2,1)S(1)} %pad_maximum_fusion), channel_id=1, replica_groups=mesh['groups'=2,'tensor'=4,'seq'=2,'load'=2] {'seq','load'}, dimensions={0}, use_global_device_ids=true | all-gather | bytes 655360 | tf_op jit(solution)/shard_map/all_gather | solution.py:185
  178.3 2.9 %fusion.55 = f32[128,4096]{1,0:T(8,128)S(1)} fusion(bf16[128,512]{0,1:T(8,128)(2,1)S(1)} %bitcast.157, bf16[512,4096]{1,0:T(8,128)(2,1)} %all-gather.3.cloned.1.call-done), kind=kOutput, calls=%fused_computation.153 | convolution fusion | flops 536870912 | bytes 6422528 | tf_op jit(solution)/shard_map/dot_general | solution.py:19
  181.3 5.5 %reduce-scatter.2.cloned.1.call-done = f32[128,4096]{1,0:T(8,128)} async-done(((f32[512,4096]{1,0:T(8,128)}), f32[128,4096]{1,0:T(8,128)}) %reduce-scatter.2.cloned.1.call-update) | async-done | bytes 2097168 | tf_op jit(solution)/shard_map/reduce_scatter | solution.py:145
  186.7 1.8 add.313
  189.6 4.4 %fusion.18 = bf16[16,8,32,128]{3,1,2,0:T(8,128)(2,1)S(1)} fusion(f32[16,8,32,128]{3,2,1,0:T(8,128)S(1)} %bitcast.151, f32[128,4095]{1,0:T(8,128)S(1)} %get-tuple-element.50, f32[128,1]{1,0:T(8,128)S(1)} %get-tuple-element.52, f32[128,1]{1,0:T(8,128)S(1)} %get-tuple-element.51, f32[128,4095]{1,0:T(8,128)S(1)} %get-tuple-element.49, f32[128,4096]{1,0:T(8,128)S(1)} %add.313, ...), kind=kLoop, calls=%fused_computation.26 | loop fusion | flops 3670016 | bytes 11538432
  195.6 4.6 %fusion.42 = (f32[2,16,128]{2,1,0:T(8,128)S(1)}, bf16[2,16,128,512]{2,3,1,0:T(8,128)(2,1)S(1)}) fusion(f32[2,512,128,16]{2,1,3,0:T(8,128)S(1)} %fusion.16, pred[128,512]{0,1:T(8,128)(4,1)S(1)} %copy-done.12), kind=kOutput, calls=%fused_computation.140 | output fusion | flops 16777728 | bytes 12664832 | tf_op jit(solution)/shard_map/sub | solution.py:202
  (133 shorter events, 34.9 us)
Async XLA Ops:
  8.0 4.9 %copy-start = (bf16[4096,128]{1,0:T(8,128)(2,1)S(1)}, bf16[4096,128]{1,0:T(8,128)(2,1)}, u32[]{:S(2)}) copy-start(bf16[4096,128]{1,0:T(8,128)(2,1)} %param.13) | copy-start | bytes 3145732
  8.0 6.6 %copy-start.1 = (bf16[128,4096]{1,0:T(8,128)(2,1)S(1)}, bf16[128,4096]{1,0:T(8,128)(2,1)}, u32[]{:S(2)}) copy-start(bf16[128,4096]{1,0:T(8,128)(2,1)} %param.10) | copy-start | bytes 3145732
  8.0 170.3 %all-gather.3.cloned.1.call-start = ((), (), s32[]{:S(2)}) async-start(), calls=%async_computation.2 | async-start | bytes 6291456 | tf_op jit(solution)/shard_map/all_gather | solution.py:109
  8.1 32.8 %collective-permute-start = (bf16[128,4096]{1,0:T(8,128)(2,1)}, bf16[128,4096]{1,0:T(8,128)(2,1)S(1)}, u32[]{:S(2)}, u32[]{:S(2)}) collective-permute-start(bf16[128,4096]{1,0:T(8,128)(2,1)} %param.10), channel_id=1, source_target_pairs={{0,4},{4,8},{8,12},{12,0},{1,5},{5,9},{9,13},{13,1},{2,6},{6,10},{... | collective-permute-start | bytes 3145736 | tf_op jit(solution)/shard_map/ppermute | solution.py:119
  11.2 175.5 %reduce-scatter.2.cloned.1.call-start = ((), (), s32[]{:S(2)}) async-start(), calls=%async_computation.1 | async-start | bytes 10485760 | tf_op jit(solution)/shard_map/reduce_scatter | solution.py:145
  21.2 15.4 %copy-start.18 = (s32[4]{0:T(128)S(1)}, s32[4]{0:T(128)}, u32[]{:S(2)}) copy-start(s32[4]{0:T(128)} %param.17) | copy-start | bytes 52
  21.2 15.4 %copy-start.19 = (s32[4]{0:T(128)S(1)}, s32[4]{0:T(128)}, u32[]{:S(2)}) copy-start(s32[4]{0:T(128)} %param.19) | copy-start | bytes 52
  40.9 17.3 %copy-start.2 = (bf16[4096,128]{1,0:T(8,128)(2,1)S(1)}, bf16[4096,128]{1,0:T(8,128)(2,1)}, u32[]{:S(2)}) copy-start(bf16[4096,128]{1,0:T(8,128)(2,1)} %param.14) | copy-start | bytes 3145732
  41.9 26.5 %collective-permute-start.1 = (bf16[128,4096]{1,0:T(8,128)(2,1)S(1)}, bf16[128,4096]{1,0:T(8,128)(2,1)}, u32[]{:S(2)}, u32[]{:S(2)}) collective-permute-start(bf16[128,4096]{1,0:T(8,128)(2,1)S(1)} %collective-permute-done), channel_id=1, source_target_pairs={{0,4},{4,8},{8,12},{12,0},{1,5},{5,9},{9,13},{13,1},{2,6},{6,10},{... | collective-permute-start | bytes 3145736 | tf_op jit(solution)/shard_map/ppermute | solution.py:119
  59.6 2.9 %copy-start.10 = (f32[128,32]{1,0:T(8,128)S(1)}, f32[128,32]{1,0:T(8,128)}, u32[]{:S(2)}) copy-start(f32[128,32]{1,0:T(8,128)} %copy.71) | copy-start | bytes 49156
  68.4 27.1 %collective-permute-start.2 = (bf16[128,4096]{1,0:T(8,128)(2,1)}, bf16[128,4096]{1,0:T(8,128)(2,1)S(1)}, u32[]{:S(2)}, u32[]{:S(2)}) collective-permute-start(bf16[128,4096]{1,0:T(8,128)(2,1)} %collective-permute-done.1), channel_id=1, source_target_pairs={{0,4},{4,8},{8,12},{12,0},{1,5},{5,9},{9,13},{13,1},{2,6},{6,10},{... | collective-permute-start | bytes 3145736 | tf_op jit(solution)/shard_map/ppermute | solution.py:119
  89.5 3.3 %copy-start.11 = (f32[128,32]{1,0:T(8,128)S(1)}, f32[128,32]{1,0:T(8,128)}, u32[]{:S(2)}) copy-start(f32[128,32]{1,0:T(8,128)} %copy.74) | copy-start | bytes 49156
  109.7 1.7 copy-start.14
  113.0 4.9 %copy-start.4 = (f32[4,128,576]{1,2,0:T(8,128)S(1)}, f32[4,128,576]{1,2,0:T(8,128)}, u32[]{:S(2)}) copy-start(f32[4,128,576]{1,2,0:T(8,128)} %constant_dynamic-update-slice_fusion.1) | copy-start | bytes 3538948
  114.5 3.1 %copy-start.8 = (f32[128,32]{1,0:T(8,128)S(1)}, f32[128,32]{1,0:T(8,128)}, u32[]{:S(2)}) copy-start(f32[128,32]{1,0:T(8,128)} %copy.76) | copy-start | bytes 49156
  114.5 3.1 %copy-start.9 = (f32[128,32]{1,0:T(8,128)S(1)}, f32[128,32]{1,0:T(8,128)}, u32[]{:S(2)}) copy-start(f32[128,32]{1,0:T(8,128)} %copy.77) | copy-start | bytes 49156
  114.5 4.8 %copy-start.7 = (bf16[256,512]{1,0:T(8,128)(2,1)S(1)}, bf16[256,512]{1,0:T(8,128)(2,1)}, u32[]{:S(2)}) copy-start(bf16[256,512]{1,0:T(8,128)(2,1)} %param.16) | copy-start | bytes 786436
  118.8 4.5 %collective-permute-start.3 = (f32[2,128,576]{1,2,0:T(8,128)}, f32[2,128,576]{1,2,0:T(8,128)}, u32[]{:S(2)}, u32[]{:S(2)}) collective-permute-start(f32[2,128,576]{1,2,0:T(8,128)} %dynamic-slice_bitcast_fusion), channel_id=1, source_target_pairs={{0,1},{1,0},{2,3},{3,2},{4,5},{5,4},{6,7},{7,6},{8,9},{9,8},{10,11... | collective-permute-start | bytes 1769480 | tf_op jit(solution)/shard_map/ppermute | solution.py:85
  123.4 11.5 %copy-start.17 = (s32[32]{0:T(128)S(1)}, s32[32]{0:T(128)}, u32[]{:S(2)}) copy-start(s32[32]{0:T(128)} %iota_add_fusion) | copy-start | bytes 388
  124.6 25.8 %copy-start.15 = (pred[512]{0:T(512)(128)(4,1)S(1)}, pred[512]{0:T(512)(128)(4,1)}, u32[]{:S(2)}) copy-start(pred[512]{0:T(512)(128)(4,1)} %get-tuple-element.79) | copy-start | bytes 1540
  124.6 25.8 %copy-start.16 = (pred[512]{0:T(512)(128)(4,1)S(1)}, pred[512]{0:T(512)(128)(4,1)}, u32[]{:S(2)}) copy-start(pred[512]{0:T(512)(128)(4,1)} %get-tuple-element.80) | copy-start | bytes 1540
  124.9 10.0 %collective-permute-start.4 = (f32[128,576]{1,0:T(8,128)S(1)}, f32[128,576]{1,0:T(8,128)S(1)}, u32[]{:S(2)}, u32[]{:S(2)}) collective-permute-start(f32[128,576]{1,0:T(8,128)S(1)} %bitcast.159), channel_id=1, source_target_pairs={{0,2},{2,0},{1,3},{3,1},{4,6},{6,4},{5,7},{7,5},{8,10},{10,8},{9,1... | collective-permute-start | bytes 884744 | tf_op jit(solution)/shard_map/ppermute | solution.py:85
  150.6 30.6 %copy-start.6 = (bf16[128,512]{1,0:T(8,128)(2,1)}, bf16[128,512]{1,0:T(8,128)(2,1)S(1)}, u32[]{:S(2)}) copy-start(bf16[128,512]{1,0:T(8,128)(2,1)S(1)} %fusion.21) | copy-start | bytes 393220
  189.6 4.6 %copy-start.5 = (bf16[512,4,128]{2,0,1:T(8,128)(2,1)S(1)}, bf16[512,4,128]{2,0,1:T(8,128)(2,1)}, u32[]{:S(2)}) copy-start(bf16[512,4,128]{2,0,1:T(8,128)(2,1)} %all_gather.22) | copy-start | bytes 1572868
  (3 other events, 4.0 us)
Sparse Core Ops, SparseCore 0:
  11.3 15.5 all-gather.2
Sparse Core Ops, SparseCore 1:
  109.8 76.9 reduce-scatter.1

commit v8 on v7

--- a/solution.py
+++ b/solution.py
@@ -129,13 +129,29 @@
             axis=1,
         )
         small_terms = lax.dynamic_update_slice_in_dim(small_terms, small_block[None], owner, 0)
-        query_terms = lax.dynamic_update_slice_in_dim(
-            query_terms, product(held, weight_query)[None], owner, 0
-        )
+        if step == 0 and ring > 2:
+            first_block, first_owner = held, owner
+        elif step == 1 and ring > 2:
+            pair = product(jnp.concatenate([first_block, held], axis=0), weight_query)
+            query_terms = lax.dynamic_update_slice_in_dim(
+                query_terms, pair[:chunk][None], first_owner, 0
+            )
+            query_terms = lax.dynamic_update_slice_in_dim(
+                query_terms, pair[chunk:][None], owner, 0
+            )
+        else:
+            query_terms = lax.dynamic_update_slice_in_dim(
+                query_terms, product(held, weight_query)[None], owner, 0
+            )
         if following is not None:
-            following, small_terms, query_terms = lax.optimization_barrier(
-                (following, small_terms, query_terms)
-            )
+            if step == 0 and ring > 2:
+                following, small_terms, first_block = lax.optimization_barrier(
+                    (following, small_terms, first_block)
+                )
+            else:
+                following, small_terms, query_terms = lax.optimization_barrier(
+                    (following, small_terms, query_terms)
+                )
         held = following
     seq_count = lax.axis_size("seq")
     load_count = lax.axis_size("load")

time: 210 us -> 208 us (level)
  waiting for transfers between devices: 15.9 us -> 34.7 us
  matrix products: 87.1 us -> 68.6 us
  other arithmetic: 21.8 us -> 18.7 us
  local copies, waits for them, and re-layouts: 19.5 us -> 21.7 us
    dot_general x18 -> x17, matrix products: 85.1 us -> 66.6 us  [product(): return jnp.dot(left, right, preferred_element_type=jnp.float32)]
    ppermute x3, waiting for transfers between devices: 3.14 us -> 18.6 us  [shards(): following = lax.ppermute(held, 'tensor', shift) if step < ring - 1 else None]
    dynamic_update_slice x0 -> x2, local copies, waits for them, and re-layouts: none -> 3.07 us  [the longest x1 1.54 us: shards(): lax.dynamic_update_slice_in_dim(query_terms, pair[:chunk][None], first_ow...]
    reduce_scatter x1, waiting for transfers between devices: 5.46 us -> 7.85 us  [shards(): lax.psum_scatter(query_terms.reshape(ring * chunk, -1), ('seq', 'load'),...]
  transfers between devices with their start and end apart: 7 -> 7, of which waited for: 3 -> 5; matrix products, arithmetic and copies ran while one was open for 53% -> 45% of each run, Pallas kernels for 0% -> 0%
where the time goes in v8:
time: 208 us; the launch traced here: 207 us
  matrix products  68.6 us (33%)
  blocking collectives  41.7 us (20%)
  waiting for transfers between devices  34.7 us (17%)
  local copies, waits for them, and re-layouts  21.7 us (10%)
  other arithmetic  18.7 us (9%)
  between operations  16.3 us (8%)
  starting transfers between devices  5.33 us (3%)
    dot_general x17, matrix products, product(): return jnp.dot(left, right, preferred_element_type=jnp.float32)  66.6 us
    ppermute x3, waiting for transfers between devices, shards(): following = lax.ppermute(held, 'tensor', shift) if step < ring - 1 else None  18.6 us
    all_gather x1, blocking collectives, shards(): kv_all = lax.all_gather(kv_local, 'tensor', axis=1, tiled=True)  14.7 us
    all_gather x1, blocking collectives, shards(): lax.all_gather(jnp.concatenate([low_query, low_keyval], axis=1), 'tensor'...  13.2 us
    all_gather x1, blocking collectives, shards(): lax.all_gather(jnp.concatenate([key_heads, value_heads], axis=1), ('seq',...  11 us
    ppermute x2, waiting for transfers between devices, ring_reduce_scatter(): total = lax.ppermute(total, axis, shift) + pick(step)  8.27 us
    reduce_scatter x1, waiting for transfers between devices, shards(): lax.psum_scatter(query_terms.reshape(ring * chunk, -1), ('seq', 'load'),...  7.85 us
    sub x1, other arithmetic, shards(): exp_scores = jnp.where(visible, jnp.exp(scores - row_top[..., None]), 0.0)  4.59 us
  transfers between devices with their start and end apart: 7, of which 5 were waited for; matrix products, arithmetic and copies ran while one was open for 45% of the time, Pallas kernels for 0%

profile of v8, /device:TPU:0, one launch (start us, length us, event | category | flops | bytes accessed | tf_op | source)
XLA Modules:
  0.0 207.1 jit_solution(4631039663662523461)
XLA Ops:
  8.1 3.1 %collective-permute-start = (bf16[128,4096]{1,0:T(8,128)(2,1)}, bf16[128,4096]{1,0:T(8,128)(2,1)}, u32[]{:S(2)}, u32[]{:S(2)}) collective-permute-start(bf16[128,4096]{1,0:T(8,128)(2,1)} %param.10), channel_id=1, source_target_pairs={{0,4},{4,8},{8,12},{12,0},{1,5},{5,9},{9,13},{13,1},{2,6},{6,10},{... | collective-permute-start | bytes 3145736 | tf_op jit(solution)/shard_map/ppermute | solution.py:119
  12.9 1.7 fusion.49
  16.1 2.9 %fusion.48 = f32[128,512]{1,0:T(8,128)S(1)} fusion(bf16[128,4096]{1,0:T(8,128)(2,1)S(1)} %copy-done.5, bf16[4096,512]{1,0:T(8,128)(2,1)} %param.12), kind=kOutput, calls=%fused_computation.146 | convolution fusion | flops 536870912 | bytes 5505024 | tf_op jit(solution)/shard_map/dot_general | solution.py:19
  21.2 15.5 %collective-permute-done = bf16[128,4096]{1,0:T(8,128)(2,1)} collective-permute-done((bf16[128,4096]{1,0:T(8,128)(2,1)}, bf16[128,4096]{1,0:T(8,128)(2,1)}, u32[]{:S(2)}, u32[]{:S(2)}) %collective-permute-start) | collective-permute-done | bytes 1048608 | tf_op jit(solution)/shard_map/ppermute | solution.py:119
  36.7 1.7 fusion.52
  38.4 1.7 fusion.53
  40.2 2.8 %fusion.51 = f32[128,512]{1,0:T(8,128)} fusion(bf16[128,4096]{1,0:T(8,128)(2,1)} %collective-permute-done, bf16[4096,512]{1,0:T(8,128)(2,1)S(1)} %copy-done.1), kind=kOutput, calls=%fused_computation.149 | convolution fusion | flops 536870912 | bytes 5505024 | tf_op jit(solution)/shard_map/dot_general | solution.py:19
  45.9 15.3 %fusion.13 = f32[256,4096]{1,0:T(8,128)S(1)} fusion(bf16[4096,4096]{1,0:T(8,128)(2,1)} %param.11, bf16[128,4096]{1,0:T(8,128)(2,1)} %collective-permute-done, bf16[128,4096]{1,0:T(8,128)(2,1)S(1)} %copy-done.6), kind=kOutput, calls=%fused_computation.21 | convolution fusion | flops 8594128896 | bytes 39845888 | tf_op jit(solution)/shard_map/dot_general | solution.py:19
  61.2 4.3 %broadcast_in_dim.276 = f32[4,128,4096]{2,1,0:T(8,128)} broadcast(f32[]{:T(128)} %constant.193.clone.1), dimensions={} | broadcast | bytes 8388612 | tf_op jit(solution)/shard_map/broadcast_in_dim | solution.py:115
  70.5 14.2 %fusion.3 = f32[4,128,4096]{2,1,0:T(8,128)} fusion(f32[4,128,4096]{2,1,0:T(8,128)} %fusion.11, s32[]{:T(128)S(6)} %select_n.272, bf16[128,4096]{1,0:T(8,128)(2,1)S(1)} %collective-permute-done.1, bf16[4096,4096]{1,0:T(8,128)(2,1)} %param.11), kind=kOutput, calls=%fused_computation.7 | convolution fusion | flops 4294967296 | bytes 36700164 | tf_op jit(solution)/shard_map/dot_general | solution.py:19
  86.8 2.9 %fusion.54 = f32[128,512]{1,0:T(8,128)S(1)} fusion(bf16[128,4096]{1,0:T(8,128)(2,1)S(1)} %collective-permute-done.1, bf16[4096,512]{1,0:T(8,128)(2,1)} %param.12), kind=kOutput, calls=%fused_computation.152 | convolution fusion | flops 536870912 | bytes 5505024 | tf_op jit(solution)/shard_map/dot_general | solution.py:19
  92.4 3.0 %collective-permute-done.2 = bf16[128,4096]{1,0:T(8,128)(2,1)S(1)} collective-permute-done((bf16[128,4096]{1,0:T(8,128)(2,1)S(1)}, bf16[128,4096]{1,0:T(8,128)(2,1)S(1)}, u32[]{:S(2)}, u32[]{:S(2)}) %collective-permute-start.2) | collective-permute-done | bytes 1048608 | tf_op jit(solution)/shard_map/ppermute | solution.py:119
  95.4 14.2 %fusion.2 = f32[4,128,4096]{2,1,0:T(8,128)} fusion(f32[4,128,4096]{2,1,0:T(8,128)} %fusion.3, s32[]{:T(128)S(6)} %select_n.277, bf16[128,4096]{1,0:T(8,128)(2,1)S(1)} %collective-permute-done.2, bf16[4096,4096]{1,0:T(8,128)(2,1)} %param.11), kind=kOutput, calls=%fused_computation.5 | convolution fusion | flops 4294967296 | bytes 36700164 | tf_op jit(solution)/shard_map/dot_general | solution.py:19
  112.2 3.1 %fusion.57 = f32[128,512]{1,0:T(8,128)S(1)} fusion(bf16[128,4096]{1,0:T(8,128)(2,1)S(1)} %collective-permute-done.2, bf16[4096,512]{1,0:T(8,128)(2,1)} %param.12), kind=kOutput, calls=%fused_computation.155 | convolution fusion | flops 536870912 | bytes 5505024 | tf_op jit(solution)/shard_map/dot_general | solution.py:19
  117.7 2.8 %all_gather.20 = bf16[512,512]{1,0:T(8,128)(2,1)S(1)} all-gather(bf16[256,512]{1,0:T(8,128)(2,1)S(1)} %copy-done.10), channel_id=1, replica_groups=mesh['groups'=2,'tensor'=4,'seq'=2,'load'=2] {'load'}, dimensions={0}, use_global_device_ids=true | all-gather | bytes 786432 | tf_op jit(solution)/shard_map/all_gather | solution.py:110
  124.3 8.3 %collective-permute-done.4 = f32[128,576]{1,0:T(8,128)S(1)} collective-permute-done((f32[128,576]{1,0:T(8,128)S(1)}, f32[128,576]{1,0:T(8,128)S(1)}, u32[]{:S(2)}, u32[]{:S(2)}) %collective-permute-start.4) | collective-permute-done | bytes 294944 | tf_op jit(solution)/shard_map/ppermute | solution.py:85
  132.9 13.2 %all-gather = bf16[128,256]{0,1:T(8,128)(2,1)S(1)} all-gather(bf16[128,64]{0,1:T(8,128)(2,1)S(1)} %copy.81), channel_id=2, replica_groups=mesh['groups'=2,'tensor'=4,'seq'=2,'load'=2] {'tensor'}, dimensions={1}, use_global_device_ids=true | all-gather | bytes 81920 | tf_op jit(solution)/shard_map/all_gather | solution.py:174
  147.1 14.7 %all_gather.21 = bf16[128,2048]{1,0:T(8,128)(2,1)S(1)} all-gather(bf16[128,512]{1,0:T(8,128)(2,1)S(1)} %fusion.25), channel_id=1, replica_groups=mesh['groups'=2,'tensor'=4,'seq'=2,'load'=2] {'tensor'}, dimensions={1}, use_global_device_ids=true | all-gather | bytes 655360 | tf_op jit(solution)/shard_map/all_gather | solution.py:188
  162.4 11.0 %all_gather.22 = bf16[512,4,128]{2,0,1:T(8,128)(2,1)} all-gather(bf16[128,4,128]{2,0,1:T(8,128)(2,1)S(1)} %pad_maximum_fusion), channel_id=1, replica_groups=mesh['groups'=2,'tensor'=4,'seq'=2,'load'=2] {'seq','load'}, dimensions={0}, use_global_device_ids=true | all-gather | bytes 655360 | tf_op jit(solution)/shard_map/all_gather | solution.py:201
  173.3 2.9 %fusion.60 = f32[128,4096]{1,0:T(8,128)S(1)} fusion(bf16[128,512]{0,1:T(8,128)(2,1)S(1)} %bitcast.152, bf16[512,4096]{1,0:T(8,128)(2,1)} %all-gather.3.cloned.1.call-done), kind=kOutput, calls=%fused_computation.158 | convolution fusion | flops 536870912 | bytes 6422528 | tf_op jit(solution)/shard_map/dot_general | solution.py:19
  176.3 7.8 %reduce-scatter.2.cloned.1.call-done = f32[128,4096]{1,0:T(8,128)} async-done(((f32[512,4096]{1,0:T(8,128)}), f32[128,4096]{1,0:T(8,128)}) %reduce-scatter.2.cloned.1.call-update) | async-done | bytes 2097168 | tf_op jit(solution)/shard_map/reduce_scatter | solution.py:161
  184.1 1.8 add.313
  187.0 4.4 %fusion.22 = bf16[16,8,32,128]{3,1,2,0:T(8,128)(2,1)S(1)} fusion(f32[16,8,32,128]{3,2,1,0:T(8,128)S(1)} %bitcast.148, f32[128,4095]{1,0:T(8,128)S(1)} %get-tuple-element.50, f32[128,1]{1,0:T(8,128)S(1)} %get-tuple-element.52, f32[128,1]{1,0:T(8,128)S(1)} %get-tuple-element.51, f32[128,4095]{1,0:T(8,128)S(1)} %get-tuple-element.49, f32[128,4096]{1,0:T(8,128)S(1)} %add.313, ...), kind=kLoop, calls=%fused_computation.30 | loop fusion | flops 3670016 | bytes 11538432
  193.0 4.6 %fusion.47 = (f32[2,16,128]{2,1,0:T(8,128)S(1)}, bf16[2,16,128,512]{2,3,1,0:T(8,128)(2,1)S(1)}) fusion(f32[2,512,128,16]{2,1,3,0:T(8,128)S(1)} %fusion.20, pred[128,512]{0,1:T(8,128)(4,1)S(1)} %copy-done.12), kind=kOutput, calls=%fused_computation.145 | output fusion | flops 16777728 | bytes 12664832 | tf_op jit(solution)/shard_map/sub | solution.py:218
  (134 shorter events, 32.6 us)
Async XLA Ops:
  8.0 4.9 %copy-start = (bf16[4096,128]{1,0:T(8,128)(2,1)S(1)}, bf16[4096,128]{1,0:T(8,128)(2,1)}, u32[]{:S(2)}) copy-start(bf16[4096,128]{1,0:T(8,128)(2,1)} %param.13) | copy-start | bytes 3145732
  8.0 6.6 %copy-start.5 = (bf16[128,4096]{1,0:T(8,128)(2,1)S(1)}, bf16[128,4096]{1,0:T(8,128)(2,1)}, u32[]{:S(2)}) copy-start(bf16[128,4096]{1,0:T(8,128)(2,1)} %param.10) | copy-start | bytes 3145732
  8.0 6.6 %copy-start.2 = (bf16[4096,128]{1,0:T(8,128)(2,1)S(1)}, bf16[4096,128]{1,0:T(8,128)(2,1)}, u32[]{:S(2)}) copy-start(bf16[4096,128]{1,0:T(8,128)(2,1)} %param.14) | copy-start | bytes 3145732
  8.0 7.2 %copy-start.18 = (s32[4]{0:T(128)S(1)}, s32[4]{0:T(128)}, u32[]{:S(2)}) copy-start(s32[4]{0:T(128)} %param.17) | copy-start | bytes 52
  8.0 7.2 %copy-start.19 = (s32[4]{0:T(128)S(1)}, s32[4]{0:T(128)}, u32[]{:S(2)}) copy-start(s32[4]{0:T(128)} %param.19) | copy-start | bytes 52
  8.1 165.3 %all-gather.3.cloned.1.call-start = ((), (), s32[]{:S(2)}) async-start(), calls=%async_computation.2 | async-start | bytes 6291456 | tf_op jit(solution)/shard_map/all_gather | solution.py:109
  8.1 28.6 %collective-permute-start = (bf16[128,4096]{1,0:T(8,128)(2,1)}, bf16[128,4096]{1,0:T(8,128)(2,1)}, u32[]{:S(2)}, u32[]{:S(2)}) collective-permute-start(bf16[128,4096]{1,0:T(8,128)(2,1)} %param.10), channel_id=1, source_target_pairs={{0,4},{4,8},{8,12},{12,0},{1,5},{5,9},{9,13},{13,1},{2,6},{6,10},{... | collective-permute-start | bytes 3145736 | tf_op jit(solution)/shard_map/ppermute | solution.py:119
  11.2 172.9 %reduce-scatter.2.cloned.1.call-start = ((), (), s32[]{:S(2)}) async-start(), calls=%async_computation.1 | async-start | bytes 10485760 | tf_op jit(solution)/shard_map/reduce_scatter | solution.py:161
  19.3 20.9 %copy-start.1 = (bf16[4096,512]{1,0:T(8,128)(2,1)S(1)}, bf16[4096,512]{1,0:T(8,128)(2,1)}, u32[]{:S(2)}) copy-start(bf16[4096,512]{1,0:T(8,128)(2,1)} %param.12) | copy-start | bytes 12582916
  40.2 5.7 %copy-start.6 = (bf16[128,4096]{1,0:T(8,128)(2,1)S(1)}, bf16[128,4096]{1,0:T(8,128)(2,1)}, u32[]{:S(2)}) copy-start(bf16[128,4096]{1,0:T(8,128)(2,1)} %param.10) | copy-start | bytes 3145732
  43.0 26.4 %collective-permute-start.1 = (bf16[128,4096]{1,0:T(8,128)(2,1)}, bf16[128,4096]{1,0:T(8,128)(2,1)S(1)}, u32[]{:S(2)}, u32[]{:S(2)}) collective-permute-start(bf16[128,4096]{1,0:T(8,128)(2,1)} %collective-permute-done), channel_id=1, source_target_pairs={{0,4},{4,8},{8,12},{12,0},{1,5},{5,9},{9,13},{13,1},{2,6},{6,10},{... | collective-permute-start | bytes 3145736 | tf_op jit(solution)/shard_map/ppermute | solution.py:119
  65.5 1.5 copy-start.8
  69.3 16.0 %copy-start.3 = (bf16[4096,128]{1,0:T(8,128)(2,1)S(1)}, bf16[4096,128]{1,0:T(8,128)(2,1)}, u32[]{:S(2)}) copy-start(bf16[4096,128]{1,0:T(8,128)(2,1)} %param.14) | copy-start | bytes 3145732
  69.4 26.1 %collective-permute-start.2 = (bf16[128,4096]{1,0:T(8,128)(2,1)S(1)}, bf16[128,4096]{1,0:T(8,128)(2,1)S(1)}, u32[]{:S(2)}, u32[]{:S(2)}) collective-permute-start(bf16[128,4096]{1,0:T(8,128)(2,1)S(1)} %collective-permute-done.1), channel_id=1, source_target_pairs={{0,4},{4,8},{8,12},{12,0},{1,5},{5,9},{9,13},{13,1},{2,6},{6,10},{... | collective-permute-start | bytes 3145736 | tf_op jit(solution)/shard_map/ppermute | solution.py:119
  86.8 2.9 %copy-start.11 = (f32[128,32]{1,0:T(8,128)S(1)}, f32[128,32]{1,0:T(8,128)}, u32[]{:S(2)}) copy-start(f32[128,32]{1,0:T(8,128)} %copy.74) | copy-start | bytes 49156
  109.7 1.7 copy-start.4
  112.2 5.5 %copy-start.10 = (bf16[256,512]{1,0:T(8,128)(2,1)S(1)}, bf16[256,512]{1,0:T(8,128)(2,1)}, u32[]{:S(2)}) copy-start(bf16[256,512]{1,0:T(8,128)(2,1)} %param.16) | copy-start | bytes 786436
  116.3 29.9 %copy-start.13 = (pred[128,4]{0,1:T(4,128)(4,1)S(1)}, pred[128,4]{0,1:T(4,128)(4,1)}, u32[]{:S(2)}) copy-start(pred[128,4]{0,1:T(4,128)(4,1)} %get-tuple-element.75) | copy-start | bytes 1540
  117.5 3.7 %collective-permute-start.3 = (f32[2,128,576]{1,2,0:T(8,128)S(1)}, f32[2,128,576]{1,2,0:T(8,128)S(1)}, u32[]{:S(2)}, u32[]{:S(2)}) collective-permute-start(f32[2,128,576]{1,2,0:T(8,128)S(1)} %dynamic-slice_bitcast_fusion), channel_id=1, source_target_pairs={{0,1},{1,0},{2,3},{3,2},{4,5},{5,4},{6,7},{7,6},{8,9},{9,8},{10,11... | collective-permute-start | bytes 1769480 | tf_op jit(solution)/shard_map/ppermute | solution.py:85
  122.4 24.5 %copy-start.16 = (pred[512]{0:T(512)(128)(4,1)S(1)}, pred[512]{0:T(512)(128)(4,1)}, u32[]{:S(2)}) copy-start(pred[512]{0:T(512)(128)(4,1)} %get-tuple-element.79) | copy-start | bytes 1540
  122.4 24.5 %copy-start.17 = (pred[512]{0:T(512)(128)(4,1)S(1)}, pred[512]{0:T(512)(128)(4,1)}, u32[]{:S(2)}) copy-start(pred[512]{0:T(512)(128)(4,1)} %get-tuple-element.80) | copy-start | bytes 1540
  122.7 9.9 %collective-permute-start.4 = (f32[128,576]{1,0:T(8,128)S(1)}, f32[128,576]{1,0:T(8,128)S(1)}, u32[]{:S(2)}, u32[]{:S(2)}) collective-permute-start(f32[128,576]{1,0:T(8,128)S(1)} %bitcast.154), channel_id=1, source_target_pairs={{0,2},{2,0},{1,3},{3,1},{4,6},{6,4},{5,7},{7,5},{8,10},{10,8},{9,1... | collective-permute-start | bytes 884744 | tf_op jit(solution)/shard_map/ppermute | solution.py:85
  147.1 29.1 %copy-start.9 = (bf16[128,512]{1,0:T(8,128)(2,1)}, bf16[128,512]{1,0:T(8,128)(2,1)S(1)}, u32[]{:S(2)}) copy-start(bf16[128,512]{1,0:T(8,128)(2,1)S(1)} %fusion.25) | copy-start | bytes 393220
  187.0 4.6 %copy-start.7 = (bf16[512,4,128]{2,0,1:T(8,128)(2,1)S(1)}, bf16[512,4,128]{2,0,1:T(8,128)(2,1)}, u32[]{:S(2)}) copy-start(bf16[512,4,128]{2,0,1:T(8,128)(2,1)} %all_gather.22) | copy-start | bytes 1572868
  (3 other events, 2.6 us)
Sparse Core Ops, SparseCore 0:
  11.3 15.5 all-gather.2
Sparse Core Ops, SparseCore 1:
  109.8 74.3 reduce-scatter.1

commit v9 on v8

--- a/solution.py
+++ b/solution.py
@@ -204,9 +204,11 @@
     piece_keys = both_heads[:, :kv_here]
     piece_values = both_heads[:, kv_here:]
     delta_query = lax.optimization_barrier(product(wide_query, up_query_all))
-    query_rows = rotate_pairs(
-        query_summed + delta_query, position, tensor_index * query_cols
-    ).astype(jnp.bfloat16)
+    query_rows = lax.optimization_barrier(
+        rotate_pairs(query_summed + delta_query, position, tensor_index * query_cols).astype(
+            jnp.bfloat16
+        )
+    )
     grouped = query_rows.reshape(block_rows, kv_here, per_kv, HEAD_DIM)
     key_ids = jnp.arange(piece_keys.shape[0], dtype=jnp.int32)
     visible = (key_ids[None, :] >= own_first[:, None]) & (key_ids[None, :] <= token_ids[:, None])

time: 208 us -> 208 us (level)
    unnamed x1 -> x0, other arithmetic: 4.37 us -> none
    convert_element_type x0 -> x1, other arithmetic: none -> 4.35 us  [shards(): rotate_pairs(query_summed + delta_query, position, tensor_index * query_c...]
where the time goes in v9:
time: 208 us; the launch traced here: 207 us
  matrix products  68.6 us (33%)
  blocking collectives  41.7 us (20%)
  waiting for transfers between devices  34.7 us (17%)
  local copies, waits for them, and re-layouts  21.7 us (10%)
  other arithmetic  18.7 us (9%)
  between operations  16.3 us (8%)
  starting transfers between devices  5.33 us (3%)
    dot_general x17, matrix products, product(): return jnp.dot(left, right, preferred_element_type=jnp.float32)  66.6 us
    ppermute x3, waiting for transfers between devices, shards(): following = lax.ppermute(held, 'tensor', shift) if step < ring - 1 else None  18.6 us
    all_gather x1, blocking collectives, shards(): kv_all = lax.all_gather(kv_local, 'tensor', axis=1, tiled=True)  14.7 us
    all_gather x1, blocking collectives, shards(): lax.all_gather(jnp.concatenate([low_query, low_keyval], axis=1), 'tensor'...  13.2 us
    all_gather x1, blocking collectives, shards(): lax.all_gather(jnp.concatenate([key_heads, value_heads], axis=1), ('seq',...  11 us
    ppermute x2, waiting for transfers between devices, ring_reduce_scatter(): total = lax.ppermute(total, axis, shift) + pick(step)  8.27 us
    reduce_scatter x1, waiting for transfers between devices, shards(): lax.psum_scatter(query_terms.reshape(ring * chunk, -1), ('seq', 'load'),...  7.85 us
    sub x1, other arithmetic, shards(): exp_scores = jnp.where(visible, jnp.exp(scores - row_top[..., None]), 0.0)  4.59 us
  transfers between devices with their start and end apart: 7, of which 5 were waited for; matrix products, arithmetic and copies ran while one was open for 45% of the time, Pallas kernels for 0%

profile of v9, /device:TPU:0, one launch (start us, length us, event | category | flops | bytes accessed | tf_op | source)
XLA Modules:
  0.0 207.1 jit_solution(12531631384162972766)
XLA Ops:
  8.1 3.1 %collective-permute-start = (bf16[128,4096]{1,0:T(8,128)(2,1)}, bf16[128,4096]{1,0:T(8,128)(2,1)}, u32[]{:S(2)}, u32[]{:S(2)}) collective-permute-start(bf16[128,4096]{1,0:T(8,128)(2,1)} %param.10), channel_id=1, source_target_pairs={{0,4},{4,8},{8,12},{12,0},{1,5},{5,9},{9,13},{13,1},{2,6},{6,10},{... | collective-permute-start | bytes 3145736 | tf_op jit(solution)/shard_map/ppermute | solution.py:119
  12.9 1.7 fusion.48
  16.1 2.9 %fusion.47 = f32[128,512]{1,0:T(8,128)S(1)} fusion(bf16[128,4096]{1,0:T(8,128)(2,1)S(1)} %copy-done.5, bf16[4096,512]{1,0:T(8,128)(2,1)} %param.12), kind=kOutput, calls=%fused_computation.145 | convolution fusion | flops 536870912 | bytes 5505024 | tf_op jit(solution)/shard_map/dot_general | solution.py:19
  21.2 15.5 %collective-permute-done = bf16[128,4096]{1,0:T(8,128)(2,1)} collective-permute-done((bf16[128,4096]{1,0:T(8,128)(2,1)}, bf16[128,4096]{1,0:T(8,128)(2,1)}, u32[]{:S(2)}, u32[]{:S(2)}) %collective-permute-start) | collective-permute-done | bytes 1048608 | tf_op jit(solution)/shard_map/ppermute | solution.py:119
  36.7 1.7 fusion.51
  38.4 1.7 fusion.52
  40.2 2.8 %fusion.50 = f32[128,512]{1,0:T(8,128)} fusion(bf16[128,4096]{1,0:T(8,128)(2,1)} %collective-permute-done, bf16[4096,512]{1,0:T(8,128)(2,1)S(1)} %copy-done.1), kind=kOutput, calls=%fused_computation.148 | convolution fusion | flops 536870912 | bytes 5505024 | tf_op jit(solution)/shard_map/dot_general | solution.py:19
  45.9 15.3 %fusion.13 = f32[256,4096]{1,0:T(8,128)S(1)} fusion(bf16[4096,4096]{1,0:T(8,128)(2,1)} %param.11, bf16[128,4096]{1,0:T(8,128)(2,1)} %collective-permute-done, bf16[128,4096]{1,0:T(8,128)(2,1)S(1)} %copy-done.6), kind=kOutput, calls=%fused_computation.21 | convolution fusion | flops 8594128896 | bytes 39845888 | tf_op jit(solution)/shard_map/dot_general | solution.py:19
  61.2 4.3 %broadcast_in_dim.276 = f32[4,128,4096]{2,1,0:T(8,128)} broadcast(f32[]{:T(128)} %constant.193.clone.1), dimensions={} | broadcast | bytes 8388612 | tf_op jit(solution)/shard_map/broadcast_in_dim | solution.py:115
  70.5 14.2 %fusion.3 = f32[4,128,4096]{2,1,0:T(8,128)} fusion(f32[4,128,4096]{2,1,0:T(8,128)} %fusion.11, s32[]{:T(128)S(6)} %select_n.272, bf16[128,4096]{1,0:T(8,128)(2,1)S(1)} %collective-permute-done.1, bf16[4096,4096]{1,0:T(8,128)(2,1)} %param.11), kind=kOutput, calls=%fused_computation.7 | convolution fusion | flops 4294967296 | bytes 36700164 | tf_op jit(solution)/shard_map/dot_general | solution.py:19
  86.8 2.9 %fusion.53 = f32[128,512]{1,0:T(8,128)S(1)} fusion(bf16[128,4096]{1,0:T(8,128)(2,1)S(1)} %collective-permute-done.1, bf16[4096,512]{1,0:T(8,128)(2,1)} %param.12), kind=kOutput, calls=%fused_computation.151 | convolution fusion | flops 536870912 | bytes 5505024 | tf_op jit(solution)/shard_map/dot_general | solution.py:19
  92.4 3.0 %collective-permute-done.2 = bf16[128,4096]{1,0:T(8,128)(2,1)S(1)} collective-permute-done((bf16[128,4096]{1,0:T(8,128)(2,1)S(1)}, bf16[128,4096]{1,0:T(8,128)(2,1)S(1)}, u32[]{:S(2)}, u32[]{:S(2)}) %collective-permute-start.2) | collective-permute-done | bytes 1048608 | tf_op jit(solution)/shard_map/ppermute | solution.py:119
  95.4 14.2 %fusion.2 = f32[4,128,4096]{2,1,0:T(8,128)} fusion(f32[4,128,4096]{2,1,0:T(8,128)} %fusion.3, s32[]{:T(128)S(6)} %select_n.277, bf16[128,4096]{1,0:T(8,128)(2,1)S(1)} %collective-permute-done.2, bf16[4096,4096]{1,0:T(8,128)(2,1)} %param.11), kind=kOutput, calls=%fused_computation.5 | convolution fusion | flops 4294967296 | bytes 36700164 | tf_op jit(solution)/shard_map/dot_general | solution.py:19
  112.2 3.1 %fusion.56 = f32[128,512]{1,0:T(8,128)S(1)} fusion(bf16[128,4096]{1,0:T(8,128)(2,1)S(1)} %collective-permute-done.2, bf16[4096,512]{1,0:T(8,128)(2,1)} %param.12), kind=kOutput, calls=%fused_computation.154 | convolution fusion | flops 536870912 | bytes 5505024 | tf_op jit(solution)/shard_map/dot_general | solution.py:19
  117.7 2.8 %all_gather.20 = bf16[512,512]{1,0:T(8,128)(2,1)S(1)} all-gather(bf16[256,512]{1,0:T(8,128)(2,1)S(1)} %copy-done.10), channel_id=1, replica_groups=mesh['groups'=2,'tensor'=4,'seq'=2,'load'=2] {'load'}, dimensions={0}, use_global_device_ids=true | all-gather | bytes 786432 | tf_op jit(solution)/shard_map/all_gather | solution.py:110
  124.3 8.3 %collective-permute-done.4 = f32[128,576]{1,0:T(8,128)S(1)} collective-permute-done((f32[128,576]{1,0:T(8,128)S(1)}, f32[128,576]{1,0:T(8,128)S(1)}, u32[]{:S(2)}, u32[]{:S(2)}) %collective-permute-start.4) | collective-permute-done | bytes 294944 | tf_op jit(solution)/shard_map/ppermute | solution.py:85
  132.9 13.2 %all-gather = bf16[128,256]{0,1:T(8,128)(2,1)S(1)} all-gather(bf16[128,64]{0,1:T(8,128)(2,1)S(1)} %copy.81), channel_id=2, replica_groups=mesh['groups'=2,'tensor'=4,'seq'=2,'load'=2] {'tensor'}, dimensions={1}, use_global_device_ids=true | all-gather | bytes 81920 | tf_op jit(solution)/shard_map/all_gather | solution.py:174
  147.1 14.7 %all_gather.21 = bf16[128,2048]{1,0:T(8,128)(2,1)S(1)} all-gather(bf16[128,512]{1,0:T(8,128)(2,1)S(1)} %fusion.24), channel_id=1, replica_groups=mesh['groups'=2,'tensor'=4,'seq'=2,'load'=2] {'tensor'}, dimensions={1}, use_global_device_ids=true | all-gather | bytes 655360 | tf_op jit(solution)/shard_map/all_gather | solution.py:188
  162.4 11.0 %all_gather.22 = bf16[512,4,128]{2,0,1:T(8,128)(2,1)} all-gather(bf16[128,4,128]{2,0,1:T(8,128)(2,1)S(1)} %pad_maximum_fusion), channel_id=1, replica_groups=mesh['groups'=2,'tensor'=4,'seq'=2,'load'=2] {'seq','load'}, dimensions={0}, use_global_device_ids=true | all-gather | bytes 655360 | tf_op jit(solution)/shard_map/all_gather | solution.py:201
  173.3 2.9 %fusion.59 = f32[128,4096]{1,0:T(8,128)S(1)} fusion(bf16[128,512]{0,1:T(8,128)(2,1)S(1)} %bitcast.148, bf16[512,4096]{1,0:T(8,128)(2,1)} %all-gather.3.cloned.1.call-done), kind=kOutput, calls=%fused_computation.157 | convolution fusion | flops 536870912 | bytes 6422528 | tf_op jit(solution)/shard_map/dot_general | solution.py:19
  176.3 7.8 %reduce-scatter.2.cloned.1.call-done = f32[128,4096]{1,0:T(8,128)} async-done(((f32[512,4096]{1,0:T(8,128)}), f32[128,4096]{1,0:T(8,128)}) %reduce-scatter.2.cloned.1.call-update) | async-done | bytes 2097168 | tf_op jit(solution)/shard_map/reduce_scatter | solution.py:161
  184.1 1.8 add.313
  187.0 4.3 %fusion.10 = bf16[128,4096]{1,0:T(8,128)(2,1)S(1)} fusion(f32[16,8,32,128]{3,2,1,0:T(8,128)S(1)} %bitcast.143, f32[128,4096]{1,0:T(8,128)S(1)} %add.313, f32[16,8,32,128]{3,2,1,0:T(8,128)S(1)} %bitcast.142, f32[128,1]{1,0:T(8,128)S(1)} %get-tuple-element.50, f32[128,4095]{1,0:T(8,128)S(1)} %get-tuple-element.52, f32[128,4095]{1,0:T(8,128)S(1)} %get-tuple-element.51, ...), kind=kLoop, calls=%fused_computation.15 | loop fusion | flops 3670016 | bytes 11538432 | tf_op jit(solution)/shard_map/convert_element_type | solution.py:208
  193.0 4.6 %fusion.46 = (f32[2,16,128]{2,1,0:T(8,128)S(1)}, bf16[2,16,128,512]{2,3,1,0:T(8,128)(2,1)S(1)}) fusion(f32[2,512,128,16]{2,1,3,0:T(8,128)S(1)} %fusion.20, pred[128,512]{0,1:T(8,128)(4,1)S(1)} %copy-done.12), kind=kOutput, calls=%fused_computation.144 | output fusion | flops 16777728 | bytes 12664832 | tf_op jit(solution)/shard_map/sub | solution.py:220
  (134 shorter events, 32.6 us)
Async XLA Ops:
  8.0 4.9 %copy-start = (bf16[4096,128]{1,0:T(8,128)(2,1)S(1)}, bf16[4096,128]{1,0:T(8,128)(2,1)}, u32[]{:S(2)}) copy-start(bf16[4096,128]{1,0:T(8,128)(2,1)} %param.13) | copy-start | bytes 3145732
  8.0 6.6 %copy-start.5 = (bf16[128,4096]{1,0:T(8,128)(2,1)S(1)}, bf16[128,4096]{1,0:T(8,128)(2,1)}, u32[]{:S(2)}) copy-start(bf16[128,4096]{1,0:T(8,128)(2,1)} %param.10) | copy-start | bytes 3145732
  8.0 6.6 %copy-start.2 = (bf16[4096,128]{1,0:T(8,128)(2,1)S(1)}, bf16[4096,128]{1,0:T(8,128)(2,1)}, u32[]{:S(2)}) copy-start(bf16[4096,128]{1,0:T(8,128)(2,1)} %param.14) | copy-start | bytes 3145732
  8.0 7.2 %copy-start.18 = (s32[4]{0:T(128)S(1)}, s32[4]{0:T(128)}, u32[]{:S(2)}) copy-start(s32[4]{0:T(128)} %param.17) | copy-start | bytes 52
  8.0 7.2 %copy-start.19 = (s32[4]{0:T(128)S(1)}, s32[4]{0:T(128)}, u32[]{:S(2)}) copy-start(s32[4]{0:T(128)} %param.19) | copy-start | bytes 52
  8.1 165.3 %all-gather.3.cloned.1.call-start = ((), (), s32[]{:S(2)}) async-start(), calls=%async_computation.2 | async-start | bytes 6291456 | tf_op jit(solution)/shard_map/all_gather | solution.py:109
  8.1 28.6 %collective-permute-start = (bf16[128,4096]{1,0:T(8,128)(2,1)}, bf16[128,4096]{1,0:T(8,128)(2,1)}, u32[]{:S(2)}, u32[]{:S(2)}) collective-permute-start(bf16[128,4096]{1,0:T(8,128)(2,1)} %param.10), channel_id=1, source_target_pairs={{0,4},{4,8},{8,12},{12,0},{1,5},{5,9},{9,13},{13,1},{2,6},{6,10},{... | collective-permute-start | bytes 3145736 | tf_op jit(solution)/shard_map/ppermute | solution.py:119
  11.2 172.9 %reduce-scatter.2.cloned.1.call-start = ((), (), s32[]{:S(2)}) async-start(), calls=%async_computation.1 | async-start | bytes 10485760 | tf_op jit(solution)/shard_map/reduce_scatter | solution.py:161
  19.3 20.9 %copy-start.1 = (bf16[4096,512]{1,0:T(8,128)(2,1)S(1)}, bf16[4096,512]{1,0:T(8,128)(2,1)}, u32[]{:S(2)}) copy-start(bf16[4096,512]{1,0:T(8,128)(2,1)} %param.12) | copy-start | bytes 12582916
  40.2 5.7 %copy-start.6 = (bf16[128,4096]{1,0:T(8,128)(2,1)S(1)}, bf16[128,4096]{1,0:T(8,128)(2,1)}, u32[]{:S(2)}) copy-start(bf16[128,4096]{1,0:T(8,128)(2,1)} %param.10) | copy-start | bytes 3145732
  43.0 26.4 %collective-permute-start.1 = (bf16[128,4096]{1,0:T(8,128)(2,1)}, bf16[128,4096]{1,0:T(8,128)(2,1)S(1)}, u32[]{:S(2)}, u32[]{:S(2)}) collective-permute-start(bf16[128,4096]{1,0:T(8,128)(2,1)} %collective-permute-done), channel_id=1, source_target_pairs={{0,4},{4,8},{8,12},{12,0},{1,5},{5,9},{9,13},{13,1},{2,6},{6,10},{... | collective-permute-start | bytes 3145736 | tf_op jit(solution)/shard_map/ppermute | solution.py:119
  65.5 1.5 copy-start.8
  69.3 16.0 %copy-start.3 = (bf16[4096,128]{1,0:T(8,128)(2,1)S(1)}, bf16[4096,128]{1,0:T(8,128)(2,1)}, u32[]{:S(2)}) copy-start(bf16[4096,128]{1,0:T(8,128)(2,1)} %param.14) | copy-start | bytes 3145732
  69.4 26.1 %collective-permute-start.2 = (bf16[128,4096]{1,0:T(8,128)(2,1)S(1)}, bf16[128,4096]{1,0:T(8,128)(2,1)S(1)}, u32[]{:S(2)}, u32[]{:S(2)}) collective-permute-start(bf16[128,4096]{1,0:T(8,128)(2,1)S(1)} %collective-permute-done.1), channel_id=1, source_target_pairs={{0,4},{4,8},{8,12},{12,0},{1,5},{5,9},{9,13},{13,1},{2,6},{6,10},{... | collective-permute-start | bytes 3145736 | tf_op jit(solution)/shard_map/ppermute | solution.py:119
  86.8 2.9 %copy-start.11 = (f32[128,32]{1,0:T(8,128)S(1)}, f32[128,32]{1,0:T(8,128)}, u32[]{:S(2)}) copy-start(f32[128,32]{1,0:T(8,128)} %copy.74) | copy-start | bytes 49156
  109.7 1.7 copy-start.4
  112.2 5.5 %copy-start.10 = (bf16[256,512]{1,0:T(8,128)(2,1)S(1)}, bf16[256,512]{1,0:T(8,128)(2,1)}, u32[]{:S(2)}) copy-start(bf16[256,512]{1,0:T(8,128)(2,1)} %param.16) | copy-start | bytes 786436
  116.3 29.9 %copy-start.13 = (pred[128,4]{0,1:T(4,128)(4,1)S(1)}, pred[128,4]{0,1:T(4,128)(4,1)}, u32[]{:S(2)}) copy-start(pred[128,4]{0,1:T(4,128)(4,1)} %get-tuple-element.75) | copy-start | bytes 1540
  117.5 3.7 %collective-permute-start.3 = (f32[2,128,576]{1,2,0:T(8,128)S(1)}, f32[2,128,576]{1,2,0:T(8,128)S(1)}, u32[]{:S(2)}, u32[]{:S(2)}) collective-permute-start(f32[2,128,576]{1,2,0:T(8,128)S(1)} %dynamic-slice_bitcast_fusion), channel_id=1, source_target_pairs={{0,1},{1,0},{2,3},{3,2},{4,5},{5,4},{6,7},{7,6},{8,9},{9,8},{10,11... | collective-permute-start | bytes 1769480 | tf_op jit(solution)/shard_map/ppermute | solution.py:85
  122.4 24.5 %copy-start.16 = (pred[512]{0:T(512)(128)(4,1)S(1)}, pred[512]{0:T(512)(128)(4,1)}, u32[]{:S(2)}) copy-start(pred[512]{0:T(512)(128)(4,1)} %get-tuple-element.79) | copy-start | bytes 1540
  122.4 24.5 %copy-start.17 = (pred[512]{0:T(512)(128)(4,1)S(1)}, pred[512]{0:T(512)(128)(4,1)}, u32[]{:S(2)}) copy-start(pred[512]{0:T(512)(128)(4,1)} %get-tuple-element.80) | copy-start | bytes 1540
  122.7 9.9 %collective-permute-start.4 = (f32[128,576]{1,0:T(8,128)S(1)}, f32[128,576]{1,0:T(8,128)S(1)}, u32[]{:S(2)}, u32[]{:S(2)}) collective-permute-start(f32[128,576]{1,0:T(8,128)S(1)} %bitcast.150), channel_id=1, source_target_pairs={{0,2},{2,0},{1,3},{3,1},{4,6},{6,4},{5,7},{7,5},{8,10},{10,8},{9,1... | collective-permute-start | bytes 884744 | tf_op jit(solution)/shard_map/ppermute | solution.py:85
  147.1 29.1 %copy-start.9 = (bf16[128,512]{1,0:T(8,128)(2,1)}, bf16[128,512]{1,0:T(8,128)(2,1)S(1)}, u32[]{:S(2)}) copy-start(bf16[128,512]{1,0:T(8,128)(2,1)S(1)} %fusion.24) | copy-start | bytes 393220
  187.0 4.6 %copy-start.7 = (bf16[512,4,128]{2,0,1:T(8,128)(2,1)S(1)}, bf16[512,4,128]{2,0,1:T(8,128)(2,1)}, u32[]{:S(2)}) copy-start(bf16[512,4,128]{2,0,1:T(8,128)(2,1)} %all_gather.22) | copy-start | bytes 1572868
  (3 other events, 2.6 us)
Sparse Core Ops, SparseCore 0:
  11.3 15.5 all-gather.2
Sparse Core Ops, SparseCore 1:
  109.8 74.3 reduce-scatter.1

commit v10 on v8

--- a/solution.py
+++ b/solution.py
@@ -113,6 +113,15 @@
     small_cols = keyval_cols + 2 * rank_share
     small_terms = jnp.zeros((ring, chunk, small_cols), jnp.float32)
     query_terms = jnp.zeros((ring, chunk, query_cols), jnp.float32)
+    seq_count = lax.axis_size("seq")
+    load_count = lax.axis_size("load")
+    rows_per_out = block_rows // chunk
+
+    def query_slot(owner):
+        out_block = owner // rows_per_out
+        target = (out_block % load_count) * seq_count + out_block // load_count
+        return target * rows_per_out + owner % rows_per_out
+
     shift = [(i, (i + 1) % ring) for i in range(ring)]
     held = tokens
     for step in range(ring):
@@ -134,14 +143,14 @@
         elif step == 1 and ring > 2:
             pair = product(jnp.concatenate([first_block, held], axis=0), weight_query)
             query_terms = lax.dynamic_update_slice_in_dim(
-                query_terms, pair[:chunk][None], first_owner, 0
+                query_terms, pair[:chunk][None], query_slot(first_owner), 0
             )
             query_terms = lax.dynamic_update_slice_in_dim(
-                query_terms, pair[chunk:][None], owner, 0
+                query_terms, pair[chunk:][None], query_slot(owner), 0
             )
         else:
             query_terms = lax.dynamic_update_slice_in_dim(
-                query_terms, product(held, weight_query)[None], owner, 0
+                query_terms, product(held, weight_query)[None], query_slot(owner), 0
             )
         if following is not None:
             if step == 0 and ring > 2:
@@ -153,13 +162,11 @@
                     (following, small_terms, query_terms)
                 )
         held = following
-    seq_count = lax.axis_size("seq")
-    load_count = lax.axis_size("load")
     by_core = small_terms.reshape(seq_count, load_count, block_rows, -1)
     per_core = ring_reduce_scatter(jnp.moveaxis(by_core, 1, 0), "load")
     small_summed = ring_reduce_scatter(per_core, "seq")
     query_summed = lax.psum_scatter(
-        query_terms.reshape(ring * chunk, -1), ("seq", "load"), scatter_dimension=0, tiled=True
+        query_terms.reshape(ring * chunk, -1), ("load", "seq"), scatter_dimension=0, tiled=True
     )
     token_ids = block_index * block_rows + jnp.arange(block_rows, dtype=jnp.int32)
     own_rank, own_first, slot_hot = tenant_table(

time: 208 us -> 208 us (level)
  no operation moved by 1% of the time
where the time goes in v10:
time: 208 us; the launch traced here: 207 us
  matrix products  68.7 us (33%)
  blocking collectives  41.9 us (20%)
  waiting for transfers between devices  34 us (16%)
  local copies, waits for them, and re-layouts  21.7 us (10%)
  other arithmetic  18.9 us (9%)
  between operations  16.4 us (8%)
  starting transfers between devices  5.68 us (3%)
    dot_general x17, matrix products, product(): return jnp.dot(left, right, preferred_element_type=jnp.float32)  66.7 us
    ppermute x3, waiting for transfers between devices, shards(): following = lax.ppermute(held, 'tensor', shift) if step < ring - 1 else None  18.6 us
    all_gather x1, blocking collectives, shards(): kv_all = lax.all_gather(kv_local, 'tensor', axis=1, tiled=True)  14.7 us
    all_gather x1, blocking collectives, shards(): lax.all_gather(jnp.concatenate([low_query, low_keyval], axis=1), 'tensor'...  13.1 us
    all_gather x1, blocking collectives, shards(): lax.all_gather(jnp.concatenate([key_heads, value_heads], axis=1), ('seq',...  11 us
    ppermute x2, waiting for transfers between devices, ring_reduce_scatter(): total = lax.ppermute(total, axis, shift) + pick(step)  8.05 us
    reduce_scatter x1, waiting for transfers between devices, shards(): lax.psum_scatter(query_terms.reshape(ring * chunk, -1), ('load', 'seq'),...  7.32 us
    sub x1, other arithmetic, shards(): exp_scores = jnp.where(visible, jnp.exp(scores - row_top[..., None]), 0.0)  4.59 us
  transfers between devices with their start and end apart: 7, of which 5 were waited for; matrix products, arithmetic and copies ran while one was open for 45% of the time, Pallas kernels for 0%

profile of v10, /device:TPU:0, one launch (start us, length us, event | category | flops | bytes accessed | tf_op | source)
XLA Modules:
  0.0 207.1 jit_solution(12137502974814978089)
XLA Ops:
  8.1 3.1 %collective-permute-start = (bf16[128,4096]{1,0:T(8,128)(2,1)}, bf16[128,4096]{1,0:T(8,128)(2,1)}, u32[]{:S(2)}, u32[]{:S(2)}) collective-permute-start(bf16[128,4096]{1,0:T(8,128)(2,1)} %param.10), channel_id=1, source_target_pairs={{0,4},{4,8},{8,12},{12,0},{1,5},{5,9},{9,13},{13,1},{2,6},{6,10},{... | collective-permute-start | bytes 3145736 | tf_op jit(solution)/shard_map/ppermute | solution.py:128
  12.9 1.7 fusion.49
  16.1 2.9 %fusion.48 = f32[128,512]{1,0:T(8,128)S(1)} fusion(bf16[128,4096]{1,0:T(8,128)(2,1)S(1)} %copy-done.5, bf16[4096,512]{1,0:T(8,128)(2,1)} %param.12), kind=kOutput, calls=%fused_computation.146 | convolution fusion | flops 536870912 | bytes 5505024 | tf_op jit(solution)/shard_map/dot_general | solution.py:19
  21.2 15.5 %collective-permute-done = bf16[128,4096]{1,0:T(8,128)(2,1)} collective-permute-done((bf16[128,4096]{1,0:T(8,128)(2,1)}, bf16[128,4096]{1,0:T(8,128)(2,1)}, u32[]{:S(2)}, u32[]{:S(2)}) %collective-permute-start) | collective-permute-done | bytes 1048608 | tf_op jit(solution)/shard_map/ppermute | solution.py:128
  36.7 1.7 fusion.52
  38.4 1.7 fusion.53
  40.2 2.8 %fusion.51 = f32[128,512]{1,0:T(8,128)} fusion(bf16[128,4096]{1,0:T(8,128)(2,1)} %collective-permute-done, bf16[4096,512]{1,0:T(8,128)(2,1)S(1)} %copy-done.1), kind=kOutput, calls=%fused_computation.149 | convolution fusion | flops 536870912 | bytes 5505024 | tf_op jit(solution)/shard_map/dot_general | solution.py:19
  45.9 15.3 %fusion.13 = f32[256,4096]{1,0:T(8,128)S(1)} fusion(bf16[4096,4096]{1,0:T(8,128)(2,1)} %param.11, bf16[128,4096]{1,0:T(8,128)(2,1)} %collective-permute-done, bf16[128,4096]{1,0:T(8,128)(2,1)S(1)} %copy-done.6), kind=kOutput, calls=%fused_computation.21 | convolution fusion | flops 8594128896 | bytes 39845888 | tf_op jit(solution)/shard_map/dot_general | solution.py:19
  61.2 4.3 %broadcast_in_dim.276 = f32[4,128,4096]{2,1,0:T(8,128)} broadcast(f32[]{:T(128)} %constant.291.clone.1), dimensions={} | broadcast | bytes 8388612 | tf_op jit(solution)/shard_map/broadcast_in_dim | solution.py:115
  70.6 14.2 %fusion.3 = f32[4,128,4096]{2,1,0:T(8,128)} fusion(f32[4,128,4096]{2,1,0:T(8,128)} %fusion.11, s32[]{:T(128)S(6)} %select_n.331, bf16[128,4096]{1,0:T(8,128)(2,1)S(1)} %collective-permute-done.1, bf16[4096,4096]{1,0:T(8,128)(2,1)} %param.11), kind=kOutput, calls=%fused_computation.7 | convolution fusion | flops 4294967296 | bytes 36700164 | tf_op jit(solution)/shard_map/dot_general | solution.py:19
  86.8 2.9 %fusion.54 = f32[128,512]{1,0:T(8,128)S(1)} fusion(bf16[128,4096]{1,0:T(8,128)(2,1)S(1)} %collective-permute-done.1, bf16[4096,512]{1,0:T(8,128)(2,1)} %param.12), kind=kOutput, calls=%fused_computation.152 | convolution fusion | flops 536870912 | bytes 5505024 | tf_op jit(solution)/shard_map/dot_general | solution.py:19
  92.4 3.0 %collective-permute-done.2 = bf16[128,4096]{1,0:T(8,128)(2,1)S(1)} collective-permute-done((bf16[128,4096]{1,0:T(8,128)(2,1)S(1)}, bf16[128,4096]{1,0:T(8,128)(2,1)S(1)}, u32[]{:S(2)}, u32[]{:S(2)}) %collective-permute-start.2) | collective-permute-done | bytes 1048608 | tf_op jit(solution)/shard_map/ppermute | solution.py:128
  95.4 14.2 %fusion.2 = f32[4,128,4096]{2,1,0:T(8,128)} fusion(f32[4,128,4096]{2,1,0:T(8,128)} %fusion.3, s32[]{:T(128)S(6)} %select_n.364, bf16[128,4096]{1,0:T(8,128)(2,1)S(1)} %collective-permute-done.2, bf16[4096,4096]{1,0:T(8,128)(2,1)} %param.11), kind=kOutput, calls=%fused_computation.5 | convolution fusion | flops 4294967296 | bytes 36700164 | tf_op jit(solution)/shard_map/dot_general | solution.py:19
  112.3 3.2 %fusion.57 = f32[128,512]{1,0:T(8,128)S(1)} fusion(bf16[128,4096]{1,0:T(8,128)(2,1)S(1)} %collective-permute-done.2, bf16[4096,512]{1,0:T(8,128)(2,1)} %param.12), kind=kOutput, calls=%fused_computation.155 | convolution fusion | flops 536870912 | bytes 5505024 | tf_op jit(solution)/shard_map/dot_general | solution.py:19
  117.9 3.1 %all_gather.20 = bf16[512,512]{1,0:T(8,128)(2,1)S(1)} all-gather(bf16[256,512]{1,0:T(8,128)(2,1)S(1)} %copy-done.10), channel_id=1, replica_groups=mesh['groups'=2,'tensor'=4,'seq'=2,'load'=2] {'load'}, dimensions={0}, use_global_device_ids=true | all-gather | bytes 786432 | tf_op jit(solution)/shard_map/all_gather | solution.py:110
  125.2 8.0 %collective-permute-done.4 = f32[128,576]{1,0:T(8,128)S(1)} collective-permute-done((f32[128,576]{1,0:T(8,128)S(1)}, f32[128,576]{1,0:T(8,128)S(1)}, u32[]{:S(2)}, u32[]{:S(2)}) %collective-permute-start.4) | collective-permute-done | bytes 294944 | tf_op jit(solution)/shard_map/ppermute | solution.py:85
  133.5 13.1 %all-gather = bf16[128,256]{0,1:T(8,128)(2,1)S(1)} all-gather(bf16[128,64]{0,1:T(8,128)(2,1)S(1)} %copy.81), channel_id=2, replica_groups=mesh['groups'=2,'tensor'=4,'seq'=2,'load'=2] {'tensor'}, dimensions={1}, use_global_device_ids=true | all-gather | bytes 81920 | tf_op jit(solution)/shard_map/all_gather | solution.py:181
  147.6 14.7 %all_gather.21 = bf16[128,2048]{1,0:T(8,128)(2,1)S(1)} all-gather(bf16[128,512]{1,0:T(8,128)(2,1)S(1)} %fusion.25), channel_id=1, replica_groups=mesh['groups'=2,'tensor'=4,'seq'=2,'load'=2] {'tensor'}, dimensions={1}, use_global_device_ids=true | all-gather | bytes 655360 | tf_op jit(solution)/shard_map/all_gather | solution.py:195
  162.9 11.0 %all_gather.22 = bf16[512,4,128]{2,0,1:T(8,128)(2,1)} all-gather(bf16[128,4,128]{2,0,1:T(8,128)(2,1)S(1)} %pad_maximum_fusion), channel_id=1, replica_groups=mesh['groups'=2,'tensor'=4,'seq'=2,'load'=2] {'seq','load'}, dimensions={0}, use_global_device_ids=true | all-gather | bytes 655360 | tf_op jit(solution)/shard_map/all_gather | solution.py:208
  173.9 2.9 %fusion.60 = f32[128,4096]{1,0:T(8,128)S(1)} fusion(bf16[128,512]{0,1:T(8,128)(2,1)S(1)} %bitcast.152, bf16[512,4096]{1,0:T(8,128)(2,1)} %all-gather.3.cloned.1.call-done), kind=kOutput, calls=%fused_computation.158 | convolution fusion | flops 536870912 | bytes 6422528 | tf_op jit(solution)/shard_map/dot_general | solution.py:19
  176.8 7.3 %reduce-scatter.2.cloned.1.call-done = f32[128,4096]{1,0:T(8,128)} async-done(((f32[512,4096]{1,0:T(8,128)}), f32[128,4096]{1,0:T(8,128)}) %reduce-scatter.2.cloned.1.call-update) | async-done | bytes 2097168 | tf_op jit(solution)/shard_map/reduce_scatter | solution.py:168
  184.1 1.8 add.373
  187.0 4.4 %fusion.22 = bf16[16,8,32,128]{3,1,2,0:T(8,128)(2,1)S(1)} fusion(f32[16,8,32,128]{3,2,1,0:T(8,128)S(1)} %bitcast.148, f32[128,4095]{1,0:T(8,128)S(1)} %get-tuple-element.50, f32[128,1]{1,0:T(8,128)S(1)} %get-tuple-element.52, f32[128,1]{1,0:T(8,128)S(1)} %get-tuple-element.51, f32[128,4095]{1,0:T(8,128)S(1)} %get-tuple-element.49, f32[128,4096]{1,0:T(8,128)S(1)} %add.373, ...), kind=kLoop, calls=%fused_computation.30 | loop fusion | flops 3670016 | bytes 11538432
  193.0 4.6 %fusion.47 = (f32[2,16,128]{2,1,0:T(8,128)S(1)}, bf16[2,16,128,512]{2,3,1,0:T(8,128)(2,1)S(1)}) fusion(f32[2,512,128,16]{2,1,3,0:T(8,128)S(1)} %fusion.20, pred[128,512]{0,1:T(8,128)(4,1)S(1)} %copy-done.12), kind=kOutput, calls=%fused_computation.145 | output fusion | flops 16777728 | bytes 12664832 | tf_op jit(solution)/shard_map/sub | solution.py:225
  (134 shorter events, 33.1 us)
Async XLA Ops:
  8.0 4.9 %copy-start = (bf16[4096,128]{1,0:T(8,128)(2,1)S(1)}, bf16[4096,128]{1,0:T(8,128)(2,1)}, u32[]{:S(2)}) copy-start(bf16[4096,128]{1,0:T(8,128)(2,1)} %param.13) | copy-start | bytes 3145732
  8.0 6.6 %copy-start.5 = (bf16[128,4096]{1,0:T(8,128)(2,1)S(1)}, bf16[128,4096]{1,0:T(8,128)(2,1)}, u32[]{:S(2)}) copy-start(bf16[128,4096]{1,0:T(8,128)(2,1)} %param.10) | copy-start | bytes 3145732
  8.0 6.6 %copy-start.2 = (bf16[4096,128]{1,0:T(8,128)(2,1)S(1)}, bf16[4096,128]{1,0:T(8,128)(2,1)}, u32[]{:S(2)}) copy-start(bf16[4096,128]{1,0:T(8,128)(2,1)} %param.14) | copy-start | bytes 3145732
  8.0 7.2 %copy-start.18 = (s32[4]{0:T(128)S(1)}, s32[4]{0:T(128)}, u32[]{:S(2)}) copy-start(s32[4]{0:T(128)} %param.17) | copy-start | bytes 52
  8.0 7.2 %copy-start.19 = (s32[4]{0:T(128)S(1)}, s32[4]{0:T(128)}, u32[]{:S(2)}) copy-start(s32[4]{0:T(128)} %param.19) | copy-start | bytes 52
  8.1 165.8 %all-gather.3.cloned.1.call-start = ((), (), s32[]{:S(2)}) async-start(), calls=%async_computation.2 | async-start | bytes 6291456 | tf_op jit(solution)/shard_map/all_gather | solution.py:109
  8.1 28.6 %collective-permute-start = (bf16[128,4096]{1,0:T(8,128)(2,1)}, bf16[128,4096]{1,0:T(8,128)(2,1)}, u32[]{:S(2)}, u32[]{:S(2)}) collective-permute-start(bf16[128,4096]{1,0:T(8,128)(2,1)} %param.10), channel_id=1, source_target_pairs={{0,4},{4,8},{8,12},{12,0},{1,5},{5,9},{9,13},{13,1},{2,6},{6,10},{... | collective-permute-start | bytes 3145736 | tf_op jit(solution)/shard_map/ppermute | solution.py:128
  11.2 172.9 %reduce-scatter.2.cloned.1.call-start = ((), (), s32[]{:S(2)}) async-start(), calls=%async_computation.1 | async-start | bytes 10485760 | tf_op jit(solution)/shard_map/reduce_scatter | solution.py:168
  19.3 20.8 %copy-start.1 = (bf16[4096,512]{1,0:T(8,128)(2,1)S(1)}, bf16[4096,512]{1,0:T(8,128)(2,1)}, u32[]{:S(2)}) copy-start(bf16[4096,512]{1,0:T(8,128)(2,1)} %param.12) | copy-start | bytes 12582916
  40.2 5.7 %copy-start.6 = (bf16[128,4096]{1,0:T(8,128)(2,1)S(1)}, bf16[128,4096]{1,0:T(8,128)(2,1)}, u32[]{:S(2)}) copy-start(bf16[128,4096]{1,0:T(8,128)(2,1)} %param.10) | copy-start | bytes 3145732
  43.0 26.4 %collective-permute-start.1 = (bf16[128,4096]{1,0:T(8,128)(2,1)}, bf16[128,4096]{1,0:T(8,128)(2,1)S(1)}, u32[]{:S(2)}, u32[]{:S(2)}) collective-permute-start(bf16[128,4096]{1,0:T(8,128)(2,1)} %collective-permute-done), channel_id=1, source_target_pairs={{0,4},{4,8},{8,12},{12,0},{1,5},{5,9},{9,13},{13,1},{2,6},{6,10},{... | collective-permute-start | bytes 3145736 | tf_op jit(solution)/shard_map/ppermute | solution.py:128
  65.5 1.5 copy-start.8
  69.3 16.0 %copy-start.3 = (bf16[4096,128]{1,0:T(8,128)(2,1)S(1)}, bf16[4096,128]{1,0:T(8,128)(2,1)}, u32[]{:S(2)}) copy-start(bf16[4096,128]{1,0:T(8,128)(2,1)} %param.14) | copy-start | bytes 3145732
  69.4 26.1 %collective-permute-start.2 = (bf16[128,4096]{1,0:T(8,128)(2,1)S(1)}, bf16[128,4096]{1,0:T(8,128)(2,1)S(1)}, u32[]{:S(2)}, u32[]{:S(2)}) collective-permute-start(bf16[128,4096]{1,0:T(8,128)(2,1)S(1)} %collective-permute-done.1), channel_id=1, source_target_pairs={{0,4},{4,8},{8,12},{12,0},{1,5},{5,9},{9,13},{13,1},{2,6},{6,10},{... | collective-permute-start | bytes 3145736 | tf_op jit(solution)/shard_map/ppermute | solution.py:128
  86.8 2.9 %copy-start.11 = (f32[128,32]{1,0:T(8,128)S(1)}, f32[128,32]{1,0:T(8,128)}, u32[]{:S(2)}) copy-start(f32[128,32]{1,0:T(8,128)} %copy.74) | copy-start | bytes 49156
  109.7 1.7 copy-start.4
  112.3 5.6 %copy-start.10 = (bf16[256,512]{1,0:T(8,128)(2,1)S(1)}, bf16[256,512]{1,0:T(8,128)(2,1)}, u32[]{:S(2)}) copy-start(bf16[256,512]{1,0:T(8,128)(2,1)} %param.16) | copy-start | bytes 786436
  116.4 30.3 %copy-start.13 = (pred[128,4]{0,1:T(4,128)(4,1)S(1)}, pred[128,4]{0,1:T(4,128)(4,1)}, u32[]{:S(2)}) copy-start(pred[128,4]{0,1:T(4,128)(4,1)} %get-tuple-element.75) | copy-start | bytes 1540
  117.7 4.0 %collective-permute-start.3 = (f32[2,128,576]{1,2,0:T(8,128)S(1)}, f32[2,128,576]{1,2,0:T(8,128)S(1)}, u32[]{:S(2)}, u32[]{:S(2)}) collective-permute-start(f32[2,128,576]{1,2,0:T(8,128)S(1)} %dynamic-slice_bitcast_fusion), channel_id=1, source_target_pairs={{0,1},{1,0},{2,3},{3,2},{4,5},{5,4},{6,7},{7,6},{8,9},{9,8},{10,11... | collective-permute-start | bytes 1769480 | tf_op jit(solution)/shard_map/ppermute | solution.py:85
  123.0 24.5 %copy-start.16 = (pred[512]{0:T(512)(128)(4,1)S(1)}, pred[512]{0:T(512)(128)(4,1)}, u32[]{:S(2)}) copy-start(pred[512]{0:T(512)(128)(4,1)} %get-tuple-element.79) | copy-start | bytes 1540
  123.0 24.5 %copy-start.17 = (pred[512]{0:T(512)(128)(4,1)S(1)}, pred[512]{0:T(512)(128)(4,1)}, u32[]{:S(2)}) copy-start(pred[512]{0:T(512)(128)(4,1)} %get-tuple-element.80) | copy-start | bytes 1540
  123.2 10.0 %collective-permute-start.4 = (f32[128,576]{1,0:T(8,128)S(1)}, f32[128,576]{1,0:T(8,128)S(1)}, u32[]{:S(2)}, u32[]{:S(2)}) collective-permute-start(f32[128,576]{1,0:T(8,128)S(1)} %bitcast.154), channel_id=1, source_target_pairs={{0,2},{2,0},{1,3},{3,1},{4,6},{6,4},{5,7},{7,5},{8,10},{10,8},{9,1... | collective-permute-start | bytes 884744 | tf_op jit(solution)/shard_map/ppermute | solution.py:85
  147.6 29.2 %copy-start.9 = (bf16[128,512]{1,0:T(8,128)(2,1)}, bf16[128,512]{1,0:T(8,128)(2,1)S(1)}, u32[]{:S(2)}) copy-start(bf16[128,512]{1,0:T(8,128)(2,1)S(1)} %fusion.25) | copy-start | bytes 393220
  187.0 4.6 %copy-start.7 = (bf16[512,4,128]{2,0,1:T(8,128)(2,1)S(1)}, bf16[512,4,128]{2,0,1:T(8,128)(2,1)}, u32[]{:S(2)}) copy-start(bf16[512,4,128]{2,0,1:T(8,128)(2,1)} %all_gather.22) | copy-start | bytes 1572868
  (3 other events, 2.6 us)
Sparse Core Ops, SparseCore 0:
  11.3 15.5 all-gather.2
Sparse Core Ops, SparseCore 1:
  109.8 74.3 reduce-scatter.1

commit v11 on v8

--- a/solution.py
+++ b/solution.py
@@ -68,6 +68,20 @@
         slot_hot[:, None, :], low_values[:, :, None], jnp.zeros((), low_values.dtype)
     )
     return wide_rows.reshape(low_values.shape[0], -1)
+
+
+def ring_gather(piece, axis):
+    count = lax.axis_size(axis)
+    me = lax.axis_index(axis)
+    if count == 1:
+        return piece
+    shift = [(i, (i + 1) % count) for i in range(count)]
+    pieces = [piece]
+    for _ in range(1, count):
+        pieces.append(lax.ppermute(pieces[-1], axis, shift))
+    stacked = jnp.stack(pieces)
+    order = (me - jnp.arange(count, dtype=jnp.int32)) % count
+    return jnp.take(stacked, order, axis=0).reshape((count * piece.shape[0],) + piece.shape[1:])
 
 
 def ring_reduce_scatter(blocks, axis):
@@ -106,10 +120,12 @@
     keyval_cols = weight_keyval.shape[1]
     rank_share = down_query.shape[1] // TENANTS
     block_rows = tokens.shape[0] * tensor_count // block_count
-    up_query_all = lax.all_gather(up_query, "load", axis=0, tiled=True)
-    up_keyval_all = lax.all_gather(up_keyval, "load", axis=0, tiled=True)
+    up_query_all = ring_gather(up_query, "load")
+    up_keyval_all = ring_gather(up_keyval, "load")
     ring = tensor_count
     chunk = tokens.shape[0]
+    seq_count = lax.axis_size("seq")
+    load_count = lax.axis_size("load")
     small_cols = keyval_cols + 2 * rank_share
     small_terms = jnp.zeros((ring, chunk, small_cols), jnp.float32)
     query_terms = jnp.zeros((ring, chunk, query_cols), jnp.float32)
@@ -153,13 +169,12 @@
                     (following, small_terms, query_terms)
                 )
         held = following
-    seq_count = lax.axis_size("seq")
-    load_count = lax.axis_size("load")
     by_core = small_terms.reshape(seq_count, load_count, block_rows, -1)
     per_core = ring_reduce_scatter(jnp.moveaxis(by_core, 1, 0), "load")
     small_summed = ring_reduce_scatter(per_core, "seq")
-    query_summed = lax.psum_scatter(
-        query_terms.reshape(ring * chunk, -1), ("seq", "load"), scatter_dimension=0, tiled=True
+    query_by_core = query_terms.reshape(seq_count, load_count, block_rows, -1)
+    query_summed = ring_reduce_scatter(
+        ring_reduce_scatter(jnp.moveaxis(query_by_core, 1, 0), "load"), "seq"
     )
     token_ids = block_index * block_rows + jnp.arange(block_rows, dtype=jnp.int32)
     own_rank, own_first, slot_hot = tenant_table(

time: 208 us -> 223 us (1.072)
  waiting for transfers between devices: 34.7 us -> 7.64 us
  other arithmetic: 18.7 us -> 40.7 us
  local copies, waits for them, and re-layouts: 21.7 us -> 37 us
  between operations: 16.3 us -> 1.36 us
  blocking collectives: 41.7 us -> 54.8 us
  starting transfers between devices: 5.33 us -> 10.3 us
    all_gather x1, blocking collectives: 11 us -> 26.5 us  [shards(): lax.all_gather(jnp.concatenate([key_heads, value_heads], axis=1), ('seq',...]
    ppermute x3, waiting for transfers between devices: 18.6 us -> 3.2 us  [shards(): following = lax.ppermute(held, 'tensor', shift) if step < ring - 1 else None]
    reduce_scatter x1 -> x0, waiting for transfers between devices: 7.85 us -> none  [shards(): lax.psum_scatter(query_terms.reshape(ring * chunk, -1), ('seq', 'load'),...]
    gather x0 -> x3, local copies, waits for them, and re-layouts: none -> 6.43 us  [ring_gather(): jnp.take(stacked, order, axis=0)]
    squeeze x1 -> x3, local copies, waits for them, and re-layouts: 1.24 us -> 7.27 us  [pick(): lax.dynamic_index_in_dim(blocks, (me - 1 - step) % count, 0, keepdims=False)]
    add x2 -> x3, other arithmetic: 1.21 us -> 6.26 us  [ring_reduce_scatter(): total = lax.ppermute(total, axis, shift) + pick(step)]
    another operation x1 -> x3, other arithmetic: 0.83 us -> 5.57 us  [the longest x2 4.74 us: ring_gather(): stacked = jnp.stack(pieces)]
    ppermute x2 -> x4, waiting for transfers between devices: 8.27 us -> 4.44 us  [ring_reduce_scatter(): total = lax.ppermute(total, axis, shift) + pick(step)]
  transfers between devices with their start and end apart: 7 -> 9, of which waited for: 5 -> 2; matrix products, arithmetic and copies ran while one was open for 45% -> 57% of each run, Pallas kernels for 0% -> 0%
where the time goes in v11:
time: 223 us
  matrix products  70.8 us (32%)
  blocking collectives  54.8 us (25%)
  other arithmetic  40.7 us (18%)
  local copies, waits for them, and re-layouts  37 us (17%)
  starting transfers between devices  10.3 us (5%)
  waiting for transfers between devices  7.64 us (3%)
    dot_general x17, matrix products, product(): return jnp.dot(left, right, preferred_element_type=jnp.float32)  68.7 us
    all_gather x1, blocking collectives, shards(): lax.all_gather(jnp.concatenate([key_heads, value_heads], axis=1), ('seq',...  26.5 us
    all_gather x1, blocking collectives, shards(): kv_all = lax.all_gather(kv_local, 'tensor', axis=1, tiled=True)  15.2 us
    all_gather x1, blocking collectives, shards(): lax.all_gather(jnp.concatenate([low_query, low_keyval], axis=1), 'tensor'...  13.1 us
    squeeze x3, local copies, waits for them, and re-layouts, pick(): lax.dynamic_index_in_dim(blocks, (me - 1 - step) % count, 0, keepdims=False)  7.27 us
    gather x3, local copies, waits for them, and re-layouts, ring_gather(): jnp.take(stacked, order, axis=0)  6.43 us
    add x3, other arithmetic, ring_reduce_scatter(): total = lax.ppermute(total, axis, shift) + pick(step)  6.26 us
    ppermute x3, starting transfers between devices, shards(): following = lax.ppermute(held, 'tensor', shift) if step < ring - 1 else None  6.18 us
  transfers between devices with their start and end apart: 9, of which 2 were waited for; matrix products, arithmetic and copies ran while one was open for 57% of the time, Pallas kernels for 0%

profile of v11, /device:TPU:0, one launch (start us, length us, event | category | flops | bytes accessed | tf_op | source)
XLA Modules:
  0.0 222.6 jit_solution(5136614753390865841)
XLA Ops:
  0.7 3.1 %collective-permute-start = (bf16[128,4096]{1,0:T(8,128)(2,1)}, bf16[128,4096]{1,0:T(8,128)(2,1)}, u32[]{:S(2)}, u32[]{:S(2)}) collective-permute-start(bf16[128,4096]{1,0:T(8,128)(2,1)} %param.10), channel_id=1, source_target_pairs={{0,4},{4,8},{8,12},{12,0},{1,5},{5,9},{9,13},{13,1},{2,6},{6,10},{... | collective-permute-start | bytes 3145736 | tf_op jit(solution)/shard_map/ppermute | solution.py:135
  12.5 3.6 %fusion.53 = f32[128,512]{1,0:T(8,128)} fusion(bf16[128,4096]{1,0:T(8,128)(2,1)S(1)} %copy-done.8, bf16[4096,512]{1,0:T(8,128)(2,1)} %param.12), kind=kOutput, calls=%fused_computation.174 | convolution fusion | flops 536870912 | bytes 5505024 | tf_op jit(solution)/shard_map/dot_general | solution.py:19
  21.9 2.3 %constant_dynamic-update-slice_fusion.3 = f32[4,128,576]{1,2,0:T(8,128)} fusion(f32[4,128,576]{1,2,0:T(8,128)} %broadcast_in_dim.289, f32[1,128,576]{1,2,0:T(8,128)} %copy.69, s32[]{:T(128)S(6)} %select_n.353), kind=kLoop, calls=%fused_computation.102 | loop fusion | bytes 589828 | tf_op jit(solution)/shard_map/dynamic_update_slice | solution.py:147
  33.3 2.7 %fusion.56 = f32[128,512]{1,0:T(8,128)} fusion(bf16[128,4096]{1,0:T(8,128)(2,1)} %collective-permute-done, bf16[4096,512]{1,0:T(8,128)(2,1)S(1)} %copy-done.2), kind=kOutput, calls=%fused_computation.177 | convolution fusion | flops 536870912 | bytes 5505024 | tf_op jit(solution)/shard_map/dot_general | solution.py:19
  40.5 15.3 %fusion.14 = f32[256,4096]{1,0:T(8,128)S(1)} fusion(bf16[4096,4096]{1,0:T(8,128)(2,1)} %param.11, bf16[128,4096]{1,0:T(8,128)(2,1)} %collective-permute-done, bf16[128,4096]{1,0:T(8,128)(2,1)S(1)} %copy-done.8), kind=kOutput, calls=%fused_computation.31 | convolution fusion | flops 8594128896 | bytes 39845888 | tf_op jit(solution)/shard_map/dot_general | solution.py:19
  55.8 4.3 %broadcast_in_dim.296 = f32[4,128,4096]{2,1,0:T(8,128)} broadcast(f32[]{:T(128)} %constant.250.clone.1), dimensions={} | broadcast | bytes 8388612 | tf_op jit(solution)/shard_map/broadcast_in_dim | solution.py:131
  65.4 14.2 %fusion.3 = f32[4,128,4096]{2,1,0:T(8,128)} fusion(f32[4,128,4096]{2,1,0:T(8,128)} %fusion.12, s32[]{:T(128)S(6)} %select_n.363, bf16[128,4096]{1,0:T(8,128)(2,1)S(1)} %collective-permute-done.1, bf16[4096,4096]{1,0:T(8,128)(2,1)} %param.11), kind=kOutput, calls=%fused_computation.10 | convolution fusion | flops 4294967296 | bytes 36700164 | tf_op jit(solution)/shard_map/dot_general | solution.py:19
  81.6 2.9 %fusion.59 = f32[128,512]{1,0:T(8,128)S(1)} fusion(bf16[128,4096]{1,0:T(8,128)(2,1)S(1)} %collective-permute-done.1, bf16[4096,512]{1,0:T(8,128)(2,1)} %param.12), kind=kOutput, calls=%fused_computation.180 | convolution fusion | flops 536870912 | bytes 5505024 | tf_op jit(solution)/shard_map/dot_general | solution.py:19
  87.2 3.2 %collective-permute-done.2 = bf16[128,4096]{1,0:T(8,128)(2,1)S(1)} collective-permute-done((bf16[128,4096]{1,0:T(8,128)(2,1)S(1)}, bf16[128,4096]{1,0:T(8,128)(2,1)S(1)}, u32[]{:S(2)}, u32[]{:S(2)}) %collective-permute-start.2) | collective-permute-done | bytes 1048608 | tf_op jit(solution)/shard_map/ppermute | solution.py:135
  90.4 14.2 %fusion.2 = f32[4,128,4096]{2,1,0:T(8,128)} fusion(f32[4,128,4096]{2,1,0:T(8,128)} %fusion.3, s32[]{:T(128)S(6)} %select_n.368, bf16[128,4096]{1,0:T(8,128)(2,1)S(1)} %collective-permute-done.2, bf16[4096,4096]{1,0:T(8,128)(2,1)} %param.11), kind=kOutput, calls=%fused_computation.8 | convolution fusion | flops 4294967296 | bytes 36700164 | tf_op jit(solution)/shard_map/dot_general | solution.py:19
  104.7 4.7 %dynamic-slice_bitcast_fusion = f32[2,128,4096]{2,1,0:T(8,128)} fusion(f32[2,2,128,4096]{3,2,1,0:T(8,128)} %bitcast.34, s32[]{:T(128)S(6)} %select_n.370), kind=kLoop, calls=%fused_computation.19 | loop fusion | bytes 8388612 | tf_op jit(solution)/shard_map/jit(dynamic_index_in_dim)/squeeze | solution.py:95
  110.7 3.0 %fusion.62 = f32[128,512]{1,0:T(8,128)S(1)} fusion(bf16[128,4096]{1,0:T(8,128)(2,1)S(1)} %collective-permute-done.2, bf16[4096,512]{1,0:T(8,128)(2,1)} %param.12), kind=kOutput, calls=%fused_computation.183 | convolution fusion | flops 536870912 | bytes 5505024 | tf_op jit(solution)/shard_map/dot_general | solution.py:19
  118.1 3.7 %fusion.9 = (bf16[2,256,2048]{2,1,0:T(8,128)(2,1)}, bf16[2,256,2048]{2,1,0:T(8,128)(2,1)}) fusion(bf16[1,256,4096]{2,1,0:T(8,128)(2,1)} %bitcast.169, bf16[1,256,4096]{2,1,0:T(8,128)(2,1)} %bitcast.42), kind=kLoop, calls=%fused_computation.21 | loop fusion | flops 8388608 | bytes 8388608 | tf_op jit(solution)/shard_map/stack | solution.py:82
  121.8 2.3 %gather_fusion.1 = bf16[2,256,2048]{2,1,0:T(8,128)(2,1)S(1)} fusion(bf16[2,256,2048]{2,1,0:T(8,128)(2,1)} %get-tuple-element.49, s32[1024]{0:T(1024)S(1)} %pad_clamp_fusion), kind=kCustom, calls=%fused_computation.1 | custom fusion | bytes 4194312 | tf_op jit(solution)/shard_map/jit(_take)/gather | solution.py:84
  124.1 3.6 %gather_fusion.2 = bf16[2,256,2048]{2,1,0:T(8,128)(2,1)} fusion(bf16[2,256,2048]{2,1,0:T(8,128)(2,1)} %get-tuple-element.50, s32[1024]{0:T(1024)S(1)} %pad_clamp_fusion), kind=kCustom, calls=%fused_computation.2 | custom fusion | bytes 4194312 | tf_op jit(solution)/shard_map/jit(_take)/gather | solution.py:84
  130.8 3.7 %maximum_select_fusion = bf16[2,256,4096]{2,1,0:T(8,128)(2,1)} fusion(bf16[2,256,2048]{2,1,0:T(8,128)(2,1)} %gather_fusion.2, bf16[2,256,2048]{2,1,0:T(8,128)(2,1)S(1)} %gather_fusion.1, pred[2]{0:T(512)(128)(4,1)S(1)} %compare_and_fusion), kind=kLoop, calls=%fused_computation.13 | loop fusion | flops 10485760 | bytes 8388610 | tf_op jit(solution)/shard_map/jit(_take)/select_n | solution.py:84
  134.6 4.4 %collective-permute-done.4 = f32[128,576]{1,0:T(8,128)} collective-permute-done((f32[128,576]{1,0:T(8,128)S(1)}, f32[128,576]{1,0:T(8,128)}, u32[]{:S(2)}, u32[]{:S(2)}) %collective-permute-start.4) | collective-permute-done | bytes 294944 | tf_op jit(solution)/shard_map/ppermute | solution.py:99
  140.4 13.1 %all-gather = bf16[128,256]{0,1:T(8,128)(2,1)S(1)} all-gather(bf16[128,64]{0,1:T(8,128)(2,1)S(1)} %copy.81), channel_id=2, replica_groups=mesh['groups'=2,'tensor'=4,'seq'=2,'load'=2] {'tensor'}, dimensions={1}, use_global_device_ids=true | all-gather | bytes 81920 | tf_op jit(solution)/shard_map/all_gather | solution.py:189
  153.5 4.0 %bitcast_add_fusion = f32[2,128,4096]{2,1,0:T(8,128)S(1)} fusion(f32[2,128,4096]{2,1,0:T(8,128)} %collective-permute-done.6, f32[2,2,128,4096]{3,2,1,0:T(8,128)} %bitcast.34, s32[]{:T(128)S(6)} %select_n.372), kind=kLoop, calls=%fused_computation.14 | loop fusion | flops 1048576 | bytes 12582916 | tf_op jit(solution)/shard_map/add | solution.py:99
  161.5 15.2 %all_gather.14 = bf16[128,2048]{1,0:T(8,128)(2,1)S(1)} all-gather(bf16[128,512]{1,0:T(8,128)(2,1)S(1)} %fusion.27), channel_id=1, replica_groups=mesh['groups'=2,'tensor'=4,'seq'=2,'load'=2] {'tensor'}, dimensions={1}, use_global_device_ids=true | all-gather | bytes 655360 | tf_op jit(solution)/shard_map/all_gather | solution.py:203
  177.2 3.1 %fusion.65 = f32[128,4096]{1,0:T(8,128)S(1)} fusion(bf16[128,512]{0,1:T(8,128)(2,1)S(1)} %bitcast.173, bf16[512,4096]{1,0:T(8,128)(2,1)} %bitcast.164), kind=kOutput, calls=%fused_computation.186 | convolution fusion | flops 536870912 | bytes 6422528 | tf_op jit(solution)/shard_map/dot_general | solution.py:19
  180.3 26.5 %all_gather.15 = bf16[512,4,128]{2,0,1:T(8,128)(2,1)S(1)} all-gather(bf16[128,4,128]{2,0,1:T(8,128)(2,1)S(1)} %pad_maximum_fusion.2), channel_id=1, replica_groups=mesh['groups'=2,'tensor'=4,'seq'=2,'load'=2] {'seq','load'}, dimensions={0}, use_global_device_ids=true | all-gather | bytes 655360 | tf_op jit(solution)/shard_map/all_gather | solution.py:216
  209.9 4.4 %fusion.24 = bf16[16,8,32,128]{3,1,2,0:T(8,128)(2,1)S(1)} fusion(f32[16,8,32,128]{3,2,1,0:T(8,128)S(1)} %bitcast.167, f32[128,4095]{1,0:T(8,128)S(1)} %get-tuple-element.52, f32[128,1]{1,0:T(8,128)S(1)} %get-tuple-element.54, f32[128,1]{1,0:T(8,128)S(1)} %get-tuple-element.53, f32[128,4095]{1,0:T(8,128)S(1)} %get-tuple-element.51, ...), kind=kLoop, calls=%fused_computation.43 | loop fusion | flops 3670016 | bytes 11538432
  215.9 4.6 %fusion.52 = (f32[2,16,128]{2,1,0:T(8,128)S(1)}, bf16[2,16,128,512]{2,3,1,0:T(8,128)(2,1)S(1)}) fusion(f32[2,512,128,16]{2,1,3,0:T(8,128)S(1)} %fusion.22, pred[128,512]{0,1:T(8,128)(4,1)S(1)} %copy-done.17), kind=kOutput, calls=%fused_computation.173 | output fusion | flops 16777728 | bytes 12664832 | tf_op jit(solution)/shard_map/sub | solution.py:233
  (162 shorter events, 59.2 us)
Async XLA Ops:
  0.6 7.2 %copy-start = (bf16[4096,128]{1,0:T(8,128)(2,1)S(1)}, bf16[4096,128]{1,0:T(8,128)(2,1)}, u32[]{:S(2)}) copy-start(bf16[4096,128]{1,0:T(8,128)(2,1)} %param.13) | copy-start | bytes 3145732
  0.6 11.9 %copy-start.8 = (bf16[128,4096]{1,0:T(8,128)(2,1)S(1)}, bf16[128,4096]{1,0:T(8,128)(2,1)}, u32[]{:S(2)}) copy-start(bf16[128,4096]{1,0:T(8,128)(2,1)} %param.10) | copy-start | bytes 3145732
  0.7 29.1 %collective-permute-start = (bf16[128,4096]{1,0:T(8,128)(2,1)}, bf16[128,4096]{1,0:T(8,128)(2,1)}, u32[]{:S(2)}, u32[]{:S(2)}) collective-permute-start(bf16[128,4096]{1,0:T(8,128)(2,1)} %param.10), channel_id=1, source_target_pairs={{0,4},{4,8},{8,12},{12,0},{1,5},{5,9},{9,13},{13,1},{2,6},{6,10},{... | collective-permute-start | bytes 3145736 | tf_op jit(solution)/shard_map/ppermute | solution.py:135
  3.7 112.6 %collective-permute-start.5 = (bf16[256,512]{1,0:T(8,128)(2,1)}, bf16[256,512]{1,0:T(8,128)(2,1)}, u32[]{:S(2)}, u32[]{:S(2)}) collective-permute-start(bf16[256,512]{1,0:T(8,128)(2,1)} %param.16), channel_id=1, source_target_pairs={{0,1},{1,0},{2,3},{3,2},{4,5},{5,4},{6,7},{7,6},{8,9},{9,8},{10,11... | collective-permute-start | bytes 786440 | tf_op jit(solution)/shard_map/ppermute | solution.py:81
  3.7 114.3 %collective-permute-start.8 = (bf16[256,4096]{1,0:T(8,128)(2,1)}, bf16[256,4096]{1,0:T(8,128)(2,1)}, u32[]{:S(2)}, u32[]{:S(2)}) collective-permute-start(bf16[256,4096]{1,0:T(8,128)(2,1)} %param.15), channel_id=1, source_target_pairs={{0,1},{1,0},{2,3},{3,2},{4,5},{5,4},{6,7},{7,6},{8,9},{9,8},{10,11... | collective-permute-start | bytes 6291464 | tf_op jit(solution)/shard_map/ppermute | solution.py:81
  5.0 11.2 %copy-start.18 = (s32[128]{0:T(128)}, s32[128]{0:T(128)S(1)}, u32[]{:S(2)}) copy-start(s32[128]{0:T(128)S(1)} %iota_add_fusion.5) | copy-start | bytes 1540
  7.8 8.9 %copy-start.19 = (s32[128]{0:T(128)}, s32[128]{0:T(128)S(1)}, u32[]{:S(2)}) copy-start(s32[128]{0:T(128)S(1)} %get-tuple-element.40) | copy-start | bytes 1540
  16.2 15.4 %copy-start.3 = (bf16[4096,128]{1,0:T(8,128)(2,1)S(1)}, bf16[4096,128]{1,0:T(8,128)(2,1)}, u32[]{:S(2)}) copy-start(bf16[4096,128]{1,0:T(8,128)(2,1)} %param.14) | copy-start | bytes 3145732
  20.8 12.5 %copy-start.2 = (bf16[4096,512]{1,0:T(8,128)(2,1)S(1)}, bf16[4096,512]{1,0:T(8,128)(2,1)}, u32[]{:S(2)}) copy-start(bf16[4096,512]{1,0:T(8,128)(2,1)} %param.12) | copy-start | bytes 12582916
  36.0 27.8 %collective-permute-start.1 = (bf16[128,4096]{1,0:T(8,128)(2,1)}, bf16[128,4096]{1,0:T(8,128)(2,1)S(1)}, u32[]{:S(2)}, u32[]{:S(2)}) collective-permute-start(bf16[128,4096]{1,0:T(8,128)(2,1)} %collective-permute-done), channel_id=1, source_target_pairs={{0,4},{4,8},{8,12},{12,0},{1,5},{5,9},{9,13},{13,1},{2,6},{6,10},{... | collective-permute-start | bytes 3145736 | tf_op jit(solution)/shard_map/ppermute | solution.py:135
  63.9 16.3 %copy-start.4 = (bf16[4096,128]{1,0:T(8,128)(2,1)S(1)}, bf16[4096,128]{1,0:T(8,128)(2,1)}, u32[]{:S(2)}) copy-start(bf16[4096,128]{1,0:T(8,128)(2,1)} %param.14) | copy-start | bytes 3145732
  63.9 26.6 %collective-permute-start.2 = (bf16[128,4096]{1,0:T(8,128)(2,1)S(1)}, bf16[128,4096]{1,0:T(8,128)(2,1)S(1)}, u32[]{:S(2)}, u32[]{:S(2)}) collective-permute-start(bf16[128,4096]{1,0:T(8,128)(2,1)S(1)} %collective-permute-done.1), channel_id=1, source_target_pairs={{0,4},{4,8},{8,12},{12,0},{1,5},{5,9},{9,13},{13,1},{2,6},{6,10},{... | collective-permute-start | bytes 3145736 | tf_op jit(solution)/shard_map/ppermute | solution.py:135
  104.7 5.2 %copy-start.5 = (bf16[4096,128]{1,0:T(8,128)(2,1)S(1)}, bf16[4096,128]{1,0:T(8,128)(2,1)}, u32[]{:S(2)}) copy-start(bf16[4096,128]{1,0:T(8,128)(2,1)} %param.14) | copy-start | bytes 3145732
  109.3 44.2 %collective-permute-start.6 = (f32[2,128,4096]{2,1,0:T(8,128)}, f32[2,128,4096]{2,1,0:T(8,128)}, u32[]{:S(2)}, u32[]{:S(2)}) collective-permute-start(f32[2,128,4096]{2,1,0:T(8,128)} %dynamic-slice_bitcast_fusion), channel_id=1, source_target_pairs={{0,1},{1,0},{2,3},{3,2},{4,5},{5,4},{6,7},{7,6},{8,9},{9,8},{10,11... | collective-permute-start | bytes 12582920 | tf_op jit(solution)/shard_map/ppermute | solution.py:99
  110.7 5.6 %copy-start.15 = (bf16[256,512]{1,0:T(8,128)(2,1)S(1)}, bf16[256,512]{1,0:T(8,128)(2,1)}, u32[]{:S(2)}) copy-start(bf16[256,512]{1,0:T(8,128)(2,1)} %param.16) | copy-start | bytes 786436
  115.8 11.9 %collective-permute-start.3 = (f32[2,128,576]{1,2,0:T(8,128)S(1)}, f32[2,128,576]{1,2,0:T(8,128)}, u32[]{:S(2)}, u32[]{:S(2)}) collective-permute-start(f32[2,128,576]{1,2,0:T(8,128)S(1)} %dynamic-slice_bitcast_fusion.2), channel_id=1, source_target_pairs={{0,1},{1,0},{2,3},{3,2},{4,5},{5,4},{6,7},{7,6},{8,9},{9,8},{10,11... | collective-permute-start | bytes 1769480 | tf_op jit(solution)/shard_map/ppermute | solution.py:99
  129.2 10.8 %copy-start.25 = (f32[128]{0:T(128)S(1)}, f32[128]{0:T(128)}, u32[]{:S(2)}) copy-start(f32[128]{0:T(128)} %rsqrt_multiply_fusion) | copy-start | bytes 1540
  129.2 10.8 %copy-start.26 = (s32[32]{0:T(128)S(1)}, s32[32]{0:T(128)}, u32[]{:S(2)}) copy-start(s32[32]{0:T(128)} %iota_add_fusion) | copy-start | bytes 388
  129.2 9.8 %collective-permute-start.4 = (f32[128,576]{1,0:T(8,128)S(1)}, f32[128,576]{1,0:T(8,128)}, u32[]{:S(2)}, u32[]{:S(2)}) collective-permute-start(f32[128,576]{1,0:T(8,128)S(1)} %bitcast.175), channel_id=1, source_target_pairs={{0,2},{2,0},{1,3},{3,1},{4,6},{6,4},{5,7},{7,5},{8,10},{10,8},{9,1... | collective-permute-start | bytes 884744 | tf_op jit(solution)/shard_map/ppermute | solution.py:99
  157.5 4.0 %copy-start.6 = (f32[2,128,4096]{2,1,0:T(8,128)}, f32[2,128,4096]{2,1,0:T(8,128)S(1)}, u32[]{:S(2)}) copy-start(f32[2,128,4096]{2,1,0:T(8,128)S(1)} %bitcast_add_fusion) | copy-start | bytes 12582916
  157.5 3.8 %copy-start.23 = (pred[512]{0:T(512)(128)(4,1)S(1)}, pred[512]{0:T(512)(128)(4,1)}, u32[]{:S(2)}) copy-start(pred[512]{0:T(512)(128)(4,1)} %get-tuple-element.81) | copy-start | bytes 1540
  159.0 47.8 %collective-permute-start.7 = (f32[128,4096]{1,0:T(8,128)}, f32[128,4096]{1,0:T(8,128)}, u32[]{:S(2)}, u32[]{:S(2)}) collective-permute-start(f32[128,4096]{1,0:T(8,128)} %dynamic-slice_bitcast_fusion.1), channel_id=1, source_target_pairs={{0,2},{2,0},{1,3},{3,1},{4,6},{6,4},{5,7},{7,5},{8,10},{10,8},{9,1... | collective-permute-start | bytes 6291464 | tf_op jit(solution)/shard_map/ppermute | solution.py:99
  161.5 45.3 %copy-start.10 = (bf16[128,512]{1,0:T(8,128)(2,1)}, bf16[128,512]{1,0:T(8,128)(2,1)S(1)}, u32[]{:S(2)}) copy-start(bf16[128,512]{1,0:T(8,128)(2,1)S(1)} %fusion.27) | copy-start | bytes 393220
  177.2 29.6 %copy-start.7 = (f32[2,128,4096]{2,1,0:T(8,128)S(1)}, f32[2,128,4096]{2,1,0:T(8,128)}, u32[]{:S(2)}) copy-start(f32[2,128,4096]{2,1,0:T(8,128)} %copy-done.6) | copy-start | bytes 12582916
  (12 other events, 26.1 us)

commit v12 on v8

--- a/solution.py
+++ b/solution.py
@@ -115,20 +115,32 @@
     query_terms = jnp.zeros((ring, chunk, query_cols), jnp.float32)
     shift = [(i, (i + 1) % ring) for i in range(ring)]
     held = tokens
+    waiting = []
     for step in range(ring):
         following = lax.ppermute(held, "tensor", shift) if step < ring - 1 else None
         owner = (tensor_index - step) % ring
-        block_ids = owner * chunk + jnp.arange(chunk, dtype=jnp.int32)
-        _, _, block_hot = tenant_table(block_ids, adapter_rank, token_lengths, adapter_slot)
-        small_block = jnp.concatenate(
-            [
-                product(held, weight_keyval),
-                select_slot(product(held, down_query), block_hot),
-                select_slot(product(held, down_keyval), block_hot),
-            ],
-            axis=1,
-        )
-        small_terms = lax.dynamic_update_slice_in_dim(small_terms, small_block[None], owner, 0)
+        defer = 0 < step < ring - 1 and ring <= 4
+        if defer:
+            waiting.append((held, owner))
+        else:
+            batch = waiting + [(held, owner)] if step == ring - 1 else [(held, owner)]
+            rows_now = jnp.concatenate([b for b, _ in batch], axis=0)
+            block_ids = jnp.concatenate(
+                [o * chunk + jnp.arange(chunk, dtype=jnp.int32) for _, o in batch]
+            )
+            _, _, block_hot = tenant_table(block_ids, adapter_rank, token_lengths, adapter_slot)
+            small_rows = jnp.concatenate(
+                [
+                    product(rows_now, weight_keyval),
+                    select_slot(product(rows_now, down_query), block_hot),
+                    select_slot(product(rows_now, down_keyval), block_hot),
+                ],
+                axis=1,
+            )
+            for index, (_, o) in enumerate(batch):
+                small_terms = lax.dynamic_update_slice_in_dim(
+                    small_terms, small_rows[index * chunk : (index + 1) * chunk][None], o, 0
+                )
         if step == 0 and ring > 2:
             first_block, first_owner = held, owner
         elif step == 1 and ring > 2:

time: 208 us -> 208 us (level)
  waiting for transfers between devices: 34.7 us -> 46.7 us
  local copies, waits for them, and re-layouts: 21.7 us -> 17.5 us
  matrix products: 68.6 us -> 64.8 us
  other arithmetic: 18.7 us -> 16.6 us
    ppermute x3, waiting for transfers between devices: 18.6 us -> 31.4 us  [shards(): following = lax.ppermute(held, 'tensor', shift) if step < ring - 1 else None]
    reduce_scatter x1, waiting for transfers between devices: 7.85 us -> 0.03 us  [shards(): lax.psum_scatter(query_terms.reshape(ring * chunk, -1), ('seq', 'load'),...]
    ppermute x2, waiting for transfers between devices: 8.27 us -> 15.3 us  [ring_reduce_scatter(): total = lax.ppermute(total, axis, shift) + pick(step)]
    unnamed x42 -> x38, local copies, waits for them, and re-layouts: 1.65 us -> 6.3 us
    dot_general x17 -> x11, matrix products: 66.6 us -> 62.7 us  [product(): return jnp.dot(left, right, preferred_element_type=jnp.float32)]
    dynamic_update_slice x4, local copies, waits for them, and re-layouts: 3.93 us -> 0.1 us  [shards(): lax.dynamic_update_slice_in_dim(small_terms, small_rows[index * chunk:(in...]
  transfers between devices with their start and end apart: 7 -> 7, of which waited for: 5 -> 4; matrix products, arithmetic and copies ran while one was open for 45% -> 39% of each run, Pallas kernels for 0% -> 0%
where the time goes in v12:
time: 208 us
  matrix products  64.8 us (31%)
  waiting for transfers between devices  46.7 us (22%)
  blocking collectives  41.3 us (20%)
  local copies, waits for them, and re-layouts  17.5 us (8%)
  other arithmetic  16.6 us (8%)
  between operations  16.4 us (8%)
  starting transfers between devices  4.53 us (2%)
    dot_general x11, matrix products, product(): return jnp.dot(left, right, preferred_element_type=jnp.float32)  62.7 us
    ppermute x3, waiting for transfers between devices, shards(): following = lax.ppermute(held, 'tensor', shift) if step < ring - 1 else None  31.4 us
    ppermute x2, waiting for transfers between devices, ring_reduce_scatter(): total = lax.ppermute(total, axis, shift) + pick(step)  15.3 us
    all_gather x1, blocking collectives, shards(): kv_all = lax.all_gather(kv_local, 'tensor', axis=1, tiled=True)  14.8 us
    all_gather x1, blocking collectives, shards(): lax.all_gather(jnp.concatenate([low_query, low_keyval], axis=1), 'tensor'...  13.1 us
    all_gather x1, blocking collectives, shards(): lax.all_gather(jnp.concatenate([key_heads, value_heads], axis=1), ('seq',...  10.8 us
    unnamed x38, local copies, waits for them, and re-layouts  6.3 us
    sub x1, other arithmetic, shards(): exp_scores = jnp.where(visible, jnp.exp(scores - row_top[..., None]), 0.0)  4.59 us
  transfers between devices with their start and end apart: 7, of which 4 were waited for; matrix products, arithmetic and copies ran while one was open for 39% of the time, Pallas kernels for 0%

profile of v12, /device:TPU:0, one launch (start us, length us, event | category | flops | bytes accessed | tf_op | source)
XLA Modules:
  0.0 207.8 jit_solution(4502990795353519355)
XLA Ops:
  8.1 3.1 %collective-permute-start = (bf16[128,4096]{1,0:T(8,128)(2,1)}, bf16[128,4096]{1,0:T(8,128)(2,1)}, u32[]{:S(2)}, u32[]{:S(2)}) collective-permute-start(bf16[128,4096]{1,0:T(8,128)(2,1)} %param.10), channel_id=1, source_target_pairs={{0,4},{4,8},{8,12},{12,0},{1,5},{5,9},{9,13},{13,1},{2,6},{6,10},{... | collective-permute-start | bytes 3145736 | tf_op jit(solution)/shard_map/ppermute | solution.py:120
  12.8 1.7 fusion.49
  15.6 2.9 %fusion.48 = f32[128,512]{1,0:T(8,128)S(1)} fusion(bf16[128,4096]{1,0:T(8,128)(2,1)S(1)} %copy-done.3, bf16[4096,512]{1,0:T(8,128)(2,1)} %param.12), kind=kOutput, calls=%fused_computation.143 | convolution fusion | flops 536870912 | bytes 5505024 | tf_op jit(solution)/shard_map/dot_general | solution.py:19
  19.9 16.8 %collective-permute-done = bf16[128,4096]{1,0:T(8,128)(2,1)} collective-permute-done((bf16[128,4096]{1,0:T(8,128)(2,1)}, bf16[128,4096]{1,0:T(8,128)(2,1)}, u32[]{:S(2)}, u32[]{:S(2)}) %collective-permute-start) | collective-permute-done | bytes 1048608 | tf_op jit(solution)/shard_map/ppermute | solution.py:120
  36.7 15.4 %fusion.13 = f32[256,4096]{1,0:T(8,128)S(1)} fusion(bf16[4096,4096]{1,0:T(8,128)(2,1)} %param.11, bf16[128,4096]{1,0:T(8,128)(2,1)} %collective-permute-done, bf16[128,4096]{1,0:T(8,128)(2,1)S(1)} %copy-done.3), kind=kOutput, calls=%fused_computation.21 | convolution fusion | flops 8594128896 | bytes 39845888 | tf_op jit(solution)/shard_map/dot_general | solution.py:19
  52.0 4.3 %broadcast_in_dim.242 = f32[4,128,4096]{2,1,0:T(8,128)} broadcast(f32[]{:T(128)} %constant.191.clone.1), dimensions={} | broadcast | bytes 8388612 | tf_op jit(solution)/shard_map/broadcast_in_dim | solution.py:115
  56.3 1.5 fusion.12
  57.8 1.5 fusion.11
  59.4 3.7 %collective-permute-done.1 = bf16[128,4096]{1,0:T(8,128)(2,1)S(1)} collective-permute-done((bf16[128,4096]{1,0:T(8,128)(2,1)}, bf16[128,4096]{1,0:T(8,128)(2,1)S(1)}, u32[]{:S(2)}, u32[]{:S(2)}) %collective-permute-start.1) | collective-permute-done | bytes 1048608 | tf_op jit(solution)/shard_map/ppermute | solution.py:120
  63.0 14.2 %fusion.3 = f32[4,128,4096]{2,1,0:T(8,128)} fusion(f32[4,128,4096]{2,1,0:T(8,128)} %fusion.11, s32[]{:T(128)S(6)} %select_n.250, bf16[128,4096]{1,0:T(8,128)(2,1)S(1)} %collective-permute-done.1, bf16[4096,4096]{1,0:T(8,128)(2,1)} %param.11), kind=kOutput, calls=%fused_computation.7 | convolution fusion | flops 4294967296 | bytes 36700164 | tf_op jit(solution)/shard_map/dot_general | solution.py:19
  77.3 11.0 %collective-permute-done.2 = bf16[128,4096]{1,0:T(8,128)(2,1)S(1)} collective-permute-done((bf16[128,4096]{1,0:T(8,128)(2,1)S(1)}, bf16[128,4096]{1,0:T(8,128)(2,1)S(1)}, u32[]{:S(2)}, u32[]{:S(2)}) %collective-permute-start.2) | collective-permute-done | bytes 1048608 | tf_op jit(solution)/shard_map/ppermute | solution.py:120
  88.3 14.2 %fusion.2 = f32[4,128,4096]{2,1,0:T(8,128)} fusion(f32[4,128,4096]{2,1,0:T(8,128)} %fusion.3, s32[]{:T(128)S(6)} %select_n.255, bf16[128,4096]{1,0:T(8,128)(2,1)S(1)} %collective-permute-done.2, bf16[4096,4096]{1,0:T(8,128)(2,1)} %param.11), kind=kOutput, calls=%fused_computation.5 | convolution fusion | flops 4294967296 | bytes 36700164 | tf_op jit(solution)/shard_map/dot_general | solution.py:19
  105.8 1.6 copy-done.2
  108.6 3.7 %fusion.53 = f32[384,128]{0,1:T(8,128)S(1)} fusion(bf16[384,4096]{1,0:T(8,128)(2,1)} %copy-done.2, bf16[4096,128]{1,0:T(8,128)(2,1)S(1)} %copy-done.7), kind=kOutput, calls=%fused_computation.148 | convolution fusion | flops 402653184 | bytes 4390912 | tf_op jit(solution)/shard_map/dot_general | solution.py:19
  112.9 5.9 %fusion.51 = f32[384,512]{1,0:T(8,128)S(1)} fusion(bf16[384,4096]{1,0:T(8,128)(2,1)} %copy-done.2, bf16[4096,512]{1,0:T(8,128)(2,1)} %param.12), kind=kOutput, calls=%fused_computation.146 | convolution fusion | flops 1610612736 | bytes 8126464 | tf_op jit(solution)/shard_map/dot_general | solution.py:19
  120.4 2.5 %all_gather.20 = bf16[512,512]{1,0:T(8,128)(2,1)S(1)} all-gather(bf16[256,512]{1,0:T(8,128)(2,1)} %param.16), channel_id=1, replica_groups=mesh['groups'=2,'tensor'=4,'seq'=2,'load'=2] {'load'}, dimensions={0}, use_global_device_ids=true | all-gather | bytes 786432 | tf_op jit(solution)/shard_map/all_gather | solution.py:110
  125.9 15.3 %collective-permute-done.4 = f32[128,576]{1,0:T(8,128)S(1)} collective-permute-done((f32[128,576]{1,0:T(8,128)S(1)}, f32[128,576]{1,0:T(8,128)S(1)}, u32[]{:S(2)}, u32[]{:S(2)}) %collective-permute-start.4) | collective-permute-done | bytes 294944 | tf_op jit(solution)/shard_map/ppermute | solution.py:85
  141.5 13.1 %all-gather = bf16[128,256]{0,1:T(8,128)(2,1)S(1)} all-gather(bf16[128,64]{0,1:T(8,128)(2,1)S(1)} %copy.69), channel_id=2, replica_groups=mesh['groups'=2,'tensor'=4,'seq'=2,'load'=2] {'tensor'}, dimensions={1}, use_global_device_ids=true | all-gather | bytes 81920 | tf_op jit(solution)/shard_map/all_gather | solution.py:186
  155.6 14.8 %all_gather.21 = bf16[128,2048]{1,0:T(8,128)(2,1)S(1)} all-gather(bf16[128,512]{1,0:T(8,128)(2,1)S(1)} %fusion.25), channel_id=1, replica_groups=mesh['groups'=2,'tensor'=4,'seq'=2,'load'=2] {'tensor'}, dimensions={1}, use_global_device_ids=true | all-gather | bytes 655360 | tf_op jit(solution)/shard_map/all_gather | solution.py:200
  171.0 10.8 %all_gather.22 = bf16[512,4,128]{2,0,1:T(8,128)(2,1)} all-gather(bf16[128,4,128]{2,0,1:T(8,128)(2,1)S(1)} %pad_maximum_fusion.1), channel_id=1, replica_groups=mesh['groups'=2,'tensor'=4,'seq'=2,'load'=2] {'seq','load'}, dimensions={0}, use_global_device_ids=true | all-gather | bytes 655360 | tf_op jit(solution)/shard_map/all_gather | solution.py:213
  181.8 2.9 %fusion.54 = f32[128,4096]{1,0:T(8,128)S(1)} fusion(bf16[128,512]{0,1:T(8,128)(2,1)S(1)} %bitcast.140, bf16[512,4096]{1,0:T(8,128)(2,1)} %all-gather.3.cloned.1.call-done), kind=kOutput, calls=%fused_computation.149 | convolution fusion | flops 536870912 | bytes 6422528 | tf_op jit(solution)/shard_map/dot_general | solution.py:19
  184.8 1.8 add.301
  187.7 4.4 %fusion.22 = bf16[16,8,32,128]{3,1,2,0:T(8,128)(2,1)S(1)} fusion(f32[16,8,32,128]{3,2,1,0:T(8,128)S(1)} %bitcast.134, f32[128,4095]{1,0:T(8,128)S(1)} %get-tuple-element.39, f32[128,1]{1,0:T(8,128)S(1)} %get-tuple-element.41, f32[128,1]{1,0:T(8,128)S(1)} %get-tuple-element.40, f32[128,4095]{1,0:T(8,128)S(1)} %get-tuple-element.38, f32[128,4096]{1,0:T(8,128)S(1)} %add.301, ...), kind=kLoop, calls=%fused_computation.30 | loop fusion | flops 3670016 | bytes 11538432
  193.7 4.6 %fusion.47 = (f32[2,16,128]{2,1,0:T(8,128)S(1)}, bf16[2,16,128,512]{2,3,1,0:T(8,128)(2,1)S(1)}) fusion(f32[2,512,128,16]{2,1,3,0:T(8,128)S(1)} %fusion.20, pred[128,512]{0,1:T(8,128)(4,1)S(1)} %copy-done.10), kind=kOutput, calls=%fused_computation.142 | output fusion | flops 16777728 | bytes 12664832 | tf_op jit(solution)/shard_map/sub | solution.py:230
  (120 shorter events, 19.7 us)
Async XLA Ops:
  8.0 4.8 %copy-start = (bf16[4096,128]{1,0:T(8,128)(2,1)S(1)}, bf16[4096,128]{1,0:T(8,128)(2,1)}, u32[]{:S(2)}) copy-start(bf16[4096,128]{1,0:T(8,128)(2,1)} %param.13) | copy-start | bytes 3145732
  8.0 6.7 %copy-start.3 = (bf16[128,4096]{1,0:T(8,128)(2,1)S(1)}, bf16[128,4096]{1,0:T(8,128)(2,1)}, u32[]{:S(2)}) copy-start(bf16[128,4096]{1,0:T(8,128)(2,1)} %param.10) | copy-start | bytes 3145732
  8.0 6.5 %copy-start.16 = (s32[4]{0:T(128)S(1)}, s32[4]{0:T(128)}, u32[]{:S(2)}) copy-start(s32[4]{0:T(128)} %param.17) | copy-start | bytes 52
  8.0 6.5 %copy-start.12 = (s32[4]{0:T(128)S(1)}, s32[4]{0:T(128)}, u32[]{:S(2)}) copy-start(s32[4]{0:T(128)} %param.19) | copy-start | bytes 52
  8.0 6.7 %copy-start.6 = (bf16[4096,128]{1,0:T(8,128)(2,1)S(1)}, bf16[4096,128]{1,0:T(8,128)(2,1)}, u32[]{:S(2)}) copy-start(bf16[4096,128]{1,0:T(8,128)(2,1)} %param.14) | copy-start | bytes 3145732
  8.1 173.7 %all-gather.3.cloned.1.call-start = ((), (), s32[]{:S(2)}) async-start(), calls=%async_computation.2 | async-start | bytes 6291456 | tf_op jit(solution)/shard_map/all_gather | solution.py:109
  8.1 28.6 %collective-permute-start = (bf16[128,4096]{1,0:T(8,128)(2,1)}, bf16[128,4096]{1,0:T(8,128)(2,1)}, u32[]{:S(2)}, u32[]{:S(2)}) collective-permute-start(bf16[128,4096]{1,0:T(8,128)(2,1)} %param.10), channel_id=1, source_target_pairs={{0,4},{4,8},{8,12},{12,0},{1,5},{5,9},{9,13},{13,1},{2,6},{6,10},{... | collective-permute-start | bytes 3145736 | tf_op jit(solution)/shard_map/ppermute | solution.py:120
  11.2 173.6 %reduce-scatter.2.cloned.1.call-start = ((), (), s32[]{:S(2)}) async-start(), calls=%async_computation.1 | async-start | bytes 10485760 | tf_op jit(solution)/shard_map/reduce_scatter | solution.py:173
  18.9 1.0 copy-start.4
  36.7 26.4 %collective-permute-start.1 = (bf16[128,4096]{1,0:T(8,128)(2,1)}, bf16[128,4096]{1,0:T(8,128)(2,1)S(1)}, u32[]{:S(2)}, u32[]{:S(2)}) collective-permute-start(bf16[128,4096]{1,0:T(8,128)(2,1)} %collective-permute-done), channel_id=1, source_target_pairs={{0,4},{4,8},{8,12},{12,0},{1,5},{5,9},{9,13},{13,1},{2,6},{6,10},{... | collective-permute-start | bytes 3145736 | tf_op jit(solution)/shard_map/ppermute | solution.py:120
  63.0 25.2 %collective-permute-start.2 = (bf16[128,4096]{1,0:T(8,128)(2,1)S(1)}, bf16[128,4096]{1,0:T(8,128)(2,1)S(1)}, u32[]{:S(2)}, u32[]{:S(2)}) collective-permute-start(bf16[128,4096]{1,0:T(8,128)(2,1)S(1)} %collective-permute-done.1), channel_id=1, source_target_pairs={{0,4},{4,8},{8,12},{12,0},{1,5},{5,9},{9,13},{13,1},{2,6},{6,10},{... | collective-permute-start | bytes 3145736 | tf_op jit(solution)/shard_map/ppermute | solution.py:120
  105.7 2.8 %copy-start.7 = (bf16[4096,128]{1,0:T(8,128)(2,1)S(1)}, bf16[4096,128]{1,0:T(8,128)(2,1)}, u32[]{:S(2)}) copy-start(bf16[4096,128]{1,0:T(8,128)(2,1)} %param.14) | copy-start | bytes 3145732
  105.8 1.6 copy-start.2
  118.7 1.3 copy-start.5
  120.1 5.1 %copy-start.11 = (f32[128]{0:T(128)S(1)}, f32[128]{0:T(128)}, u32[]{:S(2)}) copy-start(f32[128]{0:T(128)} %get-tuple-element.66) | copy-start | bytes 1540
  120.2 3.4 %collective-permute-start.3 = (f32[2,128,576]{1,2,0:T(8,128)S(1)}, f32[2,128,576]{1,2,0:T(8,128)S(1)}, u32[]{:S(2)}, u32[]{:S(2)}) collective-permute-start(f32[2,128,576]{1,2,0:T(8,128)S(1)} %dynamic-slice_bitcast_fusion), channel_id=1, source_target_pairs={{0,1},{1,0},{2,3},{3,2},{4,5},{5,4},{6,7},{7,6},{8,9},{9,8},{10,11... | collective-permute-start | bytes 1769480 | tf_op jit(solution)/shard_map/ppermute | solution.py:85
  120.3 20.9 %copy-start.15 = (f32[128]{0:T(128)S(1)}, f32[128]{0:T(128)}, u32[]{:S(2)}) copy-start(f32[128]{0:T(128)} %rsqrt_multiply_fusion) | copy-start | bytes 1540
  123.7 31.7 %copy-start.13 = (pred[512]{0:T(512)(128)(4,1)S(1)}, pred[512]{0:T(512)(128)(4,1)}, u32[]{:S(2)}) copy-start(pred[512]{0:T(512)(128)(4,1)} %get-tuple-element.71) | copy-start | bytes 1540
  123.7 31.7 %copy-start.14 = (pred[512]{0:T(512)(128)(4,1)S(1)}, pred[512]{0:T(512)(128)(4,1)}, u32[]{:S(2)}) copy-start(pred[512]{0:T(512)(128)(4,1)} %get-tuple-element.72) | copy-start | bytes 1540
  123.9 17.3 %collective-permute-start.4 = (f32[128,576]{1,0:T(8,128)S(1)}, f32[128,576]{1,0:T(8,128)S(1)}, u32[]{:S(2)}, u32[]{:S(2)}) collective-permute-start(f32[128,576]{1,0:T(8,128)S(1)} %bitcast.142), channel_id=1, source_target_pairs={{0,2},{2,0},{1,3},{3,1},{4,6},{6,4},{5,7},{7,5},{8,10},{10,8},{9,1... | collective-permute-start | bytes 884744 | tf_op jit(solution)/shard_map/ppermute | solution.py:85
  155.6 29.1 %copy-start.9 = (bf16[128,512]{1,0:T(8,128)(2,1)}, bf16[128,512]{1,0:T(8,128)(2,1)S(1)}, u32[]{:S(2)}) copy-start(bf16[128,512]{1,0:T(8,128)(2,1)S(1)} %fusion.25) | copy-start | bytes 393220
  187.7 4.6 %copy-start.8 = (bf16[512,4,128]{2,0,1:T(8,128)(2,1)S(1)}, bf16[512,4,128]{2,0,1:T(8,128)(2,1)}, u32[]{:S(2)}) copy-start(bf16[512,4,128]{2,0,1:T(8,128)(2,1)} %all_gather.22) | copy-start | bytes 1572868
  192.3 1.3 copy-start.10
  198.2 2.1 %copy-start.1 = (bf16[4096,128]{1,0:T(8,128)(2,1)S(1)}, bf16[4096,128]{1,0:T(8,128)(2,1)}, u32[]{:S(2)}) copy-start(bf16[4096,128]{1,0:T(8,128)(2,1)} %param.13) | copy-start | bytes 3145732
Sparse Core Ops, SparseCore 0:
  11.3 15.5 all-gather.2
Sparse Core Ops, SparseCore 1:
  102.6 79.2 reduce-scatter.1

commit v13 on v8

--- a/solution.py
+++ b/solution.py
@@ -30,6 +30,7 @@
     cosine = jnp.cos(angles)
     sine_angle = jnp.sin(angles)
     signed_sine = jnp.where((col % 2 == 0)[None, :], -sine_angle, sine_angle)
+    cosine, signed_sine = lax.optimization_barrier((cosine, signed_sine))
     cosine = jnp.tile(cosine, (1, cols // width))
     signed_sine = jnp.tile(signed_sine, (1, cols // width))
     is_even = (jnp.arange(cols, dtype=jnp.int32) % 2 == 0)[None, :]

time: 208 us -> 207 us (level)
  no operation moved by 1% of the time
where the time goes in v13:
time: 207 us
  matrix products  68.5 us (33%)
  blocking collectives  41.8 us (20%)
  waiting for transfers between devices  33.8 us (16%)
  local copies, waits for them, and re-layouts  22.2 us (11%)
  other arithmetic  18.4 us (9%)
  between operations  16.3 us (8%)
  starting transfers between devices  5.62 us (3%)
    dot_general x17, matrix products, product(): return jnp.dot(left, right, preferred_element_type=jnp.float32)  66.4 us
    ppermute x3, waiting for transfers between devices, shards(): following = lax.ppermute(held, 'tensor', shift) if step < ring - 1 else None  18.6 us
    all_gather x1, blocking collectives, shards(): kv_all = lax.all_gather(kv_local, 'tensor', axis=1, tiled=True)  15 us
    all_gather x1, blocking collectives, shards(): lax.all_gather(jnp.concatenate([low_query, low_keyval], axis=1), 'tensor'...  13.1 us
    all_gather x1, blocking collectives, shards(): lax.all_gather(jnp.concatenate([key_heads, value_heads], axis=1), ('seq',...  11.1 us
    ppermute x2, waiting for transfers between devices, ring_reduce_scatter(): total = lax.ppermute(total, axis, shift) + pick(step)  7.78 us
    reduce_scatter x1, waiting for transfers between devices, shards(): lax.psum_scatter(query_terms.reshape(ring * chunk, -1), ('seq', 'load'),...  7.43 us
    sub x1, other arithmetic, shards(): exp_scores = jnp.where(visible, jnp.exp(scores - row_top[..., None]), 0.0)  4.59 us
  transfers between devices with their start and end apart: 7, of which 5 were waited for; matrix products, arithmetic and copies ran while one was open for 45% of the time, Pallas kernels for 0%

profile of v13, /device:TPU:0, one launch (start us, length us, event | category | flops | bytes accessed | tf_op | source)
XLA Modules:
  0.0 206.6 jit_solution(1513930682166711280)
XLA Ops:
  8.1 3.1 %collective-permute-start = (bf16[128,4096]{1,0:T(8,128)(2,1)}, bf16[128,4096]{1,0:T(8,128)(2,1)}, u32[]{:S(2)}, u32[]{:S(2)}) collective-permute-start(bf16[128,4096]{1,0:T(8,128)(2,1)} %param.10), channel_id=1, source_target_pairs={{0,4},{4,8},{8,12},{12,0},{1,5},{5,9},{9,13},{13,1},{2,6},{6,10},{... | collective-permute-start | bytes 3145736 | tf_op jit(solution)/shard_map/ppermute | solution.py:120
  12.9 1.7 fusion.49
  16.1 2.9 %fusion.48 = f32[128,512]{1,0:T(8,128)S(1)} fusion(bf16[128,4096]{1,0:T(8,128)(2,1)S(1)} %copy-done.5, bf16[4096,512]{1,0:T(8,128)(2,1)} %param.12), kind=kOutput, calls=%fused_computation.146 | convolution fusion | flops 536870912 | bytes 5505024 | tf_op jit(solution)/shard_map/dot_general | solution.py:19
  21.2 15.5 %collective-permute-done = bf16[128,4096]{1,0:T(8,128)(2,1)} collective-permute-done((bf16[128,4096]{1,0:T(8,128)(2,1)}, bf16[128,4096]{1,0:T(8,128)(2,1)}, u32[]{:S(2)}, u32[]{:S(2)}) %collective-permute-start) | collective-permute-done | bytes 1048608 | tf_op jit(solution)/shard_map/ppermute | solution.py:120
  36.7 1.7 fusion.52
  38.4 1.7 fusion.53
  40.2 2.8 %fusion.51 = f32[128,512]{1,0:T(8,128)} fusion(bf16[128,4096]{1,0:T(8,128)(2,1)} %collective-permute-done, bf16[4096,512]{1,0:T(8,128)(2,1)S(1)} %copy-done.1), kind=kOutput, calls=%fused_computation.149 | convolution fusion | flops 536870912 | bytes 5505024 | tf_op jit(solution)/shard_map/dot_general | solution.py:19
  45.9 15.3 %fusion.13 = f32[256,4096]{1,0:T(8,128)S(1)} fusion(bf16[4096,4096]{1,0:T(8,128)(2,1)} %param.11, bf16[128,4096]{1,0:T(8,128)(2,1)} %collective-permute-done, bf16[128,4096]{1,0:T(8,128)(2,1)S(1)} %copy-done.6), kind=kOutput, calls=%fused_computation.21 | convolution fusion | flops 8594128896 | bytes 39845888 | tf_op jit(solution)/shard_map/dot_general | solution.py:19
  61.2 4.3 %broadcast_in_dim.276 = f32[4,128,4096]{2,1,0:T(8,128)} broadcast(f32[]{:T(128)} %constant.193.clone.1), dimensions={} | broadcast | bytes 8388612 | tf_op jit(solution)/shard_map/broadcast_in_dim | solution.py:116
  70.5 14.2 %fusion.3 = f32[4,128,4096]{2,1,0:T(8,128)} fusion(f32[4,128,4096]{2,1,0:T(8,128)} %fusion.11, s32[]{:T(128)S(6)} %select_n.264, bf16[128,4096]{1,0:T(8,128)(2,1)S(1)} %collective-permute-done.1, bf16[4096,4096]{1,0:T(8,128)(2,1)} %param.11), kind=kOutput, calls=%fused_computation.7 | convolution fusion | flops 4294967296 | bytes 36700164 | tf_op jit(solution)/shard_map/dot_general | solution.py:19
  86.8 2.9 %fusion.54 = f32[128,512]{1,0:T(8,128)S(1)} fusion(bf16[128,4096]{1,0:T(8,128)(2,1)S(1)} %collective-permute-done.1, bf16[4096,512]{1,0:T(8,128)(2,1)} %param.12), kind=kOutput, calls=%fused_computation.152 | convolution fusion | flops 536870912 | bytes 5505024 | tf_op jit(solution)/shard_map/dot_general | solution.py:19
  92.4 3.0 %collective-permute-done.2 = bf16[128,4096]{1,0:T(8,128)(2,1)S(1)} collective-permute-done((bf16[128,4096]{1,0:T(8,128)(2,1)S(1)}, bf16[128,4096]{1,0:T(8,128)(2,1)S(1)}, u32[]{:S(2)}, u32[]{:S(2)}) %collective-permute-start.2) | collective-permute-done | bytes 1048608 | tf_op jit(solution)/shard_map/ppermute | solution.py:120
  95.4 14.2 %fusion.2 = f32[4,128,4096]{2,1,0:T(8,128)} fusion(f32[4,128,4096]{2,1,0:T(8,128)} %fusion.3, s32[]{:T(128)S(6)} %select_n.269, bf16[128,4096]{1,0:T(8,128)(2,1)S(1)} %collective-permute-done.2, bf16[4096,4096]{1,0:T(8,128)(2,1)} %param.11), kind=kOutput, calls=%fused_computation.5 | convolution fusion | flops 4294967296 | bytes 36700164 | tf_op jit(solution)/shard_map/dot_general | solution.py:19
  111.7 2.9 %fusion.57 = f32[128,512]{1,0:T(8,128)S(1)} fusion(bf16[128,4096]{1,0:T(8,128)(2,1)S(1)} %collective-permute-done.2, bf16[4096,512]{1,0:T(8,128)(2,1)} %param.12), kind=kOutput, calls=%fused_computation.155 | convolution fusion | flops 536870912 | bytes 5505024 | tf_op jit(solution)/shard_map/dot_general | solution.py:19
  118.1 2.6 %all_gather.20 = bf16[512,512]{1,0:T(8,128)(2,1)S(1)} all-gather(bf16[256,512]{1,0:T(8,128)(2,1)S(1)} %copy-done.10), channel_id=1, replica_groups=mesh['groups'=2,'tensor'=4,'seq'=2,'load'=2] {'load'}, dimensions={0}, use_global_device_ids=true | all-gather | bytes 786432 | tf_op jit(solution)/shard_map/all_gather | solution.py:111
  124.3 7.8 %collective-permute-done.4 = f32[128,576]{1,0:T(8,128)S(1)} collective-permute-done((f32[128,576]{1,0:T(8,128)S(1)}, f32[128,576]{1,0:T(8,128)S(1)}, u32[]{:S(2)}, u32[]{:S(2)}) %collective-permute-start.4) | collective-permute-done | bytes 294944 | tf_op jit(solution)/shard_map/ppermute | solution.py:86
  132.4 13.1 %all-gather = bf16[128,256]{0,1:T(8,128)(2,1)S(1)} all-gather(bf16[128,64]{0,1:T(8,128)(2,1)S(1)} %copy.81), channel_id=2, replica_groups=mesh['groups'=2,'tensor'=4,'seq'=2,'load'=2] {'tensor'}, dimensions={1}, use_global_device_ids=true | all-gather | bytes 81920 | tf_op jit(solution)/shard_map/all_gather | solution.py:175
  146.5 15.0 %all_gather.21 = bf16[128,2048]{1,0:T(8,128)(2,1)S(1)} all-gather(bf16[128,512]{1,0:T(8,128)(2,1)S(1)} %fusion.25), channel_id=1, replica_groups=mesh['groups'=2,'tensor'=4,'seq'=2,'load'=2] {'tensor'}, dimensions={1}, use_global_device_ids=true | all-gather | bytes 655360 | tf_op jit(solution)/shard_map/all_gather | solution.py:189
  162.1 11.1 %all_gather.22 = bf16[512,4,128]{2,0,1:T(8,128)(2,1)} all-gather(bf16[128,4,128]{2,0,1:T(8,128)(2,1)S(1)} %pad_maximum_fusion), channel_id=1, replica_groups=mesh['groups'=2,'tensor'=4,'seq'=2,'load'=2] {'seq','load'}, dimensions={0}, use_global_device_ids=true | all-gather | bytes 655360 | tf_op jit(solution)/shard_map/all_gather | solution.py:202
  173.2 2.9 %fusion.60 = f32[128,4096]{1,0:T(8,128)S(1)} fusion(bf16[128,512]{0,1:T(8,128)(2,1)S(1)} %bitcast.152, bf16[512,4096]{1,0:T(8,128)(2,1)} %all-gather.3.cloned.1.call-done), kind=kOutput, calls=%fused_computation.158 | convolution fusion | flops 536870912 | bytes 6422528 | tf_op jit(solution)/shard_map/dot_general | solution.py:19
  176.1 7.4 %reduce-scatter.2.cloned.1.call-done = f32[128,4096]{1,0:T(8,128)} async-done(((f32[512,4096]{1,0:T(8,128)}), f32[128,4096]{1,0:T(8,128)}) %reduce-scatter.2.cloned.1.call-update) | async-done | bytes 2097168 | tf_op jit(solution)/shard_map/reduce_scatter | solution.py:162
  183.6 1.8 add.313
  186.5 4.4 %fusion.22 = bf16[16,8,32,128]{3,1,2,0:T(8,128)(2,1)S(1)} fusion(f32[16,8,32,128]{3,2,1,0:T(8,128)S(1)} %bitcast.148, f32[128,4095]{1,0:T(8,128)S(1)} %get-tuple-element.58, f32[128,1]{1,0:T(8,128)S(1)} %get-tuple-element.60, f32[128,1]{1,0:T(8,128)S(1)} %get-tuple-element.59, f32[128,4095]{1,0:T(8,128)S(1)} %get-tuple-element.57, f32[128,4096]{1,0:T(8,128)S(1)} %add.313, ...), kind=kLoop, calls=%fused_computation.30 | loop fusion | flops 3670016 | bytes 11538432
  192.4 4.6 %fusion.47 = (f32[2,16,128]{2,1,0:T(8,128)S(1)}, bf16[2,16,128,512]{2,3,1,0:T(8,128)(2,1)S(1)}) fusion(f32[2,512,128,16]{2,1,3,0:T(8,128)S(1)} %fusion.20, pred[128,512]{0,1:T(8,128)(4,1)S(1)} %copy-done.12), kind=kOutput, calls=%fused_computation.145 | output fusion | flops 16777728 | bytes 12664832 | tf_op jit(solution)/shard_map/sub | solution.py:219
  (132 shorter events, 33.1 us)
Async XLA Ops:
  8.0 4.9 %copy-start = (bf16[4096,128]{1,0:T(8,128)(2,1)S(1)}, bf16[4096,128]{1,0:T(8,128)(2,1)}, u32[]{:S(2)}) copy-start(bf16[4096,128]{1,0:T(8,128)(2,1)} %param.13) | copy-start | bytes 3145732
  8.0 6.6 %copy-start.5 = (bf16[128,4096]{1,0:T(8,128)(2,1)S(1)}, bf16[128,4096]{1,0:T(8,128)(2,1)}, u32[]{:S(2)}) copy-start(bf16[128,4096]{1,0:T(8,128)(2,1)} %param.10) | copy-start | bytes 3145732
  8.0 6.6 %copy-start.2 = (bf16[4096,128]{1,0:T(8,128)(2,1)S(1)}, bf16[4096,128]{1,0:T(8,128)(2,1)}, u32[]{:S(2)}) copy-start(bf16[4096,128]{1,0:T(8,128)(2,1)} %param.14) | copy-start | bytes 3145732
  8.0 7.2 %copy-start.17 = (s32[4]{0:T(128)S(1)}, s32[4]{0:T(128)}, u32[]{:S(2)}) copy-start(s32[4]{0:T(128)} %param.17) | copy-start | bytes 52
  8.0 7.2 %copy-start.18 = (s32[4]{0:T(128)S(1)}, s32[4]{0:T(128)}, u32[]{:S(2)}) copy-start(s32[4]{0:T(128)} %param.19) | copy-start | bytes 52
  8.1 165.1 %all-gather.3.cloned.1.call-start = ((), (), s32[]{:S(2)}) async-start(), calls=%async_computation.2 | async-start | bytes 6291456 | tf_op jit(solution)/shard_map/all_gather | solution.py:110
  8.1 28.6 %collective-permute-start = (bf16[128,4096]{1,0:T(8,128)(2,1)}, bf16[128,4096]{1,0:T(8,128)(2,1)}, u32[]{:S(2)}, u32[]{:S(2)}) collective-permute-start(bf16[128,4096]{1,0:T(8,128)(2,1)} %param.10), channel_id=1, source_target_pairs={{0,4},{4,8},{8,12},{12,0},{1,5},{5,9},{9,13},{13,1},{2,6},{6,10},{... | collective-permute-start | bytes 3145736 | tf_op jit(solution)/shard_map/ppermute | solution.py:120
  11.2 172.4 %reduce-scatter.2.cloned.1.call-start = ((), (), s32[]{:S(2)}) async-start(), calls=%async_computation.1 | async-start | bytes 10485760 | tf_op jit(solution)/shard_map/reduce_scatter | solution.py:162
  19.3 20.9 %copy-start.1 = (bf16[4096,512]{1,0:T(8,128)(2,1)S(1)}, bf16[4096,512]{1,0:T(8,128)(2,1)}, u32[]{:S(2)}) copy-start(bf16[4096,512]{1,0:T(8,128)(2,1)} %param.12) | copy-start | bytes 12582916
  40.2 5.7 %copy-start.6 = (bf16[128,4096]{1,0:T(8,128)(2,1)S(1)}, bf16[128,4096]{1,0:T(8,128)(2,1)}, u32[]{:S(2)}) copy-start(bf16[128,4096]{1,0:T(8,128)(2,1)} %param.10) | copy-start | bytes 3145732
  43.0 26.4 %collective-permute-start.1 = (bf16[128,4096]{1,0:T(8,128)(2,1)}, bf16[128,4096]{1,0:T(8,128)(2,1)S(1)}, u32[]{:S(2)}, u32[]{:S(2)}) collective-permute-start(bf16[128,4096]{1,0:T(8,128)(2,1)} %collective-permute-done), channel_id=1, source_target_pairs={{0,4},{4,8},{8,12},{12,0},{1,5},{5,9},{9,13},{13,1},{2,6},{6,10},{... | collective-permute-start | bytes 3145736 | tf_op jit(solution)/shard_map/ppermute | solution.py:120
  65.5 1.5 copy-start.8
  69.3 16.0 %copy-start.3 = (bf16[4096,128]{1,0:T(8,128)(2,1)S(1)}, bf16[4096,128]{1,0:T(8,128)(2,1)}, u32[]{:S(2)}) copy-start(bf16[4096,128]{1,0:T(8,128)(2,1)} %param.14) | copy-start | bytes 3145732
  69.4 26.1 %collective-permute-start.2 = (bf16[128,4096]{1,0:T(8,128)(2,1)S(1)}, bf16[128,4096]{1,0:T(8,128)(2,1)S(1)}, u32[]{:S(2)}, u32[]{:S(2)}) collective-permute-start(bf16[128,4096]{1,0:T(8,128)(2,1)S(1)} %collective-permute-done.1), channel_id=1, source_target_pairs={{0,4},{4,8},{8,12},{12,0},{1,5},{5,9},{9,13},{13,1},{2,6},{6,10},{... | collective-permute-start | bytes 3145736 | tf_op jit(solution)/shard_map/ppermute | solution.py:120
  86.8 2.9 %copy-start.11 = (f32[128,32]{1,0:T(8,128)S(1)}, f32[128,32]{1,0:T(8,128)}, u32[]{:S(2)}) copy-start(f32[128,32]{1,0:T(8,128)} %copy.74) | copy-start | bytes 49156
  109.7 1.2 copy-start.4
  111.7 6.4 %copy-start.10 = (bf16[256,512]{1,0:T(8,128)(2,1)S(1)}, bf16[256,512]{1,0:T(8,128)(2,1)}, u32[]{:S(2)}) copy-start(bf16[256,512]{1,0:T(8,128)(2,1)} %param.16) | copy-start | bytes 786436
  116.8 3.8 %collective-permute-start.3 = (f32[2,128,576]{1,2,0:T(8,128)S(1)}, f32[2,128,576]{1,2,0:T(8,128)S(1)}, u32[]{:S(2)}, u32[]{:S(2)}) collective-permute-start(f32[2,128,576]{1,2,0:T(8,128)S(1)} %dynamic-slice_bitcast_fusion), channel_id=1, source_target_pairs={{0,1},{1,0},{2,3},{3,2},{4,5},{5,4},{6,7},{7,6},{8,9},{9,8},{10,11... | collective-permute-start | bytes 1769480 | tf_op jit(solution)/shard_map/ppermute | solution.py:86
  122.0 24.3 %copy-start.15 = (pred[512]{0:T(512)(128)(4,1)S(1)}, pred[512]{0:T(512)(128)(4,1)}, u32[]{:S(2)}) copy-start(pred[512]{0:T(512)(128)(4,1)} %get-tuple-element.87) | copy-start | bytes 1540
  122.0 24.3 %copy-start.16 = (pred[512]{0:T(512)(128)(4,1)S(1)}, pred[512]{0:T(512)(128)(4,1)}, u32[]{:S(2)}) copy-start(pred[512]{0:T(512)(128)(4,1)} %get-tuple-element.88) | copy-start | bytes 1540
  122.2 9.8 %collective-permute-start.4 = (f32[128,576]{1,0:T(8,128)S(1)}, f32[128,576]{1,0:T(8,128)S(1)}, u32[]{:S(2)}, u32[]{:S(2)}) collective-permute-start(f32[128,576]{1,0:T(8,128)S(1)} %bitcast.154), channel_id=1, source_target_pairs={{0,2},{2,0},{1,3},{3,1},{4,6},{6,4},{5,7},{7,5},{8,10},{10,8},{9,1... | collective-permute-start | bytes 884744 | tf_op jit(solution)/shard_map/ppermute | solution.py:86
  146.5 29.6 %copy-start.9 = (bf16[128,512]{1,0:T(8,128)(2,1)}, bf16[128,512]{1,0:T(8,128)(2,1)S(1)}, u32[]{:S(2)}) copy-start(bf16[128,512]{1,0:T(8,128)(2,1)S(1)} %fusion.25) | copy-start | bytes 393220
  186.5 4.6 %copy-start.7 = (bf16[512,4,128]{2,0,1:T(8,128)(2,1)S(1)}, bf16[512,4,128]{2,0,1:T(8,128)(2,1)}, u32[]{:S(2)}) copy-start(bf16[512,4,128]{2,0,1:T(8,128)(2,1)} %all_gather.22) | copy-start | bytes 1572868
  191.1 1.3 copy-start.12
  (2 other events, 1.2 us)
Sparse Core Ops, SparseCore 0:
  11.3 15.5 all-gather.2
Sparse Core Ops, SparseCore 1:
  109.8 73.7 reduce-scatter.1

commit v14 on v12

--- a/solution.py
+++ b/solution.py
@@ -30,6 +30,7 @@
     cosine = jnp.cos(angles)
     sine_angle = jnp.sin(angles)
     signed_sine = jnp.where((col % 2 == 0)[None, :], -sine_angle, sine_angle)
+    cosine, signed_sine = lax.optimization_barrier((cosine, signed_sine))
     cosine = jnp.tile(cosine, (1, cols // width))
     signed_sine = jnp.tile(signed_sine, (1, cols // width))
     is_even = (jnp.arange(cols, dtype=jnp.int32) % 2 == 0)[None, :]
@@ -68,6 +69,20 @@
         slot_hot[:, None, :], low_values[:, :, None], jnp.zeros((), low_values.dtype)
     )
     return wide_rows.reshape(low_values.shape[0], -1)
+
+
+def ring_gather(piece, axis):
+    count = lax.axis_size(axis)
+    me = lax.axis_index(axis)
+    if count == 1:
+        return piece
+    shift = [(i, (i + 1) % count) for i in range(count)]
+    pieces = [piece]
+    for _ in range(1, count):
+        pieces.append(lax.ppermute(pieces[-1], axis, shift))
+    stacked = jnp.stack(pieces)
+    order = (me - jnp.arange(count, dtype=jnp.int32)) % count
+    return jnp.take(stacked, order, axis=0).reshape((count * piece.shape[0],) + piece.shape[1:])
 
 
 def ring_reduce_scatter(blocks, axis):
@@ -183,8 +198,8 @@
         small_summed[:, keyval_cols : keyval_cols + rank_share], own_rank, first_rank
     )
     low_keyval = scale_ranks(small_summed[:, keyval_cols + rank_share :], own_rank, first_rank)
-    low_both = lax.all_gather(
-        jnp.concatenate([low_query, low_keyval], axis=1), "tensor", axis=1
+    low_both = jnp.moveaxis(
+        ring_gather(jnp.concatenate([low_query, low_keyval], axis=1)[None], "tensor"), 0, 1
     )
     full_query = low_both[:, :, :rank_share].reshape(block_rows, -1)
     full_keyval = low_both[:, :, rank_share:].reshape(block_rows, -1)

time: 208 us -> 210 us (level)
  waiting for transfers between devices: 46.7 us -> 63.8 us
  blocking collectives: 41.3 us -> 25 us
    ppermute x0 -> x3, waiting for transfers between devices: none -> 17 us  [ring_gather(): pieces.append(lax.ppermute(pieces[-1], axis, shift))]
    all_gather x1 -> x0, blocking collectives: 13.1 us -> none  [shards(): lax.all_gather(jnp.concatenate([low_query, low_keyval], axis=1), 'tensor'...]
    all_gather x1, blocking collectives: 10.8 us -> 7.23 us  [shards(): lax.all_gather(jnp.concatenate([key_heads, value_heads], axis=1), ('seq',...]
    unnamed x38 -> x36, local copies, waits for them, and re-layouts: 6.3 us -> 6.28 us
  transfers between devices with their start and end apart: 7 -> 10, of which waited for: 4 -> 7; matrix products, arithmetic and copies ran while one was open for 39% -> 39% of each run, Pallas kernels for 0% -> 0%
where the time goes in v14:
time: 210 us; the launch traced here: 209 us
  matrix products  64.8 us (31%)
  waiting for transfers between devices  63.8 us (30%)
  blocking collectives  25 us (12%)
  local copies, waits for them, and re-layouts  18.2 us (9%)
  other arithmetic  16.7 us (8%)
  between operations  16.4 us (8%)
  starting transfers between devices  4.56 us (2%)
    dot_general x11, matrix products, product(): return jnp.dot(left, right, preferred_element_type=jnp.float32)  62.8 us
    ppermute x3, waiting for transfers between devices, shards(): following = lax.ppermute(held, 'tensor', shift) if step < ring - 1 else None  31.4 us
    ppermute x3, waiting for transfers between devices, ring_gather(): pieces.append(lax.ppermute(pieces[-1], axis, shift))  17 us
    all_gather x1, blocking collectives, shards(): kv_all = lax.all_gather(kv_local, 'tensor', axis=1, tiled=True)  15.3 us
    ppermute x2, waiting for transfers between devices, ring_reduce_scatter(): total = lax.ppermute(total, axis, shift) + pick(step)  15.2 us
    all_gather x1, blocking collectives, shards(): lax.all_gather(jnp.concatenate([key_heads, value_heads], axis=1), ('seq',...  7.23 us
    unnamed x36, local copies, waits for them, and re-layouts  6.28 us
    sub x1, other arithmetic, shards(): exp_scores = jnp.where(visible, jnp.exp(scores - row_top[..., None]), 0.0)  4.59 us
  transfers between devices with their start and end apart: 10, of which 7 were waited for; matrix products, arithmetic and copies ran while one was open for 39% of the time, Pallas kernels for 0%

profile of v14, /device:TPU:0, one launch (start us, length us, event | category | flops | bytes accessed | tf_op | source)
XLA Modules:
  0.0 209.5 jit_solution(3298140219634324234)
XLA Ops:
  8.1 3.1 %collective-permute-start = (bf16[128,4096]{1,0:T(8,128)(2,1)}, bf16[128,4096]{1,0:T(8,128)(2,1)}, u32[]{:S(2)}, u32[]{:S(2)}) collective-permute-start(bf16[128,4096]{1,0:T(8,128)(2,1)} %param.10), channel_id=1, source_target_pairs={{0,4},{4,8},{8,12},{12,0},{1,5},{5,9},{9,13},{13,1},{2,6},{6,10},{... | collective-permute-start | bytes 3145736 | tf_op jit(solution)/shard_map/ppermute | solution.py:135
  12.8 1.7 fusion.54
  15.6 2.9 %fusion.53 = f32[128,512]{1,0:T(8,128)S(1)} fusion(bf16[128,4096]{1,0:T(8,128)(2,1)S(1)} %copy-done.3, bf16[4096,512]{1,0:T(8,128)(2,1)} %param.12), kind=kOutput, calls=%fused_computation.161 | convolution fusion | flops 536870912 | bytes 5505024 | tf_op jit(solution)/shard_map/dot_general | solution.py:19
  19.9 16.8 %collective-permute-done = bf16[128,4096]{1,0:T(8,128)(2,1)} collective-permute-done((bf16[128,4096]{1,0:T(8,128)(2,1)}, bf16[128,4096]{1,0:T(8,128)(2,1)}, u32[]{:S(2)}, u32[]{:S(2)}) %collective-permute-start) | collective-permute-done | bytes 1048608 | tf_op jit(solution)/shard_map/ppermute | solution.py:135
  36.7 15.4 %fusion.13 = f32[256,4096]{1,0:T(8,128)S(1)} fusion(bf16[4096,4096]{1,0:T(8,128)(2,1)} %param.11, bf16[128,4096]{1,0:T(8,128)(2,1)} %collective-permute-done, bf16[128,4096]{1,0:T(8,128)(2,1)S(1)} %copy-done.3), kind=kOutput, calls=%fused_computation.22 | convolution fusion | flops 8594128896 | bytes 39845888 | tf_op jit(solution)/shard_map/dot_general | solution.py:19
  52.0 4.2 %broadcast_in_dim.255 = f32[4,128,4096]{2,1,0:T(8,128)} broadcast(f32[]{:T(128)} %constant.213.clone.1), dimensions={} | broadcast | bytes 8388612 | tf_op jit(solution)/shard_map/broadcast_in_dim | solution.py:130
  59.3 3.7 %collective-permute-done.1 = bf16[128,4096]{1,0:T(8,128)(2,1)S(1)} collective-permute-done((bf16[128,4096]{1,0:T(8,128)(2,1)}, bf16[128,4096]{1,0:T(8,128)(2,1)S(1)}, u32[]{:S(2)}, u32[]{:S(2)}) %collective-permute-start.1) | collective-permute-done | bytes 1048608 | tf_op jit(solution)/shard_map/ppermute | solution.py:135
  63.0 14.2 %fusion.3 = f32[4,128,4096]{2,1,0:T(8,128)} fusion(f32[4,128,4096]{2,1,0:T(8,128)} %fusion.11, s32[]{:T(128)S(6)} %select_n.282, bf16[128,4096]{1,0:T(8,128)(2,1)S(1)} %collective-permute-done.1, bf16[4096,4096]{1,0:T(8,128)(2,1)} %param.11), kind=kOutput, calls=%fused_computation.8 | convolution fusion | flops 4294967296 | bytes 36700164 | tf_op jit(solution)/shard_map/dot_general | solution.py:19
  77.3 11.0 %collective-permute-done.2 = bf16[128,4096]{1,0:T(8,128)(2,1)S(1)} collective-permute-done((bf16[128,4096]{1,0:T(8,128)(2,1)S(1)}, bf16[128,4096]{1,0:T(8,128)(2,1)S(1)}, u32[]{:S(2)}, u32[]{:S(2)}) %collective-permute-start.2) | collective-permute-done | bytes 1048608 | tf_op jit(solution)/shard_map/ppermute | solution.py:135
  88.3 14.2 %fusion.2 = f32[4,128,4096]{2,1,0:T(8,128)} fusion(f32[4,128,4096]{2,1,0:T(8,128)} %fusion.3, s32[]{:T(128)S(6)} %select_n.287, bf16[128,4096]{1,0:T(8,128)(2,1)S(1)} %collective-permute-done.2, bf16[4096,4096]{1,0:T(8,128)(2,1)} %param.11), kind=kOutput, calls=%fused_computation.6 | convolution fusion | flops 4294967296 | bytes 36700164 | tf_op jit(solution)/shard_map/dot_general | solution.py:19
  105.8 1.6 copy-done.2
  108.6 3.7 %fusion.58 = f32[384,128]{0,1:T(8,128)S(1)} fusion(bf16[384,4096]{1,0:T(8,128)(2,1)} %copy-done.2, bf16[4096,128]{1,0:T(8,128)(2,1)S(1)} %copy-done.7), kind=kOutput, calls=%fused_computation.166 | convolution fusion | flops 402653184 | bytes 4390912 | tf_op jit(solution)/shard_map/dot_general | solution.py:19
  112.8 5.9 %fusion.56 = f32[384,512]{1,0:T(8,128)S(1)} fusion(bf16[384,4096]{1,0:T(8,128)(2,1)} %copy-done.2, bf16[4096,512]{1,0:T(8,128)(2,1)} %param.12), kind=kOutput, calls=%fused_computation.164 | convolution fusion | flops 1610612736 | bytes 8126464 | tf_op jit(solution)/shard_map/dot_general | solution.py:19
  120.4 2.5 %all_gather.12 = bf16[512,512]{1,0:T(8,128)(2,1)S(1)} all-gather(bf16[256,512]{1,0:T(8,128)(2,1)} %param.16), channel_id=1, replica_groups=mesh['groups'=2,'tensor'=4,'seq'=2,'load'=2] {'load'}, dimensions={0}, use_global_device_ids=true | all-gather | bytes 786432 | tf_op jit(solution)/shard_map/all_gather | solution.py:125
  125.8 15.2 %collective-permute-done.4 = f32[128,576]{1,0:T(8,128)S(1)} collective-permute-done((f32[128,576]{1,0:T(8,128)S(1)}, f32[128,576]{1,0:T(8,128)S(1)}, u32[]{:S(2)}, u32[]{:S(2)}) %collective-permute-start.4) | collective-permute-done | bytes 294944 | tf_op jit(solution)/shard_map/ppermute | solution.py:100
  141.4 5.7 %collective-permute-done.5 = bf16[1,128,64]{2,1,0:T(8,128)(2,1)S(1)} collective-permute-done((bf16[1,128,64]{2,1,0:T(8,128)(2,1)S(1)}, bf16[1,128,64]{2,1,0:T(8,128)(2,1)S(1)}, u32[]{:S(2)}, u32[]{:S(2)}) %collective-permute-start.5) | collective-permute-done | bytes 16416 | tf_op jit(solution)/shard_map/ppermute | solution.py:82
  147.1 5.7 %collective-permute-done.6 = bf16[1,128,64]{2,1,0:T(8,128)(2,1)S(1)} collective-permute-done((bf16[1,128,64]{2,1,0:T(8,128)(2,1)S(1)}, bf16[1,128,64]{2,1,0:T(8,128)(2,1)S(1)}, u32[]{:S(2)}, u32[]{:S(2)}) %collective-permute-start.6) | collective-permute-done | bytes 16416 | tf_op jit(solution)/shard_map/ppermute | solution.py:82
  152.8 5.7 %collective-permute-done.7 = bf16[1,128,64]{2,1,0:T(8,128)(2,1)S(1)} collective-permute-done((bf16[1,128,64]{2,1,0:T(8,128)(2,1)S(1)}, bf16[1,128,64]{2,1,0:T(8,128)(2,1)S(1)}, u32[]{:S(2)}, u32[]{:S(2)}) %collective-permute-start.7) | collective-permute-done | bytes 16416 | tf_op jit(solution)/shard_map/ppermute | solution.py:82
  160.5 15.3 %all_gather.13 = bf16[128,2048]{1,0:T(8,128)(2,1)S(1)} all-gather(bf16[128,512]{1,0:T(8,128)(2,1)S(1)} %fusion.25), channel_id=1, replica_groups=mesh['groups'=2,'tensor'=4,'seq'=2,'load'=2] {'tensor'}, dimensions={1}, use_global_device_ids=true | all-gather | bytes 655360 | tf_op jit(solution)/shard_map/all_gather | solution.py:215
  176.3 7.2 %all_gather.14 = bf16[512,4,128]{2,0,1:T(8,128)(2,1)} all-gather(bf16[128,4,128]{2,0,1:T(8,128)(2,1)S(1)} %pad_maximum_fusion.1), channel_id=1, replica_groups=mesh['groups'=2,'tensor'=4,'seq'=2,'load'=2] {'seq','load'}, dimensions={0}, use_global_device_ids=true | all-gather | bytes 655360 | tf_op jit(solution)/shard_map/all_gather | solution.py:228
  183.5 2.9 %fusion.59 = f32[128,4096]{1,0:T(8,128)S(1)} fusion(bf16[128,512]{0,1:T(8,128)(2,1)S(1)} %bitcast.152, bf16[512,4096]{1,0:T(8,128)(2,1)} %all-gather.2.cloned.1.call-done), kind=kOutput, calls=%fused_computation.167 | convolution fusion | flops 536870912 | bytes 6422528 | tf_op jit(solution)/shard_map/dot_general | solution.py:19
  186.5 1.8 add.337
  189.4 4.4 %fusion.22 = bf16[16,8,32,128]{3,1,2,0:T(8,128)(2,1)S(1)} fusion(f32[16,8,32,128]{3,2,1,0:T(8,128)S(1)} %bitcast.146, f32[128,4095]{1,0:T(8,128)S(1)} %get-tuple-element.47, f32[128,1]{1,0:T(8,128)S(1)} %get-tuple-element.49, f32[128,1]{1,0:T(8,128)S(1)} %get-tuple-element.48, f32[128,4095]{1,0:T(8,128)S(1)} %get-tuple-element.46, f32[128,4096]{1,0:T(8,128)S(1)} %add.337, ...), kind=kLoop, calls=%fused_computation.31 | loop fusion | flops 3670016 | bytes 11538432
  195.4 4.6 %fusion.52 = (f32[2,16,128]{2,1,0:T(8,128)S(1)}, bf16[2,16,128,512]{2,3,1,0:T(8,128)(2,1)S(1)}) fusion(f32[2,512,128,16]{2,1,3,0:T(8,128)S(1)} %fusion.20, pred[128,512]{0,1:T(8,128)(4,1)S(1)} %copy-done.10), kind=kOutput, calls=%fused_computation.160 | output fusion | flops 16777728 | bytes 12664832 | tf_op jit(solution)/shard_map/sub | solution.py:245
  (130 shorter events, 23.7 us)
Async XLA Ops:
  8.0 4.8 %copy-start = (bf16[4096,128]{1,0:T(8,128)(2,1)S(1)}, bf16[4096,128]{1,0:T(8,128)(2,1)}, u32[]{:S(2)}) copy-start(bf16[4096,128]{1,0:T(8,128)(2,1)} %param.13) | copy-start | bytes 3145732
  8.0 6.7 %copy-start.3 = (bf16[128,4096]{1,0:T(8,128)(2,1)S(1)}, bf16[128,4096]{1,0:T(8,128)(2,1)}, u32[]{:S(2)}) copy-start(bf16[128,4096]{1,0:T(8,128)(2,1)} %param.10) | copy-start | bytes 3145732
  8.0 6.5 %copy-start.14 = (s32[4]{0:T(128)S(1)}, s32[4]{0:T(128)}, u32[]{:S(2)}) copy-start(s32[4]{0:T(128)} %param.17) | copy-start | bytes 52
  8.0 6.5 %copy-start.12 = (s32[4]{0:T(128)S(1)}, s32[4]{0:T(128)}, u32[]{:S(2)}) copy-start(s32[4]{0:T(128)} %param.19) | copy-start | bytes 52
  8.0 6.7 %copy-start.6 = (bf16[4096,128]{1,0:T(8,128)(2,1)S(1)}, bf16[4096,128]{1,0:T(8,128)(2,1)}, u32[]{:S(2)}) copy-start(bf16[4096,128]{1,0:T(8,128)(2,1)} %param.14) | copy-start | bytes 3145732
  8.1 175.4 %all-gather.2.cloned.1.call-start = ((), (), s32[]{:S(2)}) async-start(), calls=%async_computation.2 | async-start | bytes 6291456 | tf_op jit(solution)/shard_map/all_gather | solution.py:124
  8.1 28.6 %collective-permute-start = (bf16[128,4096]{1,0:T(8,128)(2,1)}, bf16[128,4096]{1,0:T(8,128)(2,1)}, u32[]{:S(2)}, u32[]{:S(2)}) collective-permute-start(bf16[128,4096]{1,0:T(8,128)(2,1)} %param.10), channel_id=1, source_target_pairs={{0,4},{4,8},{8,12},{12,0},{1,5},{5,9},{9,13},{13,1},{2,6},{6,10},{... | collective-permute-start | bytes 3145736 | tf_op jit(solution)/shard_map/ppermute | solution.py:135
  11.2 175.3 %reduce-scatter.2.cloned.1.call-start = ((), (), s32[]{:S(2)}) async-start(), calls=%async_computation.1 | async-start | bytes 10485760 | tf_op jit(solution)/shard_map/reduce_scatter | solution.py:188
  36.7 26.4 %collective-permute-start.1 = (bf16[128,4096]{1,0:T(8,128)(2,1)}, bf16[128,4096]{1,0:T(8,128)(2,1)S(1)}, u32[]{:S(2)}, u32[]{:S(2)}) collective-permute-start(bf16[128,4096]{1,0:T(8,128)(2,1)} %collective-permute-done), channel_id=1, source_target_pairs={{0,4},{4,8},{8,12},{12,0},{1,5},{5,9},{9,13},{13,1},{2,6},{6,10},{... | collective-permute-start | bytes 3145736 | tf_op jit(solution)/shard_map/ppermute | solution.py:135
  63.0 25.2 %collective-permute-start.2 = (bf16[128,4096]{1,0:T(8,128)(2,1)S(1)}, bf16[128,4096]{1,0:T(8,128)(2,1)S(1)}, u32[]{:S(2)}, u32[]{:S(2)}) collective-permute-start(bf16[128,4096]{1,0:T(8,128)(2,1)S(1)} %collective-permute-done.1), channel_id=1, source_target_pairs={{0,4},{4,8},{8,12},{12,0},{1,5},{5,9},{9,13},{13,1},{2,6},{6,10},{... | collective-permute-start | bytes 3145736 | tf_op jit(solution)/shard_map/ppermute | solution.py:135
  105.7 2.8 %copy-start.7 = (bf16[4096,128]{1,0:T(8,128)(2,1)S(1)}, bf16[4096,128]{1,0:T(8,128)(2,1)}, u32[]{:S(2)}) copy-start(bf16[4096,128]{1,0:T(8,128)(2,1)} %param.14) | copy-start | bytes 3145732
  105.8 1.6 copy-start.2
  120.1 5.0 %copy-start.11 = (f32[128]{0:T(128)S(1)}, f32[128]{0:T(128)}, u32[]{:S(2)}) copy-start(f32[128]{0:T(128)} %get-tuple-element.76) | copy-start | bytes 1540
  120.2 3.4 %collective-permute-start.3 = (f32[2,128,576]{1,2,0:T(8,128)S(1)}, f32[2,128,576]{1,2,0:T(8,128)S(1)}, u32[]{:S(2)}, u32[]{:S(2)}) collective-permute-start(f32[2,128,576]{1,2,0:T(8,128)S(1)} %dynamic-slice_bitcast_fusion), channel_id=1, source_target_pairs={{0,1},{1,0},{2,3},{3,2},{4,5},{5,4},{6,7},{7,6},{8,9},{9,8},{10,11... | collective-permute-start | bytes 1769480 | tf_op jit(solution)/shard_map/ppermute | solution.py:100
  120.3 20.8 %copy-start.13 = (f32[128]{0:T(128)S(1)}, f32[128]{0:T(128)}, u32[]{:S(2)}) copy-start(f32[128]{0:T(128)} %rsqrt_multiply_fusion) | copy-start | bytes 1540
  120.3 21.0 %copy-start.15 = (s32[4]{0:T(128)S(1)}, s32[4]{0:T(128)}, u32[]{:S(2)}) copy-start(s32[4]{0:T(128)} %fusion.43) | copy-start | bytes 52
  123.8 17.2 %collective-permute-start.4 = (f32[128,576]{1,0:T(8,128)S(1)}, f32[128,576]{1,0:T(8,128)S(1)}, u32[]{:S(2)}, u32[]{:S(2)}) collective-permute-start(f32[128,576]{1,0:T(8,128)S(1)} %bitcast.154), channel_id=1, source_target_pairs={{0,2},{2,0},{1,3},{3,1},{4,6},{6,4},{5,7},{7,5},{8,10},{10,8},{9,1... | collective-permute-start | bytes 884744 | tf_op jit(solution)/shard_map/ppermute | solution.py:100
  141.3 5.8 %collective-permute-start.5 = (bf16[1,128,64]{2,1,0:T(8,128)(2,1)S(1)}, bf16[1,128,64]{2,1,0:T(8,128)(2,1)S(1)}, u32[]{:S(2)}, u32[]{:S(2)}) collective-permute-start(bf16[1,128,64]{2,1,0:T(8,128)(2,1)S(1)} %get-tuple-element.66), channel_id=1, source_target_pairs={{0,4},{4,8},{8,12},{12,0},{1,5},{5,9},{9,13},{13,1},{2,6},{6,10},{... | collective-permute-start | bytes 49160 | tf_op jit(solution)/shard_map/ppermute | solution.py:82
  147.1 5.7 %collective-permute-start.6 = (bf16[1,128,64]{2,1,0:T(8,128)(2,1)S(1)}, bf16[1,128,64]{2,1,0:T(8,128)(2,1)S(1)}, u32[]{:S(2)}, u32[]{:S(2)}) collective-permute-start(bf16[1,128,64]{2,1,0:T(8,128)(2,1)S(1)} %collective-permute-done.5), channel_id=1, source_target_pairs={{0,4},{4,8},{8,12},{12,0},{1,5},{5,9},{9,13},{13,1},{2,6},{6,10},{... | collective-permute-start | bytes 49160 | tf_op jit(solution)/shard_map/ppermute | solution.py:82
  152.8 5.7 %collective-permute-start.7 = (bf16[1,128,64]{2,1,0:T(8,128)(2,1)S(1)}, bf16[1,128,64]{2,1,0:T(8,128)(2,1)S(1)}, u32[]{:S(2)}, u32[]{:S(2)}) collective-permute-start(bf16[1,128,64]{2,1,0:T(8,128)(2,1)S(1)} %collective-permute-done.6), channel_id=1, source_target_pairs={{0,4},{4,8},{8,12},{12,0},{1,5},{5,9},{9,13},{13,1},{2,6},{6,10},{... | collective-permute-start | bytes 49160 | tf_op jit(solution)/shard_map/ppermute | solution.py:82
  160.4 26.0 %copy-start.9 = (bf16[128,512]{1,0:T(8,128)(2,1)}, bf16[128,512]{1,0:T(8,128)(2,1)S(1)}, u32[]{:S(2)}) copy-start(bf16[128,512]{1,0:T(8,128)(2,1)S(1)} %fusion.25) | copy-start | bytes 393220
  189.4 4.6 %copy-start.8 = (bf16[512,4,128]{2,0,1:T(8,128)(2,1)S(1)}, bf16[512,4,128]{2,0,1:T(8,128)(2,1)}, u32[]{:S(2)}) copy-start(bf16[512,4,128]{2,0,1:T(8,128)(2,1)} %all_gather.14) | copy-start | bytes 1572868
  194.1 1.3 copy-start.10
  200.0 2.1 %copy-start.1 = (bf16[4096,128]{1,0:T(8,128)(2,1)S(1)}, bf16[4096,128]{1,0:T(8,128)(2,1)}, u32[]{:S(2)}) copy-start(bf16[4096,128]{1,0:T(8,128)(2,1)} %param.13) | copy-start | bytes 3145732
  (2 other events, 2.3 us)
Sparse Core Ops, SparseCore 0:
  11.3 15.5 all-gather.1
Sparse Core Ops, SparseCore 1:
  102.6 76.3 reduce-scatter.1

commit v15 on v12

--- a/solution.py
+++ b/solution.py
@@ -30,6 +30,7 @@
     cosine = jnp.cos(angles)
     sine_angle = jnp.sin(angles)
     signed_sine = jnp.where((col % 2 == 0)[None, :], -sine_angle, sine_angle)
+    cosine, signed_sine = lax.optimization_barrier((cosine, signed_sine))
     cosine = jnp.tile(cosine, (1, cols // width))
     signed_sine = jnp.tile(signed_sine, (1, cols // width))
     is_even = (jnp.arange(cols, dtype=jnp.int32) % 2 == 0)[None, :]
@@ -119,8 +120,7 @@
     for step in range(ring):
         following = lax.ppermute(held, "tensor", shift) if step < ring - 1 else None
         owner = (tensor_index - step) % ring
-        defer = 0 < step < ring - 1 and ring <= 4
-        if defer:
+        if step == 1 and ring > 2:
             waiting.append((held, owner))
         else:
             batch = waiting + [(held, owner)] if step == ring - 1 else [(held, owner)]

time: 208 us -> 208 us (level)
  waiting for transfers between devices: 46.7 us -> 41.4 us
  matrix products: 64.8 us -> 67.3 us
    ppermute x3, waiting for transfers between devices: 31.4 us -> 28.5 us  [shards(): following = lax.ppermute(held, 'tensor', shift) if step < ring - 1 else None]
    dot_general x11 -> x14, matrix products: 62.7 us -> 65.2 us  [product(): return jnp.dot(left, right, preferred_element_type=jnp.float32)]
    ppermute x2, waiting for transfers between devices: 15.3 us -> 12.9 us  [ring_reduce_scatter(): total = lax.ppermute(total, axis, shift) + pick(step)]
    unnamed x38 -> x41, local copies, waits for them, and re-layouts: 6.3 us -> 5.01 us
  transfers between devices with their start and end apart: 7 -> 7, of which waited for: 4 -> 4; matrix products, arithmetic and copies ran while one was open for 39% -> 41% of each run, Pallas kernels for 0% -> 0%
where the time goes in v15:
time: 208 us
  matrix products  67.3 us (32%)
  blocking collectives  43 us (21%)
  waiting for transfers between devices  41.4 us (20%)
  local copies, waits for them, and re-layouts  18.2 us (9%)
  other arithmetic  17.1 us (8%)
  between operations  16.3 us (8%)
  starting transfers between devices  4.61 us (2%)
    dot_general x14, matrix products, product(): return jnp.dot(left, right, preferred_element_type=jnp.float32)  65.2 us
    ppermute x3, waiting for transfers between devices, shards(): following = lax.ppermute(held, 'tensor', shift) if step < ring - 1 else None  28.5 us
    all_gather x1, blocking collectives, shards(): kv_all = lax.all_gather(kv_local, 'tensor', axis=1, tiled=True)  15.9 us
    all_gather x1, blocking collectives, shards(): lax.all_gather(jnp.concatenate([low_query, low_keyval], axis=1), 'tensor'...  13.2 us
    ppermute x2, waiting for transfers between devices, ring_reduce_scatter(): total = lax.ppermute(total, axis, shift) + pick(step)  12.9 us
    all_gather x1, blocking collectives, shards(): lax.all_gather(jnp.concatenate([key_heads, value_heads], axis=1), ('seq',...  11.5 us
    unnamed x41, local copies, waits for them, and re-layouts  5.01 us
    sub x1, other arithmetic, shards(): exp_scores = jnp.where(visible, jnp.exp(scores - row_top[..., None]), 0.0)  4.59 us
  transfers between devices with their start and end apart: 7, of which 4 were waited for; matrix products, arithmetic and copies ran while one was open for 41% of the time, Pallas kernels for 0%

profile of v15, /device:TPU:0, one launch (start us, length us, event | category | flops | bytes accessed | tf_op | source)
XLA Modules:
  0.0 207.9 jit_solution(16079708099475719391)
XLA Ops:
  8.1 3.1 %collective-permute-start = (bf16[128,4096]{1,0:T(8,128)(2,1)}, bf16[128,4096]{1,0:T(8,128)(2,1)}, u32[]{:S(2)}, u32[]{:S(2)}) collective-permute-start(bf16[128,4096]{1,0:T(8,128)(2,1)} %param.10), channel_id=1, source_target_pairs={{0,4},{4,8},{8,12},{12,0},{1,5},{5,9},{9,13},{13,1},{2,6},{6,10},{... | collective-permute-start | bytes 3145736 | tf_op jit(solution)/shard_map/ppermute | solution.py:121
  13.1 2.9 %fusion.48 = f32[128,512]{1,0:T(8,128)S(1)} fusion(bf16[128,4096]{1,0:T(8,128)(2,1)S(1)} %copy-done.3, bf16[4096,512]{1,0:T(8,128)(2,1)} %param.12), kind=kOutput, calls=%fused_computation.146 | convolution fusion | flops 536870912 | bytes 5505024 | tf_op jit(solution)/shard_map/dot_general | solution.py:19
  17.4 19.3 %collective-permute-done = bf16[128,4096]{1,0:T(8,128)(2,1)} collective-permute-done((bf16[128,4096]{1,0:T(8,128)(2,1)}, bf16[128,4096]{1,0:T(8,128)(2,1)}, u32[]{:S(2)}, u32[]{:S(2)}) %collective-permute-start) | collective-permute-done | bytes 1048608 | tf_op jit(solution)/shard_map/ppermute | solution.py:121
  36.7 15.7 %fusion.13 = f32[256,4096]{1,0:T(8,128)S(1)} fusion(bf16[4096,4096]{1,0:T(8,128)(2,1)} %param.11, bf16[128,4096]{1,0:T(8,128)(2,1)} %collective-permute-done, bf16[128,4096]{1,0:T(8,128)(2,1)} %param.10), kind=kOutput, calls=%fused_computation.21 | convolution fusion | flops 8594128896 | bytes 39845888 | tf_op jit(solution)/shard_map/dot_general | solution.py:19
  52.3 4.2 %broadcast_in_dim.265 = f32[4,128,4096]{2,1,0:T(8,128)} broadcast(f32[]{:T(128)} %constant.192.clone.1), dimensions={} | broadcast | bytes 8388612 | tf_op jit(solution)/shard_map/broadcast_in_dim | solution.py:116
  56.6 1.5 fusion.12
  58.1 1.5 fusion.11
  59.6 3.4 %collective-permute-done.1 = bf16[128,4096]{1,0:T(8,128)(2,1)S(1)} collective-permute-done((bf16[128,4096]{1,0:T(8,128)(2,1)}, bf16[128,4096]{1,0:T(8,128)(2,1)S(1)}, u32[]{:S(2)}, u32[]{:S(2)}) %collective-permute-start.1) | collective-permute-done | bytes 1048608 | tf_op jit(solution)/shard_map/ppermute | solution.py:121
  63.0 14.2 %fusion.3 = f32[4,128,4096]{2,1,0:T(8,128)} fusion(f32[4,128,4096]{2,1,0:T(8,128)} %fusion.11, s32[]{:T(128)S(6)} %select_n.254, bf16[128,4096]{1,0:T(8,128)(2,1)S(1)} %collective-permute-done.1, bf16[4096,4096]{1,0:T(8,128)(2,1)} %param.11), kind=kOutput, calls=%fused_computation.7 | convolution fusion | flops 4294967296 | bytes 36700164 | tf_op jit(solution)/shard_map/dot_general | solution.py:19
  78.6 2.9 %fusion.51 = f32[128,512]{1,0:T(8,128)S(1)} fusion(bf16[128,4096]{1,0:T(8,128)(2,1)S(1)} %collective-permute-done.1, bf16[4096,512]{1,0:T(8,128)(2,1)} %param.12), kind=kOutput, calls=%fused_computation.149 | convolution fusion | flops 536870912 | bytes 5505024 | tf_op jit(solution)/shard_map/dot_general | solution.py:19
  82.5 5.8 %collective-permute-done.2 = bf16[128,4096]{1,0:T(8,128)(2,1)} collective-permute-done((bf16[128,4096]{1,0:T(8,128)(2,1)S(1)}, bf16[128,4096]{1,0:T(8,128)(2,1)}, u32[]{:S(2)}, u32[]{:S(2)}) %collective-permute-start.2) | collective-permute-done | bytes 1048608 | tf_op jit(solution)/shard_map/ppermute | solution.py:121
  88.4 16.7 %fusion.2 = f32[4,128,4096]{2,1,0:T(8,128)} fusion(f32[4,128,4096]{2,1,0:T(8,128)} %fusion.3, s32[]{:T(128)S(6)} %select_n.259, bf16[128,4096]{1,0:T(8,128)(2,1)} %collective-permute-done.2, bf16[4096,4096]{1,0:T(8,128)(2,1)} %param.11), kind=kOutput, calls=%fused_computation.5 | convolution fusion | flops 4294967296 | bytes 36700164 | tf_op jit(solution)/shard_map/dot_general | solution.py:19
  110.4 2.3 %fusion.56 = f32[256,128]{0,1:T(8,128)S(1)} fusion(bf16[256,4096]{1,0:T(8,128)(2,1)S(1)} %constant_dynamic-update-slice_fusion, bf16[4096,128]{1,0:T(8,128)(2,1)} %param.14), kind=kOutput, calls=%fused_computation.154 | convolution fusion | flops 268435456 | bytes 3276800 | tf_op jit(solution)/shard_map/dot_general | solution.py:19
  113.1 4.3 %fusion.54 = f32[256,512]{1,0:T(8,128)S(1)} fusion(bf16[256,4096]{1,0:T(8,128)(2,1)S(1)} %constant_dynamic-update-slice_fusion, bf16[4096,512]{1,0:T(8,128)(2,1)} %param.12), kind=kOutput, calls=%fused_computation.152 | convolution fusion | flops 1073741824 | bytes 6815744 | tf_op jit(solution)/shard_map/dot_general | solution.py:19
  120.8 2.5 %all_gather.20 = bf16[512,512]{1,0:T(8,128)(2,1)S(1)} all-gather(bf16[256,512]{1,0:T(8,128)(2,1)} %param.16), channel_id=1, replica_groups=mesh['groups'=2,'tensor'=4,'seq'=2,'load'=2] {'load'}, dimensions={0}, use_global_device_ids=true | all-gather | bytes 786432 | tf_op jit(solution)/shard_map/all_gather | solution.py:111
  123.6 1.4 collective-permute-start.4
  125.8 12.8 %collective-permute-done.4 = f32[128,576]{1,0:T(8,128)S(1)} collective-permute-done((f32[128,576]{1,0:T(8,128)S(1)}, f32[128,576]{1,0:T(8,128)S(1)}, u32[]{:S(2)}, u32[]{:S(2)}) %collective-permute-start.4) | collective-permute-done | bytes 294944 | tf_op jit(solution)/shard_map/ppermute | solution.py:86
  139.1 13.2 %all-gather = bf16[128,256]{0,1:T(8,128)(2,1)S(1)} all-gather(bf16[128,64]{0,1:T(8,128)(2,1)S(1)} %copy.75), channel_id=2, replica_groups=mesh['groups'=2,'tensor'=4,'seq'=2,'load'=2] {'tensor'}, dimensions={1}, use_global_device_ids=true | all-gather | bytes 81920 | tf_op jit(solution)/shard_map/all_gather | solution.py:186
  153.2 15.9 %all_gather.21 = bf16[128,2048]{1,0:T(8,128)(2,1)S(1)} all-gather(bf16[128,512]{1,0:T(8,128)(2,1)S(1)} %fusion.25), channel_id=1, replica_groups=mesh['groups'=2,'tensor'=4,'seq'=2,'load'=2] {'tensor'}, dimensions={1}, use_global_device_ids=true | all-gather | bytes 655360 | tf_op jit(solution)/shard_map/all_gather | solution.py:200
  169.6 11.5 %all_gather.22 = bf16[512,4,128]{2,0,1:T(8,128)(2,1)} all-gather(bf16[128,4,128]{2,0,1:T(8,128)(2,1)S(1)} %pad_maximum_fusion.1), channel_id=1, replica_groups=mesh['groups'=2,'tensor'=4,'seq'=2,'load'=2] {'seq','load'}, dimensions={0}, use_global_device_ids=true | all-gather | bytes 655360 | tf_op jit(solution)/shard_map/all_gather | solution.py:213
  181.1 3.0 %fusion.57 = f32[128,4096]{1,0:T(8,128)S(1)} fusion(bf16[128,512]{0,1:T(8,128)(2,1)S(1)} %bitcast.148, bf16[512,4096]{1,0:T(8,128)(2,1)} %all-gather.3.cloned.1.call-done), kind=kOutput, calls=%fused_computation.155 | convolution fusion | flops 536870912 | bytes 6422528 | tf_op jit(solution)/shard_map/dot_general | solution.py:19
  184.2 1.8 add.305
  187.1 4.4 %fusion.22 = bf16[16,8,32,128]{3,1,2,0:T(8,128)(2,1)S(1)} fusion(f32[16,8,32,128]{3,2,1,0:T(8,128)S(1)} %bitcast.142, f32[128,4095]{1,0:T(8,128)S(1)} %get-tuple-element.52, f32[128,1]{1,0:T(8,128)S(1)} %get-tuple-element.54, f32[128,1]{1,0:T(8,128)S(1)} %get-tuple-element.53, f32[128,4095]{1,0:T(8,128)S(1)} %get-tuple-element.51, f32[128,4096]{1,0:T(8,128)S(1)} %add.305, ...), kind=kLoop, calls=%fused_computation.30 | loop fusion | flops 3670016 | bytes 11538432
  193.8 4.6 %fusion.47 = (f32[2,16,128]{2,1,0:T(8,128)S(1)}, bf16[2,16,128,512]{2,3,1,0:T(8,128)(2,1)S(1)}) fusion(f32[2,512,128,16]{2,1,3,0:T(8,128)S(1)} %fusion.20, pred[128,512]{0,1:T(8,128)(4,1)S(1)} %copy-done.9), kind=kOutput, calls=%fused_computation.145 | output fusion | flops 16777728 | bytes 12664832 | tf_op jit(solution)/shard_map/sub | solution.py:230
  (132 shorter events, 22.7 us)
Async XLA Ops:
  8.0 3.5 %copy-start = (bf16[4096,128]{1,0:T(8,128)(2,1)S(1)}, bf16[4096,128]{1,0:T(8,128)(2,1)}, u32[]{:S(2)}) copy-start(bf16[4096,128]{1,0:T(8,128)(2,1)} %param.13) | copy-start | bytes 3145732
  8.0 3.5 %copy-start.3 = (bf16[128,4096]{1,0:T(8,128)(2,1)S(1)}, bf16[128,4096]{1,0:T(8,128)(2,1)}, u32[]{:S(2)}) copy-start(bf16[128,4096]{1,0:T(8,128)(2,1)} %param.10) | copy-start | bytes 3145732
  8.0 3.3 %copy-start.18 = (s32[4]{0:T(128)S(1)}, s32[4]{0:T(128)}, u32[]{:S(2)}) copy-start(s32[4]{0:T(128)} %param.18) | copy-start | bytes 52
  8.0 4.0 %copy-start.2 = (bf16[4096,128]{1,0:T(8,128)(2,1)S(1)}, bf16[4096,128]{1,0:T(8,128)(2,1)}, u32[]{:S(2)}) copy-start(bf16[4096,128]{1,0:T(8,128)(2,1)} %param.14) | copy-start | bytes 3145732
  8.0 173.1 %all-gather.3.cloned.1.call-start = ((), (), s32[]{:S(2)}) async-start(), calls=%async_computation.2 | async-start | bytes 6291456 | tf_op jit(solution)/shard_map/all_gather | solution.py:110
  8.1 28.6 %collective-permute-start = (bf16[128,4096]{1,0:T(8,128)(2,1)}, bf16[128,4096]{1,0:T(8,128)(2,1)}, u32[]{:S(2)}, u32[]{:S(2)}) collective-permute-start(bf16[128,4096]{1,0:T(8,128)(2,1)} %param.10), channel_id=1, source_target_pairs={{0,4},{4,8},{8,12},{12,0},{1,5},{5,9},{9,13},{13,1},{2,6},{6,10},{... | collective-permute-start | bytes 3145736 | tf_op jit(solution)/shard_map/ppermute | solution.py:121
  11.2 173.0 %reduce-scatter.2.cloned.1.call-start = ((), (), s32[]{:S(2)}) async-start(), calls=%async_computation.1 | async-start | bytes 10485760 | tf_op jit(solution)/shard_map/reduce_scatter | solution.py:173
  11.5 1.1 copy-start.12
  11.5 1.1 copy-start.17
  36.7 26.4 %collective-permute-start.1 = (bf16[128,4096]{1,0:T(8,128)(2,1)}, bf16[128,4096]{1,0:T(8,128)(2,1)S(1)}, u32[]{:S(2)}, u32[]{:S(2)}) collective-permute-start(bf16[128,4096]{1,0:T(8,128)(2,1)} %collective-permute-done), channel_id=1, source_target_pairs={{0,4},{4,8},{8,12},{12,0},{1,5},{5,9},{9,13},{13,1},{2,6},{6,10},{... | collective-permute-start | bytes 3145736 | tf_op jit(solution)/shard_map/ppermute | solution.py:121
  63.0 25.3 %collective-permute-start.2 = (bf16[128,4096]{1,0:T(8,128)(2,1)S(1)}, bf16[128,4096]{1,0:T(8,128)(2,1)}, u32[]{:S(2)}, u32[]{:S(2)}) collective-permute-start(bf16[128,4096]{1,0:T(8,128)(2,1)S(1)} %collective-permute-done.1), channel_id=1, source_target_pairs={{0,4},{4,8},{8,12},{12,0},{1,5},{5,9},{9,13},{13,1},{2,6},{6,10},{... | collective-permute-start | bytes 3145736 | tf_op jit(solution)/shard_map/ppermute | solution.py:121
  117.5 1.3 copy-start.5
  117.6 1.4 copy-start.11
  117.7 1.4 copy-start.15
  117.7 1.4 copy-start.16
  118.9 4.4 %collective-permute-start.3 = (f32[2,128,576]{1,2,0:T(8,128)S(1)}, f32[2,128,576]{1,2,0:T(8,128)S(1)}, u32[]{:S(2)}, u32[]{:S(2)}) collective-permute-start(f32[2,128,576]{1,2,0:T(8,128)S(1)} %dynamic-slice_bitcast_fusion), channel_id=1, source_target_pairs={{0,1},{1,0},{2,3},{3,2},{4,5},{5,4},{6,7},{7,6},{8,9},{9,8},{10,11... | collective-permute-start | bytes 1769480 | tf_op jit(solution)/shard_map/ppermute | solution.py:86
  123.4 28.9 %copy-start.10 = (pred[128,4]{0,1:T(4,128)(4,1)S(1)}, pred[128,4]{0,1:T(4,128)(4,1)}, u32[]{:S(2)}) copy-start(pred[128,4]{0,1:T(4,128)(4,1)} %get-tuple-element.79) | copy-start | bytes 1540
  123.6 15.1 %collective-permute-start.4 = (f32[128,576]{1,0:T(8,128)S(1)}, f32[128,576]{1,0:T(8,128)S(1)}, u32[]{:S(2)}, u32[]{:S(2)}) collective-permute-start(f32[128,576]{1,0:T(8,128)S(1)} %bitcast.150), channel_id=1, source_target_pairs={{0,2},{2,0},{1,3},{3,1},{4,6},{6,4},{5,7},{7,5},{8,10},{10,8},{9,1... | collective-permute-start | bytes 884744 | tf_op jit(solution)/shard_map/ppermute | solution.py:86
  125.8 27.0 %copy-start.8 = (f32[128,128]{1,0:T(8,128)S(1)}, f32[128,128]{1,0:T(8,128)}, u32[]{:S(2)}) copy-start(f32[128,128]{1,0:T(8,128)} %get-tuple-element.23) | copy-start | bytes 196612
  138.7 14.3 %copy-start.13 = (pred[512]{0:T(512)(128)(4,1)S(1)}, pred[512]{0:T(512)(128)(4,1)}, u32[]{:S(2)}) copy-start(pred[512]{0:T(512)(128)(4,1)} %get-tuple-element.81) | copy-start | bytes 1540
  138.7 14.3 %copy-start.14 = (pred[512]{0:T(512)(128)(4,1)S(1)}, pred[512]{0:T(512)(128)(4,1)}, u32[]{:S(2)}) copy-start(pred[512]{0:T(512)(128)(4,1)} %get-tuple-element.82) | copy-start | bytes 1540
  153.2 30.9 %copy-start.7 = (bf16[128,512]{1,0:T(8,128)(2,1)}, bf16[128,512]{1,0:T(8,128)(2,1)S(1)}, u32[]{:S(2)}) copy-start(bf16[128,512]{1,0:T(8,128)(2,1)S(1)} %fusion.25) | copy-start | bytes 393220
  192.5 1.3 copy-start.9
  198.4 2.1 %copy-start.1 = (bf16[4096,128]{1,0:T(8,128)(2,1)S(1)}, bf16[4096,128]{1,0:T(8,128)(2,1)}, u32[]{:S(2)}) copy-start(bf16[4096,128]{1,0:T(8,128)(2,1)} %param.13) | copy-start | bytes 3145732
  (2 other events, 2.1 us)
Sparse Core Ops, SparseCore 0:
  11.3 15.5 all-gather.2
Sparse Core Ops, SparseCore 1:
  105.1 77.5 reduce-scatter.1
